TPU v7x, 1024 devices: a whole 4x4x32 slice. The times are simulated.
1024 devices in a mesh: group: 64 (over z_lo, x, core), section: 16 (over y, z_hi).
Axes of the slice: x: 4, y: 4, z: 32 (z_hi: 4, z_lo: 8; z = z_hi * 8 + z_lo), core: 2. Of those that a mesh axis runs over, the one named last changes fastest.
Arguments:
- proj_rows: bfloat16 [16, 8192, 2560], P('section', 'group')
- out_grad: bfloat16 [16, 8192, 2048], P('section', 'group'), may hold values from -6 to 6
- prefix_kv: bfloat16 [16, 512, 512], P('section', 'group'), may hold values from -6 to 6
- prefix_len: int32 [8], replicated, may hold values from 1 to 192, 512 in all
- comp_len: int32 [64], replicated, may hold values from 1 to 128, as said below
- owner: int32 [64], replicated, may hold values from 0 to 7, as said below
Outputs:
- passed_grad: bfloat16 [16, 8192, 2048], P('section', 'group')
- comp_kv_grad: bfloat16 [16, 8192, 512], P('section', 'group')
- prefix_grad: bfloat16 [16, 512, 512], P('section', 'group')
Inputs may be any that keep to these rules, and one draw needn't show every extreme that they name: `owner`: each prompt has exactly 8 completions. `comp_len`: some completion has length exactly 128. `prefix_len`: the lengths sum to 512.
All inputs are finite; a program needn't handle non-finite values.
Results may differ from a plain program's by a relative error of at most 0.012.
Values may be sent and summed in bfloat16 or wider, within the bound.
No kernel may reach another device: no remote copies, remote signals or barrier semaphores. Data moves between devices by JAX's collectives and lax.ppermute only.
A program may use at most 32 MiB of HBM per device.

v0:
```python
import jax
import jax.numpy as jnp
from jax import lax
from jax.sharding import PartitionSpec as P

HEADS = 16
KV_HEADS = 2
HEAD_DIM = 128


def from_behind(value, axis, steps):
    count = lax.axis_size(axis)
    pairs = [(source, (source + steps) % count) for source in range(count)]
    return lax.ppermute(value, axis, pairs)


def score_block(q_four, keys):
    total = keys.shape[0]
    k_three = keys.reshape(total, KV_HEADS, HEAD_DIM)
    return jnp.einsum(
        "rgqh,mgh->gqrm", q_four, k_three, preferred_element_type=jnp.float32
    ) * HEAD_DIM ** (-0.5)


def key_terms(d_low, w_low, q_four, d_four, total):
    grad_k = jnp.einsum(
        "gqrm,rgqh->mgh", d_low, q_four, preferred_element_type=jnp.float32
    ) * HEAD_DIM ** (-0.5)
    grad_v = jnp.einsum("gqrm,rgqh->mgh", w_low, d_four, preferred_element_type=jnp.float32)
    return (grad_k.reshape(total, KV_HEADS * HEAD_DIM), grad_v.reshape(total, KV_HEADS * HEAD_DIM))


def per_device(proj_rows, out_grad, prefix_kv, prefix_len, comp_len, owner):
    width = HEADS * HEAD_DIM
    kv_width = KV_HEADS * HEAD_DIM
    per = HEADS // KV_HEADS
    rows = proj_rows[0]
    count = rows.shape[0]
    queries = rows[:, :width]
    own_keys = rows[:, width : width + kv_width]
    own_values = rows[:, width + kv_width :]
    member = lax.axis_index("group")
    groups = lax.axis_size("group")
    picked = jnp.arange(groups) == member
    prompt = jnp.sum(jnp.where(picked, owner, 0))
    length = jnp.sum(jnp.where(picked, comp_len, 0))
    prompt_count = prefix_len.shape[0]
    prompt_ids = jnp.arange(prompt_count)
    offset = jnp.sum(jnp.where(prompt_ids < prompt, prefix_len, 0))
    span = jnp.sum(jnp.where(prompt_ids == prompt, prefix_len, 0))
    token_ids = jnp.arange(count)
    live = token_ids < length
    dout = jnp.where(live[:, None], out_grad[0], jnp.zeros_like(out_grad[0]))
    gathered = lax.all_gather(prefix_kv[0], "group", axis=0, tiled=True)
    slots = gathered.shape[0]
    window = min(slots, 3 * slots // prompt_count)
    first = jnp.minimum(offset, slots - window)
    window_rows = lax.dynamic_slice_in_dim(gathered, first, window, 0)
    positions = first + jnp.arange(window)
    inside = (positions >= offset) & (positions < offset + span)
    causal = token_ids[:, None] >= token_ids[None, :]
    keys = jnp.concatenate([window_rows[:, :kv_width], own_keys], axis=0)
    values = jnp.concatenate([window_rows[:, kv_width:], own_values], axis=0)
    allowed = jnp.concatenate([jnp.broadcast_to(inside[None, :], (count, window)), causal], axis=1)
    total_keys = window + count
    q_four = queries.reshape(count, KV_HEADS, per, HEAD_DIM)
    d_four = dout.reshape(count, KV_HEADS, per, HEAD_DIM)
    v_three = values.reshape(total_keys, KV_HEADS, HEAD_DIM)
    scores = jnp.where(allowed[None, None], score_block(q_four, keys), jnp.float32(-1e30))
    top = jnp.max(scores, axis=-1, keepdims=True)
    expo = jnp.exp(scores - top)
    denom = jnp.sum(expo, axis=-1, keepdims=True)
    weights = expo / denom
    w_low = weights.astype(jnp.bfloat16)
    output = jnp.einsum("gqrm,mgh->gqrh", w_low, v_three, preferred_element_type=jnp.float32)
    delta = jnp.einsum("rgqh,gqrh->gqr", d_four.astype(jnp.float32), output)
    dprob = jnp.einsum("rgqh,mgh->gqrm", d_four, v_three, preferred_element_type=jnp.float32)
    d_low = (weights * (dprob - delta[..., None])).astype(jnp.bfloat16)
    k_three = keys.reshape(total_keys, KV_HEADS, HEAD_DIM)
    grad_q = jnp.einsum(
        "gqrm,mgh->rgqh", d_low, k_three, preferred_element_type=jnp.float32
    ) * HEAD_DIM ** (-0.5)
    grad_q = grad_q.reshape(count, width).astype(jnp.bfloat16)
    grad_own_k, grad_own_v = key_terms(
        d_low[..., window:], w_low[..., window:], q_four, d_four, count
    )
    own_grad = jnp.concatenate([grad_own_k, grad_own_v], axis=1).astype(jnp.bfloat16)
    passed = from_behind(grad_q[None], "section", -1)
    grad_pk, grad_pv = key_terms(d_low[..., :window], w_low[..., :window], q_four, d_four, window)
    window_term = jnp.concatenate([grad_pk, grad_pv], axis=1)
    full_term = lax.dynamic_update_slice_in_dim(
        jnp.zeros((slots, 2 * kv_width), jnp.float32), window_term, first, 0
    )
    prefix_grad = lax.psum_scatter(full_term, "group", scatter_dimension=0, tiled=True)
    return (passed, own_grad[None], prefix_grad.astype(jnp.bfloat16)[None])


def solution(mesh):
    in_specs = (
        P("section", "group", None),
        P("section", "group", None),
        P("section", "group", None),
        P(),
        P(),
        P(),
    )
    out_specs = (
        P("section", "group", None),
        P("section", "group", None),
        P("section", "group", None),
    )
    return jax.shard_map(
        per_device, mesh=mesh, in_specs=in_specs, out_specs=out_specs, check_vma=False
    )
```

profile of v0, /device:TPU:1, one launch (start us, length us, event | category | flops | bytes accessed | tf_op | source)
XLA Modules:
  0.0 647.6 jit_solution(15553446187395088677)
XLA Ops:
  7.3 1.5 copy.17
  8.8 0.6 fusion.30
  9.5 1.4 fusion.33
  11.6 149.7 %all-gather = bf16[1,512,512]{2,1,0:T(8,128)(2,1)S(1)} all-gather(bf16[1,8,512]{2,1,0:T(8,128)(2,1)S(1)} %copy-done.7), channel_id=2, replica_groups=mesh['group'=64,'section'=16] {'group'}, dimensions={1}, use_global_device_ids=true | all-gather | bytes 532480 | tf_op jit(solution)/shard_map/all_gather | solution.py:54
  161.5 0.7 reshape.100
  163.7 0.7 compare_and_fusion
  164.4 0.7 iota_compare_fusion.1
  165.1 0.9 copy.61
  166.1 0.9 fusion.38
  167.4 0.7 copy-done.4
  168.6 0.9 fusion.8
  169.5 0.6 fusion.2
  170.6 0.6 copy-done.1
  171.3 0.5 dynamic_update_slice.3
  171.8 1.0 copy-done
  172.8 1.8 fusion.7
  174.9 34.9 %collective-permute-start = (bf16[1,128,2048]{2,1,0:T(8,128)(2,1)S(1)}, bf16[1,128,2048]{2,1,0:T(8,128)(2,1)S(1)}, u32[]{:S(2)}, u32[]{:S(2)}) collective-permute-start(bf16[1,128,2048]{2,1,0:T(8,128)(2,1)S(1)} %copy.25), channel_id=1, source_target_pairs={{0,15},{1,0},{2,1},{3,2},{4,3},{5,4},{6,5},{7,6},{8,7},{9,8},{10,9... | collective-permute-start | bytes 1572872 | tf_op jit(solution)/shard_map/ppermute | solution.py:14
  209.7 1.3 fusion.12
  211.2 1.5 fusion.13
  212.8 0.7 pad_maximum_fusion.3
  213.5 7.2 %collective-permute-done = bf16[1,128,2048]{2,1,0:T(8,128)(2,1)S(1)} collective-permute-done((bf16[1,128,2048]{2,1,0:T(8,128)(2,1)S(1)}, bf16[1,128,2048]{2,1,0:T(8,128)(2,1)S(1)}, u32[]{:S(2)}, u32[]{:S(2)}) %collective-permute-start) | collective-permute-done | bytes 524320 | tf_op jit(solution)/shard_map/ppermute | solution.py:14
  220.7 418.0 %reduce-scatter.2.cloned.1.call-done = f32[8,512]{1,0:T(8,128)} async-done(((f32[512,512]{1,0:T(8,128)}), f32[8,512]{1,0:T(8,128)}) %reduce-scatter.2.cloned.1.call-update) | async-done | bytes 16400 | tf_op jit(solution)/shard_map/reduce_scatter | solution.py:94
  638.7 1.3 convert_bitcast_fusion
  640.0 0.8 copy.89
  (44 shorter events, 2.4 us)
Async XLA Ops:
  7.2 1.7 copy-start.9
  7.2 1.7 copy-start.8
  7.2 2.3 copy-start.10
  7.2 4.4 copy-start.7
  7.2 631.5 %reduce-scatter.2.cloned.1.call-start = ((), (), s32[]{:S(2)}) async-start(), calls=%async_computation.1 | async-start | bytes 1064960 | tf_op jit(solution)/shard_map/reduce_scatter | solution.py:94
  7.3 157.8 %copy-start.3 = (bf16[1,128,2048]{2,1,0:T(8,128)(2,1)S(1)}, bf16[1,128,2048]{2,1,0:T(8,128)(2,1)}, u32[]{:S(2)}) copy-start(bf16[1,128,2048]{2,1,0:T(8,128)(2,1)} %param.7) | copy-start | bytes 1572868
  167.1 1.0 copy-start.4
  167.1 1.5 copy-start.6
  167.4 2.1 copy-start.2
  170.1 1.1 copy-start.1
  171.8 1.0 copy-start
  171.8 39.4 %copy-start.5 = (bf16[16,8,16,128]{3,2,1,0:T(8,128)(2,1)S(1)}, bf16[16,8,16,128]{3,2,1,0:T(8,128)(2,1)}, u32[]{:S(2)}) copy-start(bf16[16,8,16,128]{3,2,1,0:T(8,128)(2,1)} %copy.61) | copy-start | bytes 1572868
  174.9 45.8 %collective-permute-start = (bf16[1,128,2048]{2,1,0:T(8,128)(2,1)S(1)}, bf16[1,128,2048]{2,1,0:T(8,128)(2,1)S(1)}, u32[]{:S(2)}, u32[]{:S(2)}) collective-permute-start(bf16[1,128,2048]{2,1,0:T(8,128)(2,1)S(1)} %copy.25), channel_id=1, source_target_pairs={{0,15},{1,0},{2,1},{3,2},{4,3},{5,4},{6,5},{7,6},{8,7},{9,8},{10,9... | collective-permute-start | bytes 1572872 | tf_op jit(solution)/shard_map/ppermute | solution.py:14
Sparse Core Ops, SparseCore 0:
  173.0 465.6 reduce-scatter.1
where the time goes:
time: 656 us; the launch traced here: 648 us
  waiting for transfers between devices  425 us (65%)
  blocking collectives  150 us (23%)
  starting transfers between devices  34.9 us (5%)
  between operations  16.4 us (2%)
  matrix products  7.89 us (1%)
  local copies, waits for them, and re-layouts  7.67 us (1%)
    reduce_scatter x1, waiting for transfers between devices, per_device(): lax.psum_scatter(full_term, 'group', scatter_dimension=0, tiled=True)  418 us
    all_gather x1, blocking collectives, per_device(): gathered = lax.all_gather(prefix_kv[0], 'group', axis=0, tiled=True)  150 us
    ppermute x1, starting transfers between devices, from_behind(): return lax.ppermute(value, axis, pairs)  34.9 us
  transfers between devices with their start and end apart: 2, of which 2 were waited for; matrix products, arithmetic and copies ran while one was open for 1% of the time, Pallas kernels for 0%

commit v1 on v0

--- a/solution.py
+++ b/solution.py
@@ -51,7 +51,10 @@
     token_ids = jnp.arange(count)
     live = token_ids < length
     dout = jnp.where(live[:, None], out_grad[0], jnp.zeros_like(out_grad[0]))
-    gathered = lax.all_gather(prefix_kv[0], "group", axis=0, tiled=True)
+    block = prefix_kv[0]
+    spread = jnp.broadcast_to(block[None], (groups,) + block.shape)
+    gathered = lax.all_to_all(spread, "group", 0, 0, tiled=True)
+    gathered = gathered.reshape(groups * block.shape[0], block.shape[1])
     slots = gathered.shape[0]
     window = min(slots, 3 * slots // prompt_count)
     first = jnp.minimum(offset, slots - window)
@@ -91,7 +94,8 @@
     full_term = lax.dynamic_update_slice_in_dim(
         jnp.zeros((slots, 2 * kv_width), jnp.float32), window_term, first, 0
     )
-    prefix_grad = lax.psum_scatter(full_term, "group", scatter_dimension=0, tiled=True)
+    pieces = full_term.reshape(groups, slots // groups, 2 * kv_width)
+    prefix_grad = lax.all_to_all(pieces, "group", 0, 0, tiled=True).sum(axis=0)
     return (passed, own_grad[None], prefix_grad.astype(jnp.bfloat16)[None])
 
 

time: 656 us -> 214 us (0.33)
  the two profiles are of different devices: /device:TPU:1 before, /device:TPU:136 now
where the time goes in v1:
time: 214 us; the launch traced here: 213 us
  waiting for transfers between devices  144 us (67%)
  starting transfers between devices  41.6 us (19%)
  local copies, waits for them, and re-layouts  11.5 us (5%)
  matrix products  6.72 us (3%)
  other arithmetic  6.53 us (3%)
  between operations  2.9 us (1%)
    ppermute x1, waiting for transfers between devices, from_behind(): return lax.ppermute(value, axis, pairs)  129 us
    all_to_all x1, waiting for transfers between devices, per_device(): gathered = lax.all_to_all(spread, 'group', 0, 0, tiled=True)  15.5 us
    ppermute x1, starting transfers between devices, from_behind(): return lax.ppermute(value, axis, pairs)  15.4 us
    all_to_all x1, starting transfers between devices, per_device(): gathered = lax.all_to_all(spread, 'group', 0, 0, tiled=True)  14.4 us
    all_to_all x1, starting transfers between devices, per_device(): prefix_grad = lax.all_to_all(pieces, 'group', 0, 0, tiled=True).sum(axis=0)  11.8 us
    unnamed x17, local copies, waits for them, and re-layouts  4.48 us
  transfers between devices with their start and end apart: 3, of which 2 were waited for; matrix products, arithmetic and copies ran while one was open for 6% of the time, Pallas kernels for 0%

profile of v1, /device:TPU:136, one launch (start us, length us, event | category | flops | bytes accessed | tf_op | source)
XLA Modules:
  0.0 213.4 jit_solution(6778074122915104830)
XLA Ops:
  0.6 1.6 broadcast_in_dim.60
  2.2 14.4 %all-to-all-start = ((bf16[64,8,512]{2,1,0:T(8,128)(2,1)}), bf16[64,8,512]{2,1,0:T(8,128)(2,1)S(1)}, u32[]{:S(2)}, u32[]{:S(2)}) async-start(bf16[64,8,512]{2,1,0:T(8,128)(2,1)} %broadcast_in_dim.60), calls=%async_computation | async-start | bytes 1048576 | tf_op jit(solution)/shard_map/all_to_all | solution.py:56
  16.6 1.3 fusion.30
  17.9 2.0 fusion.33
  20.7 1.4 copy.17
  23.6 0.9 copy.61
  24.5 0.7 compare_and_fusion
  26.1 15.5 %all-to-all-done = bf16[64,8,512]{2,1,0:T(8,128)(2,1)S(1)} async-done(((bf16[64,8,512]{2,1,0:T(8,128)(2,1)}), bf16[64,8,512]{2,1,0:T(8,128)(2,1)S(1)}, u32[]{:S(2)}, u32[]{:S(2)}) %all-to-all-start) | async-done | bytes 524320 | tf_op jit(solution)/shard_map/all_to_all | solution.py:56
  41.7 0.7 reshape.114
  42.5 0.9 fusion.38
  43.8 0.7 copy-done.5
  45.0 0.9 fusion.8
  47.0 0.7 copy-done
  47.7 1.1 broadcast_in_dim.68
  48.8 1.8 dynamic_update_slice.3
  50.6 11.8 %all-to-all-start.1 = ((f32[64,8,512]{2,1,0:T(8,128)}), f32[64,8,512]{2,1,0:T(8,128)S(1)}, u32[]{:S(2)}, u32[]{:S(2)}) async-start(f32[64,8,512]{2,1,0:T(8,128)} %bitcast.26), calls=%async_computation.1 | async-start | bytes 2097152 | tf_op jit(solution)/shard_map/all_to_all | solution.py:98
  62.9 1.0 copy.25
  64.0 15.4 %collective-permute-start = (bf16[1,128,2048]{2,1,0:T(8,128)(2,1)}, bf16[1,128,2048]{2,1,0:T(8,128)(2,1)S(1)}, u32[]{:S(2)}, u32[]{:S(2)}) collective-permute-start(bf16[1,128,2048]{2,1,0:T(8,128)(2,1)} %copy.25), channel_id=1, source_target_pairs={{0,15},{1,0},{2,1},{3,2},{4,3},{5,4},{6,5},{7,6},{8,7},{9,8},{10,9... | collective-permute-start | bytes 1572872 | tf_op jit(solution)/shard_map/ppermute | solution.py:14
  79.3 1.3 fusion.12
  80.8 1.6 fusion.13
  82.5 0.7 pad_maximum_fusion.3
  83.2 128.7 %collective-permute-done = bf16[1,128,2048]{2,1,0:T(8,128)(2,1)S(1)} collective-permute-done((bf16[1,128,2048]{2,1,0:T(8,128)(2,1)}, bf16[1,128,2048]{2,1,0:T(8,128)(2,1)S(1)}, u32[]{:S(2)}, u32[]{:S(2)}) %collective-permute-start) | collective-permute-done | bytes 524320 | tf_op jit(solution)/shard_map/ppermute | solution.py:14
  211.9 0.7 reduce_sum.59
  212.6 0.8 copy.89
  (36 shorter events, 3.8 us)
Async XLA Ops:
  0.6 23.0 %copy-start.3 = (bf16[1,128,2048]{2,1,0:T(8,128)(2,1)S(1)}, bf16[1,128,2048]{2,1,0:T(8,128)(2,1)}, u32[]{:S(2)}) copy-start(bf16[1,128,2048]{2,1,0:T(8,128)(2,1)} %param.7) | copy-start | bytes 1572868
  2.2 39.4 %all-to-all-start = ((bf16[64,8,512]{2,1,0:T(8,128)(2,1)}), bf16[64,8,512]{2,1,0:T(8,128)(2,1)S(1)}, u32[]{:S(2)}, u32[]{:S(2)}) async-start(bf16[64,8,512]{2,1,0:T(8,128)(2,1)} %broadcast_in_dim.60), calls=%async_computation | async-start | bytes 1048576 | tf_op jit(solution)/shard_map/all_to_all | solution.py:56
  22.1 24.4 %copy-start.4 = (bf16[128,2048]{0,1:T(8,128)(2,1)}, bf16[128,2048]{0,1:T(8,128)(2,1)S(1)}, u32[]{:S(2)}) copy-start(bf16[128,2048]{0,1:T(8,128)(2,1)S(1)} %slice.37) | copy-start | bytes 1572868
  43.5 1.0 copy-start.5
  43.5 1.5 copy-start.6
  43.8 2.1 copy-start.2
  46.5 1.1 copy-start
  47.6 14.8 %copy-start.1 = (bf16[2,8,128,320]{2,3,1,0:T(8,128)(2,1)S(1)}, bf16[2,8,128,320]{2,3,1,0:T(8,128)(2,1)}, u32[]{:S(2)}) copy-start(bf16[2,8,128,320]{2,3,1,0:T(8,128)(2,1)} %copy-done) | copy-start | bytes 3932164
  50.6 161.3 %all-to-all-start.1 = ((f32[64,8,512]{2,1,0:T(8,128)}), f32[64,8,512]{2,1,0:T(8,128)S(1)}, u32[]{:S(2)}, u32[]{:S(2)}) async-start(f32[64,8,512]{2,1,0:T(8,128)} %bitcast.26), calls=%async_computation.1 | async-start | bytes 2097152 | tf_op jit(solution)/shard_map/all_to_all | solution.py:98
  64.0 148.0 %collective-permute-start = (bf16[1,128,2048]{2,1,0:T(8,128)(2,1)}, bf16[1,128,2048]{2,1,0:T(8,128)(2,1)S(1)}, u32[]{:S(2)}, u32[]{:S(2)}) collective-permute-start(bf16[1,128,2048]{2,1,0:T(8,128)(2,1)} %copy.25), channel_id=1, source_target_pairs={{0,15},{1,0},{2,1},{3,2},{4,3},{5,4},{6,5},{7,6},{8,7},{9,8},{10,9... | collective-permute-start | bytes 1572872 | tf_op jit(solution)/shard_map/ppermute | solution.py:14

commit v2 on v0

--- a/solution.py
+++ b/solution.py
@@ -1,11 +1,38 @@
 import jax
 import jax.numpy as jnp
 from jax import lax
-from jax.sharding import PartitionSpec as P
+from jax.sharding import Mesh, PartitionSpec as P
 
 HEADS = 16
 KV_HEADS = 2
 HEAD_DIM = 128
+
+FAR = "group_z"
+NEAR = ("group_x", "group_core")
+GROUP = (FAR,) + NEAR
+SECTION = ("section_y", "section_z")
+
+
+def gather_prefix(block):
+    far = lax.axis_size(FAR)
+    near = lax.axis_size(NEAR)
+    rows, width = block.shape
+    spread = jnp.broadcast_to(block[None], (far, rows, width))
+    column = lax.all_to_all(spread, FAR, 0, 0, tiled=True).reshape(far * rows, width)
+    spread = jnp.broadcast_to(column[None], (near, far * rows, width))
+    whole = lax.all_to_all(spread, NEAR, 0, 0, tiled=True)
+    whole = whole.reshape(near, far, rows, width).transpose(1, 0, 2, 3)
+    return whole.reshape(far * near * rows, width)
+
+
+def scatter_sum(term):
+    far = lax.axis_size(FAR)
+    near = lax.axis_size(NEAR)
+    slots, width = term.shape
+    rows = slots // (far * near)
+    parts = term.reshape(far, near, rows, width).transpose(1, 0, 2, 3)
+    parts = lax.all_to_all(parts, NEAR, 0, 0, tiled=True).sum(axis=0)
+    return lax.all_to_all(parts, FAR, 0, 0, tiled=True).sum(axis=0)
 
 
 def from_behind(value, axis, steps):
@@ -39,8 +66,10 @@
     queries = rows[:, :width]
     own_keys = rows[:, width : width + kv_width]
     own_values = rows[:, width + kv_width :]
-    member = lax.axis_index("group")
-    groups = lax.axis_size("group")
+    member = (lax.axis_index(FAR) * lax.axis_size(NEAR[0]) + lax.axis_index(NEAR[0])) * lax.axis_size(
+        NEAR[1]
+    ) + lax.axis_index(NEAR[1])
+    groups = lax.axis_size(FAR) * lax.axis_size(NEAR)
     picked = jnp.arange(groups) == member
     prompt = jnp.sum(jnp.where(picked, owner, 0))
     length = jnp.sum(jnp.where(picked, comp_len, 0))
@@ -51,7 +80,7 @@
     token_ids = jnp.arange(count)
     live = token_ids < length
     dout = jnp.where(live[:, None], out_grad[0], jnp.zeros_like(out_grad[0]))
-    gathered = lax.all_gather(prefix_kv[0], "group", axis=0, tiled=True)
+    gathered = gather_prefix(prefix_kv[0])
     slots = gathered.shape[0]
     window = min(slots, 3 * slots // prompt_count)
     first = jnp.minimum(offset, slots - window)
@@ -85,30 +114,27 @@
         d_low[..., window:], w_low[..., window:], q_four, d_four, count
     )
     own_grad = jnp.concatenate([grad_own_k, grad_own_v], axis=1).astype(jnp.bfloat16)
-    passed = from_behind(grad_q[None], "section", -1)
+    passed = from_behind(grad_q[None], SECTION, -1)
     grad_pk, grad_pv = key_terms(d_low[..., :window], w_low[..., :window], q_four, d_four, window)
     window_term = jnp.concatenate([grad_pk, grad_pv], axis=1)
     full_term = lax.dynamic_update_slice_in_dim(
         jnp.zeros((slots, 2 * kv_width), jnp.float32), window_term, first, 0
     )
-    prefix_grad = lax.psum_scatter(full_term, "group", scatter_dimension=0, tiled=True)
+    prefix_grad = scatter_sum(full_term)
     return (passed, own_grad[None], prefix_grad.astype(jnp.bfloat16)[None])
 
 
 def solution(mesh):
-    in_specs = (
-        P("section", "group", None),
-        P("section", "group", None),
-        P("section", "group", None),
-        P(),
-        P(),
-        P(),
+    group_size = mesh.shape["group"]
+    section_size = mesh.shape["section"]
+    near_x, near_core = 4, 2
+    layout = mesh.devices.reshape(
+        group_size // (near_x * near_core), near_x, near_core, section_size // 4, 4
     )
-    out_specs = (
-        P("section", "group", None),
-        P("section", "group", None),
-        P("section", "group", None),
+    split = Mesh(layout, GROUP + SECTION)
+    placed = P(SECTION, GROUP, None)
+    in_specs = (placed, placed, placed, P(), P(), P())
+    out_specs = (placed, placed, placed)
+    return jax.shard_map(
+        per_device, mesh=split, in_specs=in_specs, out_specs=out_specs, check_vma=False
     )
-    return jax.shard_map(
-        per_device, mesh=mesh, in_specs=in_specs, out_specs=out_specs, check_vma=False
-    )

time: 656 us -> 183 us (0.28)
  the two profiles are of different devices: /device:TPU:1 before, /device:TPU:137 now
where the time goes in v2:
time: 183 us; the launch traced here: 182 us
  waiting for transfers between devices  96.9 us (53%)
  starting transfers between devices  40.7 us (22%)
  blocking collectives  18.5 us (10%)
  local copies, waits for them, and re-layouts  9.36 us (5%)
  other arithmetic  7.16 us (4%)
  matrix products  6.57 us (4%)
  between operations  2.99 us (2%)
    ppermute x1, waiting for transfers between devices, from_behind(): return lax.ppermute(value, axis, pairs)  91.3 us
    all_to_all x1, blocking collectives, scatter_sum(): parts = lax.all_to_all(parts, NEAR, 0, 0, tiled=True).sum(axis=0)  18.5 us
    ppermute x1, starting transfers between devices, from_behind(): return lax.ppermute(value, axis, pairs)  15.1 us
    all_to_all x1, starting transfers between devices, gather_prefix(): lax.all_to_all(spread, FAR, 0, 0, tiled=True).reshape(far * rows, width)  10.7 us
    all_to_all x1, starting transfers between devices, scatter_sum(): return lax.all_to_all(parts, FAR, 0, 0, tiled=True).sum(axis=0)  9.36 us
    all_to_all x1, waiting for transfers between devices, gather_prefix(): whole = lax.all_to_all(spread, NEAR, 0, 0, tiled=True)  5.55 us
    all_to_all x1, starting transfers between devices, gather_prefix(): whole = lax.all_to_all(spread, NEAR, 0, 0, tiled=True)  5.53 us
  transfers between devices with their start and end apart: 4, of which 2 were waited for; matrix products, arithmetic and copies ran while one was open for 7% of the time, Pallas kernels for 0%

profile of v2, /device:TPU:137, one launch (start us, length us, event | category | flops | bytes accessed | tf_op | source)
XLA Modules:
  0.0 182.2 jit_solution(5529208016360315730)
XLA Ops:
  0.6 1.4 broadcast_in_dim.67
  2.0 10.7 %all-to-all-start = ((bf16[8,8,512]{2,1,0:T(8,128)(2,1)}), bf16[8,8,512]{2,1,0:T(8,128)(2,1)S(1)}, u32[]{:S(2)}, u32[]{:S(2)}) async-start(bf16[8,8,512]{2,1,0:T(8,128)(2,1)} %broadcast_in_dim.67), calls=%async_computation | async-start | bytes 131072 | tf_op jit(solution)/shard_map/all_to_all | solution.py:21
  12.7 1.3 fusion.30
  14.0 2.0 %fusion.33 = (s32[]{:T(128)}, s32[]{:T(128)}) fusion(s32[8]{0:T(128)} %param.9, s32[]{:T(128)} %get-tuple-element.11), kind=kLoop, calls=%fused_computation.54 | loop fusion | flops 46 | bytes 44 | tf_op jit(solution)/shard_map/reduce_sum | solution.py:79
  18.1 0.7 iota_compare_fusion.1
  18.8 0.8 broadcast_in_dim.69
  19.7 5.5 %all-to-all-start.1 = ((bf16[8,64,512]{2,1,0:T(8,128)(2,1)}), bf16[8,64,512]{2,1,0:T(8,128)(2,1)S(1)}, u32[]{:S(2)}, u32[]{:S(2)}) async-start(bf16[8,64,512]{2,1,0:T(8,128)(2,1)} %broadcast_in_dim.69), calls=%async_computation.1 | async-start | bytes 1048576 | tf_op jit(solution)/shard_map/all_to_all | solution.py:23
  25.2 0.7 compare_and_fusion
  25.9 1.1 slice.37
  27.0 1.0 copy.85
  28.2 0.9 fusion.36
  29.1 5.5 %all-to-all-done.1 = bf16[8,64,512]{2,1,0:T(8,128)(2,1)S(1)} async-done(((bf16[8,64,512]{2,1,0:T(8,128)(2,1)}), bf16[8,64,512]{2,1,0:T(8,128)(2,1)S(1)}, u32[]{:S(2)}, u32[]{:S(2)}) %all-to-all-start.1) | async-done | bytes 524320 | tf_op jit(solution)/shard_map/all_to_all | solution.py:23
  35.0 2.0 %fusion.38 = (f32[2,8,128]{2,1,0:T(8,128)S(1)}, f32[2,8,128,320]{2,3,1,0:T(8,128)S(1)}) fusion(pred[128,320]{0,1:T(8,128)(4,1)S(1)} %pad_add_fusion, bf16[128,2,8,128]{0,3,2,1:T(8,128)(2,1)} %bitcast.100, bf16[320,2,128,1]{2,1,0,3:T(2,128)(2,1)S(1)} %bitcast.93), kind=kOutput, calls=%fused_computation.61 | convolution fusion | flops 170393920 | bytes 3358720 | tf_op jit(solution)/shard_map/sub | solution.py:100
  37.7 0.9 fusion.8
  38.7 0.6 fusion.2
  41.5 18.5 %all_to_all.20 = f32[8,8,8,512]{3,2,1,0:T(8,128)S(1)} all-to-all(f32[8,8,8,512]{3,2,1,0:T(8,128)S(1)} %copy.101), channel_id=1, replica_groups=mesh['group_z'=8,'group_x'=4,'group_core'=2,'section_y'=4,'section_z'=4]..., dimensions={0} | all-to-all | bytes 2097152 | tf_op jit(solution)/shard_map/all_to_all | solution.py:34
  60.0 0.7 reduce_sum.68
  60.8 9.4 %all-to-all-start.3 = ((f32[8,8,512]{2,1,0:T(8,128)}), f32[8,8,512]{2,1,0:T(8,128)S(1)}, u32[]{:S(2)}, u32[]{:S(2)}) async-start(f32[8,8,512]{2,1,0:T(8,128)} %reduce_sum.68), calls=%async_computation.3 | async-start | bytes 262144 | tf_op jit(solution)/shard_map/all_to_all | solution.py:35
  70.6 1.0 copy.92
  71.7 15.1 %collective-permute-start = (bf16[1,128,2048]{2,1,0:T(8,128)(2,1)}, bf16[1,128,2048]{2,1,0:T(8,128)(2,1)S(1)}, u32[]{:S(2)}, u32[]{:S(2)}) collective-permute-start(bf16[1,128,2048]{2,1,0:T(8,128)(2,1)} %copy.92), channel_id=1, source_target_pairs={{0,15},{1,0},{2,1},{3,2},{4,3},{5,4},{6,5},{7,6},{8,7},{9,8},{10,9... | collective-permute-start | bytes 1572872 | tf_op jit(solution)/shard_map/ppermute | solution.py:41
  87.2 1.5 fusion.13
  88.8 0.7 pad_maximum_fusion.3
  89.4 91.3 %collective-permute-done = bf16[1,128,2048]{2,1,0:T(8,128)(2,1)S(1)} collective-permute-done((bf16[1,128,2048]{2,1,0:T(8,128)(2,1)}, bf16[1,128,2048]{2,1,0:T(8,128)(2,1)S(1)}, u32[]{:S(2)}, u32[]{:S(2)}) %collective-permute-start) | collective-permute-done | bytes 524320 | tf_op jit(solution)/shard_map/ppermute | solution.py:41
  181.4 0.8 copy.159
  (38 shorter events, 5.0 us)
Async XLA Ops:
  0.6 27.4 %copy-start.3 = (bf16[1,128,2048]{2,1,0:T(8,128)(2,1)S(1)}, bf16[1,128,2048]{2,1,0:T(8,128)(2,1)}, u32[]{:S(2)}) copy-start(bf16[1,128,2048]{2,1,0:T(8,128)(2,1)} %param.7) | copy-start | bytes 1572868
  2.0 16.8 %all-to-all-start = ((bf16[8,8,512]{2,1,0:T(8,128)(2,1)}), bf16[8,8,512]{2,1,0:T(8,128)(2,1)S(1)}, u32[]{:S(2)}, u32[]{:S(2)}) async-start(bf16[8,8,512]{2,1,0:T(8,128)(2,1)} %broadcast_in_dim.67), calls=%async_computation | async-start | bytes 131072 | tf_op jit(solution)/shard_map/all_to_all | solution.py:21
  19.7 15.0 %all-to-all-start.1 = ((bf16[8,64,512]{2,1,0:T(8,128)(2,1)}), bf16[8,64,512]{2,1,0:T(8,128)(2,1)S(1)}, u32[]{:S(2)}, u32[]{:S(2)}) async-start(bf16[8,64,512]{2,1,0:T(8,128)(2,1)} %broadcast_in_dim.69), calls=%async_computation.1 | async-start | bytes 1048576 | tf_op jit(solution)/shard_map/all_to_all | solution.py:23
  37.3 1.4 copy-start.2
  38.7 1.0 copy-start.4
  39.7 1.1 copy-start
  41.4 28.7 %copy-start.1 = (bf16[2,8,128,320]{2,3,1,0:T(8,128)(2,1)S(1)}, bf16[2,8,128,320]{2,3,1,0:T(8,128)(2,1)}, u32[]{:S(2)}) copy-start(bf16[2,8,128,320]{2,3,1,0:T(8,128)(2,1)} %copy-done) | copy-start | bytes 3932164
  60.8 26.0 %copy-start.5 = (bf16[128,2048]{0,1:T(8,128)(2,1)S(1)}, bf16[128,2048]{0,1:T(8,128)(2,1)}, u32[]{:S(2)}) copy-start(bf16[128,2048]{0,1:T(8,128)(2,1)} %copy.85) | copy-start | bytes 1572868
  60.8 120.0 %all-to-all-start.3 = ((f32[8,8,512]{2,1,0:T(8,128)}), f32[8,8,512]{2,1,0:T(8,128)S(1)}, u32[]{:S(2)}, u32[]{:S(2)}) async-start(f32[8,8,512]{2,1,0:T(8,128)} %reduce_sum.68), calls=%async_computation.3 | async-start | bytes 262144 | tf_op jit(solution)/shard_map/all_to_all | solution.py:35
  71.7 109.1 %collective-permute-start = (bf16[1,128,2048]{2,1,0:T(8,128)(2,1)}, bf16[1,128,2048]{2,1,0:T(8,128)(2,1)S(1)}, u32[]{:S(2)}, u32[]{:S(2)}) collective-permute-start(bf16[1,128,2048]{2,1,0:T(8,128)(2,1)} %copy.92), channel_id=1, source_target_pairs={{0,15},{1,0},{2,1},{3,2},{4,3},{5,4},{6,5},{7,6},{8,7},{9,8},{10,9... | collective-permute-start | bytes 1572872 | tf_op jit(solution)/shard_map/ppermute | solution.py:41

commit v3 on v2

--- a/solution.py
+++ b/solution.py
@@ -25,14 +25,17 @@
     return whole.reshape(far * near * rows, width)
 
 
-def scatter_sum(term):
+def scatter_sum(term, hold):
     far = lax.axis_size(FAR)
     near = lax.axis_size(NEAR)
     slots, width = term.shape
     rows = slots // (far * near)
     parts = term.reshape(far, near, rows, width).transpose(1, 0, 2, 3)
+    parts = parts.reshape(near, far * rows, width)
     parts = lax.all_to_all(parts, NEAR, 0, 0, tiled=True).sum(axis=0)
-    return lax.all_to_all(parts, FAR, 0, 0, tiled=True).sum(axis=0)
+    parts = parts.reshape(far, rows, width)
+    parts, hold = lax.optimization_barrier((parts, hold))
+    return lax.all_to_all(parts, FAR, 0, 0, tiled=True).sum(axis=0), hold
 
 
 def from_behind(value, axis, steps):
@@ -120,7 +123,7 @@
     full_term = lax.dynamic_update_slice_in_dim(
         jnp.zeros((slots, 2 * kv_width), jnp.float32), window_term, first, 0
     )
-    prefix_grad = scatter_sum(full_term)
+    prefix_grad, passed = scatter_sum(full_term, passed)
     return (passed, own_grad[None], prefix_grad.astype(jnp.bfloat16)[None])
 
 

time: 183 us -> 183 us (level)
  the two profiles are of different devices: /device:TPU:137 before, /device:TPU:1 now
where the time goes in v3:
time: 183 us; the launch traced here: 181 us
  waiting for transfers between devices  104 us (57%)
  starting transfers between devices  44.8 us (24%)
  local copies, waits for them, and re-layouts  11.5 us (6%)
  other arithmetic  8.98 us (5%)
  matrix products  8.25 us (5%)
  between operations  3.01 us (2%)
    ppermute x1, waiting for transfers between devices, from_behind(): return lax.ppermute(value, axis, pairs)  88.2 us
    ppermute x1, starting transfers between devices, from_behind(): return lax.ppermute(value, axis, pairs)  15.1 us
    all_to_all x1, starting transfers between devices, gather_prefix(): lax.all_to_all(spread, FAR, 0, 0, tiled=True).reshape(far * rows, width)  13.1 us
    all_to_all x1, starting transfers between devices, gather_prefix(): whole = lax.all_to_all(spread, NEAR, 0, 0, tiled=True)  8.92 us
    all_to_all x1, waiting for transfers between devices, scatter_sum(): return (lax.all_to_all(parts, FAR, 0, 0, tiled=True).sum(axis=0), hold)  7.61 us
    all_to_all x1, waiting for transfers between devices, gather_prefix(): whole = lax.all_to_all(spread, NEAR, 0, 0, tiled=True)  6.33 us
    all_to_all x1, starting transfers between devices, scatter_sum(): parts = lax.all_to_all(parts, NEAR, 0, 0, tiled=True).sum(axis=0)  4.33 us
  transfers between devices with their start and end apart: 5, of which 4 were waited for; matrix products, arithmetic and copies ran while one was open for 8% of the time, Pallas kernels for 0%

profile of v3, /device:TPU:1, one launch (start us, length us, event | category | flops | bytes accessed | tf_op | source)
XLA Modules:
  0.0 180.9 jit_solution(15131591425031977219)
XLA Ops:
  0.6 1.4 broadcast_in_dim.72
  2.0 13.1 %all-to-all-start = ((bf16[8,8,512]{2,1,0:T(8,128)(2,1)}), bf16[8,8,512]{2,1,0:T(8,128)(2,1)S(1)}, u32[]{:S(2)}, u32[]{:S(2)}) async-start(bf16[8,8,512]{2,1,0:T(8,128)(2,1)} %broadcast_in_dim.72), calls=%async_computation | async-start | bytes 131072 | tf_op jit(solution)/shard_map/all_to_all | solution.py:21
  15.1 1.3 fusion.33
  16.4 2.0 %fusion.36 = (s32[]{:T(128)}, s32[]{:T(128)}) fusion(s32[8]{0:T(128)} %param.9, s32[]{:T(128)} %get-tuple-element.15), kind=kLoop, calls=%fused_computation.59 | loop fusion | flops 46 | bytes 44 | tf_op jit(solution)/shard_map/reduce_sum | solution.py:82
  20.5 1.3 copy.95
  22.6 2.3 %all-to-all-done = bf16[8,8,512]{2,1,0:T(8,128)(2,1)S(1)} async-done(((bf16[8,8,512]{2,1,0:T(8,128)(2,1)}), bf16[8,8,512]{2,1,0:T(8,128)(2,1)S(1)}, u32[]{:S(2)}, u32[]{:S(2)}) %all-to-all-start) | async-done | bytes 65568 | tf_op jit(solution)/shard_map/all_to_all | solution.py:21
  24.9 0.8 broadcast_in_dim.74
  25.7 8.9 %all-to-all-start.1 = ((bf16[8,64,512]{2,1,0:T(8,128)(2,1)}), bf16[8,64,512]{2,1,0:T(8,128)(2,1)S(1)}, u32[]{:S(2)}, u32[]{:S(2)}) async-start(bf16[8,64,512]{2,1,0:T(8,128)(2,1)} %broadcast_in_dim.74), calls=%async_computation.1 | async-start | bytes 1048576 | tf_op jit(solution)/shard_map/all_to_all | solution.py:23
  35.4 1.0 copy.54
  36.9 0.9 fusion.42
  37.8 6.3 %all-to-all-done.1 = bf16[8,64,512]{2,1,0:T(8,128)(2,1)S(1)} async-done(((bf16[8,64,512]{2,1,0:T(8,128)(2,1)}), bf16[8,64,512]{2,1,0:T(8,128)(2,1)S(1)}, u32[]{:S(2)}, u32[]{:S(2)}) %all-to-all-start.1) | async-done | bytes 524320 | tf_op jit(solution)/shard_map/all_to_all | solution.py:23
  44.4 2.4 %fusion.44 = (f32[2,8,128]{2,1,0:T(8,128)S(1)}, f32[2,8,128,320]{2,3,1,0:T(8,128)}) fusion(pred[128,320]{0,1:T(8,128)(4,1)S(1)} %pad_add_fusion, bf16[128,2,8,128]{0,3,2,1:T(8,128)(2,1)S(1)} %bitcast.103, bf16[320,2,128,1]{2,1,0,3:T(2,128)(2,1)S(1)} %bitcast.100), kind=kOutput, calls=%fused_computation.69 | convolution fusion | flops 170393920 | bytes 3358720 | tf_op jit(solution)/shard_map/sub | solution.py:103
  46.9 2.0 %fusion.14 = bf16[2,8,128,320]{2,3,1,0:T(8,128)(2,1)S(1)} fusion(f32[2,8,128,320]{2,3,1,0:T(8,128)} %get-tuple-element.14, f32[2,8,128]{2,1,0:T(8,128)S(1)} %get-tuple-element.13), kind=kLoop, calls=%fused_computation.24 | loop fusion | flops 1310720 | bytes 3940352 | tf_op jit(solution)/shard_map/convert_element_type | solution.py:106
  49.3 0.8 fusion.8
  53.4 1.1 copy.120
  54.5 4.3 %all-to-all-start.2 = ((f32[8,64,512]{2,1,0:T(8,128)}), f32[8,64,512]{2,1,0:T(8,128)S(1)}, u32[]{:S(2)}, u32[]{:S(2)}) async-start(f32[8,64,512]{2,1,0:T(8,128)} %bitcast.83), calls=%async_computation.2 | async-start | bytes 2097152 | tf_op jit(solution)/shard_map/all_to_all | solution.py:35
  58.8 1.9 %fusion.7 = bf16[2,128,8,128]{3,1,2,0:T(8,128)(2,1)S(1)} fusion(bf16[2,8,128,320]{2,3,1,0:T(8,128)(2,1)} %copy-done.1, bf16[320,2,128,1]{2,1,0,3:T(2,128)(2,1)} %bitcast.101), kind=kOutput, calls=%fused_computation.13 | convolution fusion | flops 168296448 | bytes 1998848 | tf_op jit(solution)/shard_map/gqrm,mgh->rgqh/dot_general | solution.py:112
  60.7 1.0 copy.67
  61.7 15.1 %collective-permute-start = (bf16[1,128,2048]{2,1,0:T(8,128)(2,1)}, bf16[1,128,2048]{2,1,0:T(8,128)(2,1)S(1)}, u32[]{:S(2)}, u32[]{:S(2)}) collective-permute-start(bf16[1,128,2048]{2,1,0:T(8,128)(2,1)} %copy.67), channel_id=1, source_target_pairs={{0,15},{1,0},{2,1},{3,2},{4,3},{5,4},{6,5},{7,6},{8,7},{9,8},{10,9... | collective-permute-start | bytes 1572872 | tf_op jit(solution)/shard_map/ppermute | solution.py:44
  77.6 88.2 %collective-permute-done = bf16[1,128,2048]{2,1,0:T(8,128)(2,1)S(1)} collective-permute-done((bf16[1,128,2048]{2,1,0:T(8,128)(2,1)}, bf16[1,128,2048]{2,1,0:T(8,128)(2,1)S(1)}, u32[]{:S(2)}, u32[]{:S(2)}) %collective-permute-start) | collective-permute-done | bytes 524320 | tf_op jit(solution)/shard_map/ppermute | solution.py:44
  165.8 3.4 %all-to-all-start.3 = ((f32[8,8,512]{2,1,0:T(8,128)}), f32[8,8,512]{2,1,0:T(8,128)S(1)}, u32[]{:S(2)}, u32[]{:S(2)}) async-start(f32[8,8,512]{2,1,0:T(8,128)} %bitcast.23), calls=%async_computation.3 | async-start | bytes 262144 | tf_op jit(solution)/shard_map/all_to_all | solution.py:38
  169.2 1.5 fusion.12
  171.9 7.6 %all-to-all-done.3 = f32[8,8,512]{2,1,0:T(8,128)S(1)} async-done(((f32[8,8,512]{2,1,0:T(8,128)}), f32[8,8,512]{2,1,0:T(8,128)S(1)}, u32[]{:S(2)}, u32[]{:S(2)}) %all-to-all-start.3) | async-done | bytes 131104 | tf_op jit(solution)/shard_map/all_to_all | solution.py:38
  180.1 0.8 copy.125
  (41 shorter events, 8.3 us)
Async XLA Ops:
  0.6 34.7 %copy-start.2 = (bf16[1,128,2560]{2,1,0:T(8,128)(2,1)S(1)}, bf16[1,128,2560]{2,1,0:T(8,128)(2,1)}, u32[]{:S(2)}) copy-start(bf16[1,128,2560]{2,1,0:T(8,128)(2,1)} %param.6) | copy-start | bytes 1966084
  2.0 22.8 %all-to-all-start = ((bf16[8,8,512]{2,1,0:T(8,128)(2,1)}), bf16[8,8,512]{2,1,0:T(8,128)(2,1)S(1)}, u32[]{:S(2)}, u32[]{:S(2)}) async-start(bf16[8,8,512]{2,1,0:T(8,128)(2,1)} %broadcast_in_dim.72), calls=%async_computation | async-start | bytes 131072 | tf_op jit(solution)/shard_map/all_to_all | solution.py:21
  25.7 18.4 %all-to-all-start.1 = ((bf16[8,64,512]{2,1,0:T(8,128)(2,1)}), bf16[8,64,512]{2,1,0:T(8,128)(2,1)S(1)}, u32[]{:S(2)}, u32[]{:S(2)}) async-start(bf16[8,64,512]{2,1,0:T(8,128)(2,1)} %broadcast_in_dim.74), calls=%async_computation.1 | async-start | bytes 1048576 | tf_op jit(solution)/shard_map/all_to_all | solution.py:23
  36.7 7.7 %copy-start.4 = (bf16[128,2048]{0,1:T(8,128)(2,1)S(1)}, bf16[128,2048]{0,1:T(8,128)(2,1)}, u32[]{:S(2)}) copy-start(bf16[128,2048]{0,1:T(8,128)(2,1)} %copy.54) | copy-start | bytes 1572868
  44.4 2.5 %copy-start.3 = (bf16[320,2,128]{2,1,0:T(2,128)(2,1)}, bf16[320,2,128]{2,1,0:T(2,128)(2,1)S(1)}, u32[]{:S(2)}) copy-start(bf16[320,2,128]{2,1,0:T(2,128)(2,1)S(1)} %reshape.117) | copy-start | bytes 491524
  48.9 1.7 copy-start
  50.7 1.0 copy-start.5
  51.7 1.1 copy-start.1
  54.5 22.4 %all-to-all-start.2 = ((f32[8,64,512]{2,1,0:T(8,128)}), f32[8,64,512]{2,1,0:T(8,128)S(1)}, u32[]{:S(2)}, u32[]{:S(2)}) async-start(f32[8,64,512]{2,1,0:T(8,128)} %bitcast.83), calls=%async_computation.2 | async-start | bytes 2097152 | tf_op jit(solution)/shard_map/all_to_all | solution.py:35
  61.7 104.1 %collective-permute-start = (bf16[1,128,2048]{2,1,0:T(8,128)(2,1)}, bf16[1,128,2048]{2,1,0:T(8,128)(2,1)S(1)}, u32[]{:S(2)}, u32[]{:S(2)}) collective-permute-start(bf16[1,128,2048]{2,1,0:T(8,128)(2,1)} %copy.67), channel_id=1, source_target_pairs={{0,15},{1,0},{2,1},{3,2},{4,3},{5,4},{6,5},{7,6},{8,7},{9,8},{10,9... | collective-permute-start | bytes 1572872 | tf_op jit(solution)/shard_map/ppermute | solution.py:44
  165.8 13.7 %all-to-all-start.3 = ((f32[8,8,512]{2,1,0:T(8,128)}), f32[8,8,512]{2,1,0:T(8,128)S(1)}, u32[]{:S(2)}, u32[]{:S(2)}) async-start(f32[8,8,512]{2,1,0:T(8,128)} %bitcast.23), calls=%async_computation.3 | async-start | bytes 262144 | tf_op jit(solution)/shard_map/all_to_all | solution.py:38

commit v4 on v2

--- a/solution.py
+++ b/solution.py
@@ -31,7 +31,9 @@
     slots, width = term.shape
     rows = slots // (far * near)
     parts = term.reshape(far, near, rows, width).transpose(1, 0, 2, 3)
+    parts = parts.reshape(near, far * rows, width)
     parts = lax.all_to_all(parts, NEAR, 0, 0, tiled=True).sum(axis=0)
+    parts = parts.reshape(far, rows, width)
     return lax.all_to_all(parts, FAR, 0, 0, tiled=True).sum(axis=0)
 
 
@@ -110,10 +112,6 @@
         "gqrm,mgh->rgqh", d_low, k_three, preferred_element_type=jnp.float32
     ) * HEAD_DIM ** (-0.5)
     grad_q = grad_q.reshape(count, width).astype(jnp.bfloat16)
-    grad_own_k, grad_own_v = key_terms(
-        d_low[..., window:], w_low[..., window:], q_four, d_four, count
-    )
-    own_grad = jnp.concatenate([grad_own_k, grad_own_v], axis=1).astype(jnp.bfloat16)
     passed = from_behind(grad_q[None], SECTION, -1)
     grad_pk, grad_pv = key_terms(d_low[..., :window], w_low[..., :window], q_four, d_four, window)
     window_term = jnp.concatenate([grad_pk, grad_pv], axis=1)
@@ -121,6 +119,9 @@
         jnp.zeros((slots, 2 * kv_width), jnp.float32), window_term, first, 0
     )
     prefix_grad = scatter_sum(full_term)
+    passed, d_own, w_own = lax.optimization_barrier((passed, d_low[..., window:], w_low[..., window:]))
+    grad_own_k, grad_own_v = key_terms(d_own, w_own, q_four, d_four, count)
+    own_grad = jnp.concatenate([grad_own_k, grad_own_v], axis=1).astype(jnp.bfloat16)
     return (passed, own_grad[None], prefix_grad.astype(jnp.bfloat16)[None])
 
 

time: 183 us -> 171 us (0.934)
  the two profiles are of different devices: /device:TPU:137 before, /device:TPU:1 now
where the time goes in v4:
time: 171 us; the launch traced here: 170 us
  waiting for transfers between devices  96.1 us (56%)
  starting transfers between devices  46.3 us (27%)
  local copies, waits for them, and re-layouts  11.8 us (7%)
  other arithmetic  7.06 us (4%)
  matrix products  5.53 us (3%)
  between operations  2.8 us (2%)
    ppermute x1, waiting for transfers between devices, from_behind(): return lax.ppermute(value, axis, pairs)  83.4 us
    ppermute x1, starting transfers between devices, from_behind(): return lax.ppermute(value, axis, pairs)  15.2 us
    all_to_all x1, starting transfers between devices, gather_prefix(): lax.all_to_all(spread, FAR, 0, 0, tiled=True).reshape(far * rows, width)  13.1 us
    all_to_all x1, starting transfers between devices, gather_prefix(): whole = lax.all_to_all(spread, NEAR, 0, 0, tiled=True)  8.92 us
    all_to_all x1, waiting for transfers between devices, gather_prefix(): whole = lax.all_to_all(spread, NEAR, 0, 0, tiled=True)  5.51 us
    all_to_all x1, starting transfers between devices, scatter_sum(): return lax.all_to_all(parts, FAR, 0, 0, tiled=True).sum(axis=0)  4.66 us
    all_to_all x1, starting transfers between devices, scatter_sum(): parts = lax.all_to_all(parts, NEAR, 0, 0, tiled=True).sum(axis=0)  4.39 us
    unnamed x20, local copies, waits for them, and re-layouts  4.2 us
  transfers between devices with their start and end apart: 5, of which 4 were waited for; matrix products, arithmetic and copies ran while one was open for 8% of the time, Pallas kernels for 0%

profile of v4, /device:TPU:1, one launch (start us, length us, event | category | flops | bytes accessed | tf_op | source)
XLA Modules:
  0.0 169.6 jit_solution(2513372353279872701)
XLA Ops:
  0.6 1.4 broadcast_in_dim.67
  2.0 13.1 %all-to-all-start = ((bf16[8,8,512]{2,1,0:T(8,128)(2,1)}), bf16[8,8,512]{2,1,0:T(8,128)(2,1)S(1)}, u32[]{:S(2)}, u32[]{:S(2)}) async-start(bf16[8,8,512]{2,1,0:T(8,128)(2,1)} %broadcast_in_dim.67), calls=%async_computation | async-start | bytes 131072 | tf_op jit(solution)/shard_map/all_to_all | solution.py:21
  15.1 1.3 fusion.28
  16.4 2.0 %fusion.31 = (s32[]{:T(128)}, s32[]{:T(128)}) fusion(s32[8]{0:T(128)} %param.9, s32[]{:T(128)} %get-tuple-element.17), kind=kLoop, calls=%fused_computation.53 | loop fusion | flops 46 | bytes 44 | tf_op jit(solution)/shard_map/reduce_sum | solution.py:81
  20.9 4.0 %all-to-all-done = bf16[8,8,512]{2,1,0:T(8,128)(2,1)S(1)} async-done(((bf16[8,8,512]{2,1,0:T(8,128)(2,1)}), bf16[8,8,512]{2,1,0:T(8,128)(2,1)S(1)}, u32[]{:S(2)}, u32[]{:S(2)}) %all-to-all-start) | async-done | bytes 65568 | tf_op jit(solution)/shard_map/all_to_all | solution.py:21
  24.9 0.8 broadcast_in_dim.69
  25.7 8.9 %all-to-all-start.1 = ((bf16[8,64,512]{2,1,0:T(8,128)(2,1)}), bf16[8,64,512]{2,1,0:T(8,128)(2,1)S(1)}, u32[]{:S(2)}, u32[]{:S(2)}) async-start(bf16[8,64,512]{2,1,0:T(8,128)(2,1)} %broadcast_in_dim.69), calls=%async_computation.1 | async-start | bytes 1048576 | tf_op jit(solution)/shard_map/all_to_all | solution.py:23
  35.3 1.1 slice.37
  36.6 1.0 copy.97
  37.7 0.9 fusion.34
  38.6 5.5 %all-to-all-done.1 = bf16[8,64,512]{2,1,0:T(8,128)(2,1)S(1)} async-done(((bf16[8,64,512]{2,1,0:T(8,128)(2,1)}), bf16[8,64,512]{2,1,0:T(8,128)(2,1)S(1)}, u32[]{:S(2)}, u32[]{:S(2)}) %all-to-all-start.1) | async-done | bytes 524320 | tf_op jit(solution)/shard_map/all_to_all | solution.py:23
  44.4 0.9 fusion.36
  45.7 0.7 copy-done.7
  46.9 0.9 fusion.8
  50.1 1.1 copy.122
  51.2 4.4 %all-to-all-start.2 = ((f32[8,64,512]{2,1,0:T(8,128)}), f32[8,64,512]{2,1,0:T(8,128)S(1)}, u32[]{:S(2)}, u32[]{:S(2)}) async-start(f32[8,64,512]{2,1,0:T(8,128)} %bitcast.88), calls=%async_computation.2 | async-start | bytes 2097152 | tf_op jit(solution)/shard_map/all_to_all | solution.py:35
  56.1 1.0 copy.58
  57.1 15.2 %collective-permute-start = (bf16[1,128,2048]{2,1,0:T(8,128)(2,1)}, bf16[1,128,2048]{2,1,0:T(8,128)(2,1)}, u32[]{:S(2)}, u32[]{:S(2)}) collective-permute-start(bf16[1,128,2048]{2,1,0:T(8,128)(2,1)} %copy.58), channel_id=1, source_target_pairs={{0,15},{1,0},{2,1},{3,2},{4,3},{5,4},{6,5},{7,6},{8,7},{9,8},{10,9... | collective-permute-start | bytes 1572872 | tf_op jit(solution)/shard_map/ppermute | solution.py:43
  72.4 0.7 reduce_sum.68
  73.1 4.7 %all-to-all-start.3 = ((f32[8,8,512]{2,1,0:T(8,128)}), f32[8,8,512]{2,1,0:T(8,128)S(1)}, u32[]{:S(2)}, u32[]{:S(2)}) async-start(f32[8,8,512]{2,1,0:T(8,128)} %bitcast.33), calls=%async_computation.3 | async-start | bytes 262144 | tf_op jit(solution)/shard_map/all_to_all | solution.py:37
  77.8 83.4 %collective-permute-done = bf16[1,128,2048]{2,1,0:T(8,128)(2,1)} collective-permute-done((bf16[1,128,2048]{2,1,0:T(8,128)(2,1)}, bf16[1,128,2048]{2,1,0:T(8,128)(2,1)}, u32[]{:S(2)}, u32[]{:S(2)}) %collective-permute-start) | collective-permute-done | bytes 524320 | tf_op jit(solution)/shard_map/ppermute | solution.py:43
  161.2 1.3 fusion.12
  163.9 3.2 %all-to-all-done.3 = f32[8,8,512]{2,1,0:T(8,128)S(1)} async-done(((f32[8,8,512]{2,1,0:T(8,128)}), f32[8,8,512]{2,1,0:T(8,128)S(1)}, u32[]{:S(2)}, u32[]{:S(2)}) %all-to-all-start.3) | async-done | bytes 131104 | tf_op jit(solution)/shard_map/all_to_all | solution.py:37
  167.7 1.9 %copy.127 = bf16[1,128,2048]{2,1,0:T(8,128)(2,1)} copy(bf16[1,128,2048]{2,1,0:T(8,128)(2,1)} %collective-permute-done) | data formatting | bytes 1048576
  (49 shorter events, 7.4 us)
Async XLA Ops:
  0.6 36.0 %copy-start.6 = (bf16[1,128,2048]{2,1,0:T(8,128)(2,1)S(1)}, bf16[1,128,2048]{2,1,0:T(8,128)(2,1)}, u32[]{:S(2)}) copy-start(bf16[1,128,2048]{2,1,0:T(8,128)(2,1)} %param.7) | copy-start | bytes 1572868
  2.0 22.8 %all-to-all-start = ((bf16[8,8,512]{2,1,0:T(8,128)(2,1)}), bf16[8,8,512]{2,1,0:T(8,128)(2,1)S(1)}, u32[]{:S(2)}, u32[]{:S(2)}) async-start(bf16[8,8,512]{2,1,0:T(8,128)(2,1)} %broadcast_in_dim.67), calls=%async_computation | async-start | bytes 131072 | tf_op jit(solution)/shard_map/all_to_all | solution.py:21
  25.7 18.4 %all-to-all-start.1 = ((bf16[8,64,512]{2,1,0:T(8,128)(2,1)}), bf16[8,64,512]{2,1,0:T(8,128)(2,1)S(1)}, u32[]{:S(2)}, u32[]{:S(2)}) async-start(bf16[8,64,512]{2,1,0:T(8,128)(2,1)} %broadcast_in_dim.69), calls=%async_computation.1 | async-start | bytes 1048576 | tf_op jit(solution)/shard_map/all_to_all | solution.py:23
  36.6 11.8 %copy-start.3 = (bf16[128,2048]{0,1:T(8,128)(2,1)}, bf16[128,2048]{0,1:T(8,128)(2,1)S(1)}, u32[]{:S(2)}) copy-start(bf16[128,2048]{0,1:T(8,128)(2,1)S(1)} %copy.51) | copy-start | bytes 1572868
  44.4 1.0 copy-start.4
  45.4 1.0 copy-start.7
  45.7 2.1 %copy-start.2 = (bf16[2,8,128,320]{2,3,1,0:T(8,128)(2,1)}, bf16[2,8,128,320]{2,3,1,0:T(8,128)(2,1)S(1)}, u32[]{:S(2)}) copy-start(bf16[2,8,128,320]{2,3,1,0:T(8,128)(2,1)S(1)} %fusion.14) | copy-start | bytes 3932164
  48.4 1.1 copy-start
  49.6 5.9 %copy-start.1 = (bf16[2,8,128,320]{2,3,1,0:T(8,128)(2,1)S(1)}, bf16[2,8,128,320]{2,3,1,0:T(8,128)(2,1)}, u32[]{:S(2)}) copy-start(bf16[2,8,128,320]{2,3,1,0:T(8,128)(2,1)} %copy-done) | copy-start | bytes 3932164
  50.1 5.5 %copy-start.5 = (bf16[320,2,128]{2,1,0:T(2,128)(2,1)S(1)}, bf16[320,2,128]{2,1,0:T(2,128)(2,1)}, u32[]{:S(2)}) copy-start(bf16[320,2,128]{2,1,0:T(2,128)(2,1)} %copy-done.4) | copy-start | bytes 491524
  51.2 21.2 %all-to-all-start.2 = ((f32[8,64,512]{2,1,0:T(8,128)}), f32[8,64,512]{2,1,0:T(8,128)S(1)}, u32[]{:S(2)}, u32[]{:S(2)}) async-start(f32[8,64,512]{2,1,0:T(8,128)} %bitcast.88), calls=%async_computation.2 | async-start | bytes 2097152 | tf_op jit(solution)/shard_map/all_to_all | solution.py:35
  56.1 105.1 %slice-start = ((bf16[2,8,128,320]{2,3,1,0:T(8,128)(2,1)}), bf16[2,8,128,128]{2,3,1,0:T(8,128)(2,1)S(1)}, s32[]{:S(2)}) async-start(bf16[2,8,128,320]{2,3,1,0:T(8,128)(2,1)} %copy-done), calls=%async_computation.4 | async-start | bytes 1048576 | tf_op jit(solution)/shard_map/slice | solution.py:122
  57.1 105.6 %slice-start.1 = ((bf16[2,8,128,320]{2,3,1,0:T(8,128)(2,1)}), bf16[2,8,128,128]{2,3,1,0:T(8,128)(2,1)S(1)}, s32[]{:S(2)}) async-start(bf16[2,8,128,320]{2,3,1,0:T(8,128)(2,1)} %copy-done.2), calls=%async_computation.5 | async-start | bytes 1048576 | tf_op jit(solution)/shard_map/slice | solution.py:122
  57.1 104.1 %collective-permute-start = (bf16[1,128,2048]{2,1,0:T(8,128)(2,1)}, bf16[1,128,2048]{2,1,0:T(8,128)(2,1)}, u32[]{:S(2)}, u32[]{:S(2)}) collective-permute-start(bf16[1,128,2048]{2,1,0:T(8,128)(2,1)} %copy.58), channel_id=1, source_target_pairs={{0,15},{1,0},{2,1},{3,2},{4,3},{5,4},{6,5},{7,6},{8,7},{9,8},{10,9... | collective-permute-start | bytes 1572872 | tf_op jit(solution)/shard_map/ppermute | solution.py:43
  73.1 89.6 %copy-start.8 = (bf16[16,8,16,128]{3,2,1,0:T(8,128)(2,1)S(1)}, bf16[16,8,16,128]{3,2,1,0:T(8,128)(2,1)}, u32[]{:S(2)}) copy-start(bf16[16,8,16,128]{3,2,1,0:T(8,128)(2,1)} %copy.97) | copy-start | bytes 1572868
  73.1 94.0 %all-to-all-start.3 = ((f32[8,8,512]{2,1,0:T(8,128)}), f32[8,8,512]{2,1,0:T(8,128)S(1)}, u32[]{:S(2)}, u32[]{:S(2)}) async-start(f32[8,8,512]{2,1,0:T(8,128)} %bitcast.33), calls=%async_computation.3 | async-start | bytes 262144 | tf_op jit(solution)/shard_map/all_to_all | solution.py:37

commit v5 on v4

--- a/solution.py
+++ b/solution.py
@@ -35,6 +35,30 @@
     parts = lax.all_to_all(parts, NEAR, 0, 0, tiled=True).sum(axis=0)
     parts = parts.reshape(far, rows, width)
     return lax.all_to_all(parts, FAR, 0, 0, tiled=True).sum(axis=0)
+
+
+def around(count, far_count, move):
+    pairs = []
+    for source in range(count):
+        near, far = divmod(source, far_count)
+        near, far = move(near, far)
+        pairs.append((source, (near % (count // far_count)) * far_count + far % far_count))
+    return pairs
+
+
+def pass_down(value, axis):
+    count = lax.axis_size(axis)
+    far_count = lax.axis_size(axis[1])
+    rows = value.shape[1]
+    cut = rows - rows // 8
+    direct = lax.ppermute(value[:, :cut], axis, around(count, far_count, lambda n, f: (n - (f == 0), f - 1)))
+    rest = value[:, cut:]
+    hop = around(count, far_count, lambda n, f: (n, f + 1))
+    rest = lax.ppermute(rest, axis, hop)
+    rest = lax.ppermute(rest, axis, hop)
+    last = around(count, far_count, lambda n, f: (n - (f == 2), f + 1))
+    rest = lax.ppermute(rest, axis, last)
+    return jnp.concatenate([direct, rest], axis=1)
 
 
 def from_behind(value, axis, steps):
@@ -112,7 +136,7 @@
         "gqrm,mgh->rgqh", d_low, k_three, preferred_element_type=jnp.float32
     ) * HEAD_DIM ** (-0.5)
     grad_q = grad_q.reshape(count, width).astype(jnp.bfloat16)
-    passed = from_behind(grad_q[None], SECTION, -1)
+    passed = pass_down(grad_q[None], SECTION)
     grad_pk, grad_pv = key_terms(d_low[..., :window], w_low[..., :window], q_four, d_four, window)
     window_term = jnp.concatenate([grad_pk, grad_pv], axis=1)
     full_term = lax.dynamic_update_slice_in_dim(

time: 171 us -> 161 us (0.942)
  waiting for transfers between devices: 96.1 us -> 74.9 us
  starting transfers between devices: 46.3 us -> 54.9 us
  other arithmetic: 7.06 us -> 8.98 us
    ppermute x1 -> x4, waiting for transfers between devices: 83.4 us -> 61.5 us  [the longest x2 36.6 us: pass_down(): rest = lax.ppermute(rest, axis, hop)]
    ppermute x1 -> x4, starting transfers between devices: 15.2 us -> 25 us  [the longest x1 15.1 us: pass_down(): lax.ppermute(value[:, :cut], axis, around(count, far_count, lambda n, f:...]
    concatenate x0 -> x1, other arithmetic: none -> 1.9 us  [pass_down(): return jnp.concatenate([direct, rest], axis=1)]
    unnamed x20 -> x19, local copies, waits for them, and re-layouts: 4.2 us -> 4.5 us
  transfers between devices with their start and end apart: 5 -> 8, of which waited for: 4 -> 7; matrix products, arithmetic and copies ran while one was open for 8% -> 10% of each run, Pallas kernels for 0% -> 0%
where the time goes in v5:
time: 161 us; the launch traced here: 160 us
  waiting for transfers between devices  74.9 us (47%)
  starting transfers between devices  54.9 us (34%)
  local copies, waits for them, and re-layouts  12.8 us (8%)
  other arithmetic  8.98 us (6%)
  matrix products  5.42 us (3%)
  between operations  2.83 us (2%)
    ppermute x2, waiting for transfers between devices, pass_down(): rest = lax.ppermute(rest, axis, hop)  36.6 us
    ppermute x1, starting transfers between devices, pass_down(): lax.ppermute(value[:, :cut], axis, around(count, far_count, lambda n, f:...  15.1 us
    ppermute x1, waiting for transfers between devices, pass_down(): lax.ppermute(value[:, :cut], axis, around(count, far_count, lambda n, f:...  14.9 us
    all_to_all x1, starting transfers between devices, gather_prefix(): lax.all_to_all(spread, FAR, 0, 0, tiled=True).reshape(far * rows, width)  13.1 us
    ppermute x1, waiting for transfers between devices, pass_down(): rest = lax.ppermute(rest, axis, last)  9.9 us
    all_to_all x1, starting transfers between devices, gather_prefix(): whole = lax.all_to_all(spread, NEAR, 0, 0, tiled=True)  8.92 us
    ppermute x1, starting transfers between devices, pass_down(): rest = lax.ppermute(rest, axis, last)  6.03 us
    all_to_all x1, waiting for transfers between devices, gather_prefix(): whole = lax.all_to_all(spread, NEAR, 0, 0, tiled=True)  5.59 us
  transfers between devices with their start and end apart: 8, of which 7 were waited for; matrix products, arithmetic and copies ran while one was open for 10% of the time, Pallas kernels for 0%

profile of v5, /device:TPU:1, one launch (start us, length us, event | category | flops | bytes accessed | tf_op | source)
XLA Modules:
  0.0 159.8 jit_solution(17112682529379844900)
XLA Ops:
  0.6 1.4 broadcast_in_dim.67
  2.0 13.1 %all-to-all-start = ((bf16[8,8,512]{2,1,0:T(8,128)(2,1)}), bf16[8,8,512]{2,1,0:T(8,128)(2,1)S(1)}, u32[]{:S(2)}, u32[]{:S(2)}) async-start(bf16[8,8,512]{2,1,0:T(8,128)(2,1)} %broadcast_in_dim.67), calls=%async_computation | async-start | bytes 131072 | tf_op jit(solution)/shard_map/all_to_all | solution.py:21
  15.1 1.3 fusion.28
  16.4 2.0 %fusion.31 = (s32[]{:T(128)}, s32[]{:T(128)}) fusion(s32[8]{0:T(128)} %param.9, s32[]{:T(128)} %get-tuple-element.17), kind=kLoop, calls=%fused_computation.54 | loop fusion | flops 46 | bytes 44 | tf_op jit(solution)/shard_map/reduce_sum | solution.py:105
  21.0 3.9 %all-to-all-done = bf16[8,8,512]{2,1,0:T(8,128)(2,1)S(1)} async-done(((bf16[8,8,512]{2,1,0:T(8,128)(2,1)}), bf16[8,8,512]{2,1,0:T(8,128)(2,1)S(1)}, u32[]{:S(2)}, u32[]{:S(2)}) %all-to-all-start) | async-done | bytes 65568 | tf_op jit(solution)/shard_map/all_to_all | solution.py:21
  25.7 8.9 %all-to-all-start.1 = ((bf16[8,64,512]{2,1,0:T(8,128)(2,1)}), bf16[8,64,512]{2,1,0:T(8,128)(2,1)S(1)}, u32[]{:S(2)}, u32[]{:S(2)}) async-start(bf16[8,64,512]{2,1,0:T(8,128)(2,1)} %broadcast_in_dim.69), calls=%async_computation.1 | async-start | bytes 1048576 | tf_op jit(solution)/shard_map/all_to_all | solution.py:23
  35.2 1.1 slice.45
  38.5 5.6 %all-to-all-done.1 = bf16[8,64,512]{2,1,0:T(8,128)(2,1)S(1)} async-done(((bf16[8,64,512]{2,1,0:T(8,128)(2,1)}), bf16[8,64,512]{2,1,0:T(8,128)(2,1)S(1)}, u32[]{:S(2)}, u32[]{:S(2)}) %all-to-all-start.1) | async-done | bytes 524320 | tf_op jit(solution)/shard_map/all_to_all | solution.py:23
  50.8 1.1 copy.128
  51.9 4.4 %all-to-all-start.2 = ((f32[8,64,512]{2,1,0:T(8,128)}), f32[8,64,512]{2,1,0:T(8,128)S(1)}, u32[]{:S(2)}, u32[]{:S(2)}) async-start(f32[8,64,512]{2,1,0:T(8,128)} %bitcast.88), calls=%async_computation.2 | async-start | bytes 2097152 | tf_op jit(solution)/shard_map/all_to_all | solution.py:35
  56.2 1.4 fusion.7
  58.6 15.1 %collective-permute-start = (bf16[1,112,2048]{2,1,0:T(8,128)(2,1)}, bf16[1,112,2048]{2,1,0:T(8,128)(2,1)}, u32[]{:S(2)}, u32[]{:S(2)}) collective-permute-start(bf16[1,112,2048]{2,1,0:T(8,128)(2,1)} %copy.99), channel_id=1, source_target_pairs={{0,15},{1,0},{2,1},{3,2},{4,3},{5,4},{6,5},{7,6},{8,7},{9,8},{10,9... | collective-permute-start | bytes 1376264 | tf_op jit(solution)/shard_map/ppermute | solution.py:54
  73.8 1.0 slice.48
  74.8 1.3 copy.100
  76.1 1.9 %collective-permute-start.1 = (bf16[1,16,2048]{2,1,0:T(8,128)(2,1)S(1)}, bf16[1,16,2048]{2,1,0:T(8,128)(2,1)S(1)}, u32[]{:S(2)}, u32[]{:S(2)}) collective-permute-start(bf16[1,16,2048]{2,1,0:T(8,128)(2,1)S(1)} %copy.100), channel_id=1, source_target_pairs={{0,1},{1,2},{2,3},{3,0},{4,5},{5,6},{6,7},{7,4},{8,9},{9,10},{10,1... | collective-permute-start | bytes 196616 | tf_op jit(solution)/shard_map/ppermute | solution.py:57
  78.0 21.7 %collective-permute-done.1 = bf16[1,16,2048]{2,1,0:T(8,128)(2,1)S(1)} collective-permute-done((bf16[1,16,2048]{2,1,0:T(8,128)(2,1)S(1)}, bf16[1,16,2048]{2,1,0:T(8,128)(2,1)S(1)}, u32[]{:S(2)}, u32[]{:S(2)}) %collective-permute-start.1) | collective-permute-done | bytes 65568 | tf_op jit(solution)/shard_map/ppermute | solution.py:57
  99.7 1.9 %collective-permute-start.2 = (bf16[1,16,2048]{2,1,0:T(8,128)(2,1)S(1)}, bf16[1,16,2048]{2,1,0:T(8,128)(2,1)}, u32[]{:S(2)}, u32[]{:S(2)}) collective-permute-start(bf16[1,16,2048]{2,1,0:T(8,128)(2,1)S(1)} %collective-permute-done.1), channel_id=1, source_target_pairs={{0,1},{1,2},{2,3},{3,0},{4,5},{5,6},{6,7},{7,4},{8,9},{9,10},{10,1... | collective-permute-start | bytes 196616 | tf_op jit(solution)/shard_map/ppermute | solution.py:58
  101.6 14.9 %collective-permute-done.2 = bf16[1,16,2048]{2,1,0:T(8,128)(2,1)} collective-permute-done((bf16[1,16,2048]{2,1,0:T(8,128)(2,1)S(1)}, bf16[1,16,2048]{2,1,0:T(8,128)(2,1)}, u32[]{:S(2)}, u32[]{:S(2)}) %collective-permute-start.2) | collective-permute-done | bytes 65568 | tf_op jit(solution)/shard_map/ppermute | solution.py:58
  116.5 6.0 %collective-permute-start.3 = (bf16[1,16,2048]{2,1,0:T(8,128)(2,1)}, bf16[1,16,2048]{2,1,0:T(8,128)(2,1)}, u32[]{:S(2)}, u32[]{:S(2)}) collective-permute-start(bf16[1,16,2048]{2,1,0:T(8,128)(2,1)} %collective-permute-done.2), channel_id=1, source_target_pairs={{0,1},{1,2},{2,15},{3,0},{4,5},{5,6},{6,3},{7,4},{8,9},{9,10},{10,... | collective-permute-start | bytes 196616 | tf_op jit(solution)/shard_map/ppermute | solution.py:60
  123.3 3.5 %all-to-all-start.3 = ((f32[8,8,512]{2,1,0:T(8,128)}), f32[8,8,512]{2,1,0:T(8,128)S(1)}, u32[]{:S(2)}, u32[]{:S(2)}) async-start(f32[8,8,512]{2,1,0:T(8,128)} %bitcast.34), calls=%async_computation.3 | async-start | bytes 262144 | tf_op jit(solution)/shard_map/all_to_all | solution.py:37
  126.8 9.9 %collective-permute-done.3 = bf16[1,16,2048]{2,1,0:T(8,128)(2,1)} collective-permute-done((bf16[1,16,2048]{2,1,0:T(8,128)(2,1)}, bf16[1,16,2048]{2,1,0:T(8,128)(2,1)}, u32[]{:S(2)}, u32[]{:S(2)}) %collective-permute-start.3) | collective-permute-done | bytes 65568 | tf_op jit(solution)/shard_map/ppermute | solution.py:60
  136.7 14.9 %collective-permute-done = bf16[1,112,2048]{2,1,0:T(8,128)(2,1)} collective-permute-done((bf16[1,112,2048]{2,1,0:T(8,128)(2,1)}, bf16[1,112,2048]{2,1,0:T(8,128)(2,1)}, u32[]{:S(2)}, u32[]{:S(2)}) %collective-permute-start) | collective-permute-done | bytes 458784 | tf_op jit(solution)/shard_map/ppermute | solution.py:54
  151.7 1.9 %pad_maximum_fusion = bf16[1,128,2048]{2,1,0:T(8,128)(2,1)} fusion(bf16[1,16,2048]{2,1,0:T(8,128)(2,1)} %collective-permute-done.3, bf16[1,112,2048]{2,1,0:T(8,128)(2,1)} %collective-permute-done), kind=kLoop, calls=%fused_computation.28 | loop fusion | flops 1048576 | bytes 1048576 | tf_op jit(solution)/shard_map/concatenate | solution.py:61
  155.2 3.9 %all-to-all-done.3 = f32[8,8,512]{2,1,0:T(8,128)S(1)} async-done(((f32[8,8,512]{2,1,0:T(8,128)}), f32[8,8,512]{2,1,0:T(8,128)S(1)}, u32[]{:S(2)}, u32[]{:S(2)}) %all-to-all-start.3) | async-done | bytes 131104 | tf_op jit(solution)/shard_map/all_to_all | solution.py:37
  (55 shorter events, 14.7 us)
Async XLA Ops:
  0.6 36.0 %copy-start.4 = (bf16[1,128,2048]{2,1,0:T(8,128)(2,1)S(1)}, bf16[1,128,2048]{2,1,0:T(8,128)(2,1)}, u32[]{:S(2)}) copy-start(bf16[1,128,2048]{2,1,0:T(8,128)(2,1)} %param.7) | copy-start | bytes 1572868
  2.0 22.8 %all-to-all-start = ((bf16[8,8,512]{2,1,0:T(8,128)(2,1)}), bf16[8,8,512]{2,1,0:T(8,128)(2,1)S(1)}, u32[]{:S(2)}, u32[]{:S(2)}) async-start(bf16[8,8,512]{2,1,0:T(8,128)(2,1)} %broadcast_in_dim.67), calls=%async_computation | async-start | bytes 131072 | tf_op jit(solution)/shard_map/all_to_all | solution.py:21
  25.7 18.4 %all-to-all-start.1 = ((bf16[8,64,512]{2,1,0:T(8,128)(2,1)}), bf16[8,64,512]{2,1,0:T(8,128)(2,1)S(1)}, u32[]{:S(2)}, u32[]{:S(2)}) async-start(bf16[8,64,512]{2,1,0:T(8,128)(2,1)} %broadcast_in_dim.69), calls=%async_computation.1 | async-start | bytes 1048576 | tf_op jit(solution)/shard_map/all_to_all | solution.py:23
  44.4 1.7 %copy-start.3 = (bf16[320,2,128]{2,1,0:T(2,128)(2,1)}, bf16[320,2,128]{2,1,0:T(2,128)(2,1)S(1)}, u32[]{:S(2)}) copy-start(bf16[320,2,128]{2,1,0:T(2,128)(2,1)S(1)} %reshape.117) | copy-start | bytes 491524
  46.0 1.0 copy-start.5
  46.1 1.5 copy-start.7
  46.4 2.1 %copy-start.2 = (bf16[2,8,128,320]{2,3,1,0:T(8,128)(2,1)}, bf16[2,8,128,320]{2,3,1,0:T(8,128)(2,1)S(1)}, u32[]{:S(2)}) copy-start(bf16[2,8,128,320]{2,3,1,0:T(8,128)(2,1)S(1)} %fusion.14) | copy-start | bytes 3932164
  49.1 1.1 copy-start
  50.3 5.9 %copy-start.1 = (bf16[2,8,128,320]{2,3,1,0:T(8,128)(2,1)S(1)}, bf16[2,8,128,320]{2,3,1,0:T(8,128)(2,1)}, u32[]{:S(2)}) copy-start(bf16[2,8,128,320]{2,3,1,0:T(8,128)(2,1)} %copy-done) | copy-start | bytes 3932164
  51.9 70.7 %all-to-all-start.2 = ((f32[8,64,512]{2,1,0:T(8,128)}), f32[8,64,512]{2,1,0:T(8,128)S(1)}, u32[]{:S(2)}, u32[]{:S(2)}) async-start(f32[8,64,512]{2,1,0:T(8,128)} %bitcast.88), calls=%async_computation.2 | async-start | bytes 2097152 | tf_op jit(solution)/shard_map/all_to_all | solution.py:35
  58.6 93.0 %collective-permute-start = (bf16[1,112,2048]{2,1,0:T(8,128)(2,1)}, bf16[1,112,2048]{2,1,0:T(8,128)(2,1)}, u32[]{:S(2)}, u32[]{:S(2)}) collective-permute-start(bf16[1,112,2048]{2,1,0:T(8,128)(2,1)} %copy.99), channel_id=1, source_target_pairs={{0,15},{1,0},{2,1},{3,2},{4,3},{5,4},{6,5},{7,6},{8,7},{9,8},{10,9... | collective-permute-start | bytes 1376264 | tf_op jit(solution)/shard_map/ppermute | solution.py:54
  74.8 78.8 %slice-start = ((bf16[2,8,128,320]{2,3,1,0:T(8,128)(2,1)}), bf16[2,8,128,128]{2,3,1,0:T(8,128)(2,1)S(1)}, s32[]{:S(2)}) async-start(bf16[2,8,128,320]{2,3,1,0:T(8,128)(2,1)} %copy-done), calls=%async_computation.4 | async-start | bytes 1048576 | tf_op jit(solution)/shard_map/slice | solution.py:146
  76.1 23.7 %collective-permute-start.1 = (bf16[1,16,2048]{2,1,0:T(8,128)(2,1)S(1)}, bf16[1,16,2048]{2,1,0:T(8,128)(2,1)S(1)}, u32[]{:S(2)}, u32[]{:S(2)}) collective-permute-start(bf16[1,16,2048]{2,1,0:T(8,128)(2,1)S(1)} %copy.100), channel_id=1, source_target_pairs={{0,1},{1,2},{2,3},{3,0},{4,5},{5,6},{6,7},{7,4},{8,9},{9,10},{10,1... | collective-permute-start | bytes 196616 | tf_op jit(solution)/shard_map/ppermute | solution.py:57
  99.7 16.8 %collective-permute-start.2 = (bf16[1,16,2048]{2,1,0:T(8,128)(2,1)S(1)}, bf16[1,16,2048]{2,1,0:T(8,128)(2,1)}, u32[]{:S(2)}, u32[]{:S(2)}) collective-permute-start(bf16[1,16,2048]{2,1,0:T(8,128)(2,1)S(1)} %collective-permute-done.1), channel_id=1, source_target_pairs={{0,1},{1,2},{2,3},{3,0},{4,5},{5,6},{6,7},{7,4},{8,9},{9,10},{10,1... | collective-permute-start | bytes 196616 | tf_op jit(solution)/shard_map/ppermute | solution.py:58
  116.5 20.2 %collective-permute-start.3 = (bf16[1,16,2048]{2,1,0:T(8,128)(2,1)}, bf16[1,16,2048]{2,1,0:T(8,128)(2,1)}, u32[]{:S(2)}, u32[]{:S(2)}) collective-permute-start(bf16[1,16,2048]{2,1,0:T(8,128)(2,1)} %collective-permute-done.2), channel_id=1, source_target_pairs={{0,1},{1,2},{2,15},{3,0},{4,5},{5,6},{6,3},{7,4},{8,9},{9,10},{10,... | collective-permute-start | bytes 196616 | tf_op jit(solution)/shard_map/ppermute | solution.py:60
  123.3 30.7 %slice-start.1 = ((bf16[2,8,128,320]{2,3,1,0:T(8,128)(2,1)}), bf16[2,8,128,128]{2,3,1,0:T(8,128)(2,1)S(1)}, s32[]{:S(2)}) async-start(bf16[2,8,128,320]{2,3,1,0:T(8,128)(2,1)} %copy-done.2), calls=%async_computation.5 | async-start | bytes 1048576 | tf_op jit(solution)/shard_map/slice | solution.py:146
  123.3 30.7 %copy-start.6 = (bf16[16,8,16,128]{3,2,1,0:T(8,128)(2,1)S(1)}, bf16[16,8,16,128]{3,2,1,0:T(8,128)(2,1)}, u32[]{:S(2)}) copy-start(bf16[16,8,16,128]{3,2,1,0:T(8,128)(2,1)} %copy.103) | copy-start | bytes 1572868
  123.3 35.8 %all-to-all-start.3 = ((f32[8,8,512]{2,1,0:T(8,128)}), f32[8,8,512]{2,1,0:T(8,128)S(1)}, u32[]{:S(2)}, u32[]{:S(2)}) async-start(f32[8,8,512]{2,1,0:T(8,128)} %bitcast.34), calls=%async_computation.3 | async-start | bytes 262144 | tf_op jit(solution)/shard_map/all_to_all | solution.py:37

commit v6 on v5

--- a/solution.py
+++ b/solution.py
@@ -50,7 +50,7 @@
     count = lax.axis_size(axis)
     far_count = lax.axis_size(axis[1])
     rows = value.shape[1]
-    cut = rows - rows // 8
+    cut = rows - 3 * rows // 16
     direct = lax.ppermute(value[:, :cut], axis, around(count, far_count, lambda n, f: (n - (f == 0), f - 1)))
     rest = value[:, cut:]
     hop = around(count, far_count, lambda n, f: (n, f + 1))

time: 161 us -> 157 us (0.975)
  waiting for transfers between devices: 74.9 us -> 68.3 us
    ppermute x1, waiting for transfers between devices: 14.9 us -> 6.05 us  [pass_down(): lax.ppermute(value[:, :cut], axis, around(count, far_count, lambda n, f:...]
    ppermute x2, waiting for transfers between devices: 36.6 us -> 45 us  [pass_down(): rest = lax.ppermute(rest, axis, hop)]
    ppermute x1, waiting for transfers between devices: 9.9 us -> 3.59 us  [pass_down(): rest = lax.ppermute(rest, axis, last)]
    all_to_all x1, starting transfers between devices: 3.5 us -> 8.16 us  [scatter_sum(): return lax.all_to_all(parts, FAR, 0, 0, tiled=True).sum(axis=0)]
    ppermute x1, starting transfers between devices: 6.03 us -> 2.51 us  [pass_down(): rest = lax.ppermute(rest, axis, last)]
  transfers between devices with their start and end apart: 8 -> 8, of which waited for: 7 -> 7; matrix products, arithmetic and copies ran while one was open for 10% -> 11% of each run, Pallas kernels for 0% -> 0%
where the time goes in v6:
time: 157 us; the launch traced here: 154 us
  waiting for transfers between devices  68.3 us (44%)
  starting transfers between devices  56.1 us (36%)
  local copies, waits for them, and re-layouts  12.7 us (8%)
  other arithmetic  8.98 us (6%)
  matrix products  5.41 us (3%)
  between operations  2.82 us (2%)
    ppermute x2, waiting for transfers between devices, pass_down(): rest = lax.ppermute(rest, axis, hop)  45 us
    ppermute x1, starting transfers between devices, pass_down(): lax.ppermute(value[:, :cut], axis, around(count, far_count, lambda n, f:...  15.1 us
    all_to_all x1, starting transfers between devices, gather_prefix(): lax.all_to_all(spread, FAR, 0, 0, tiled=True).reshape(far * rows, width)  13.1 us
    all_to_all x1, starting transfers between devices, gather_prefix(): whole = lax.all_to_all(spread, NEAR, 0, 0, tiled=True)  8.92 us
    all_to_all x1, starting transfers between devices, scatter_sum(): return lax.all_to_all(parts, FAR, 0, 0, tiled=True).sum(axis=0)  8.16 us
    ppermute x1, waiting for transfers between devices, pass_down(): lax.ppermute(value[:, :cut], axis, around(count, far_count, lambda n, f:...  6.05 us
    all_to_all x1, waiting for transfers between devices, gather_prefix(): whole = lax.all_to_all(spread, NEAR, 0, 0, tiled=True)  5.59 us
    all_to_all x1, starting transfers between devices, scatter_sum(): parts = lax.all_to_all(parts, NEAR, 0, 0, tiled=True).sum(axis=0)  4.49 us
  transfers between devices with their start and end apart: 8, of which 7 were waited for; matrix products, arithmetic and copies ran while one was open for 11% of the time, Pallas kernels for 0%

profile of v6, /device:TPU:1, one launch (start us, length us, event | category | flops | bytes accessed | tf_op | source)
XLA Modules:
  0.0 154.3 jit_solution(4736917034060062888)
XLA Ops:
  0.6 1.4 broadcast_in_dim.67
  2.0 13.1 %all-to-all-start = ((bf16[8,8,512]{2,1,0:T(8,128)(2,1)}), bf16[8,8,512]{2,1,0:T(8,128)(2,1)S(1)}, u32[]{:S(2)}, u32[]{:S(2)}) async-start(bf16[8,8,512]{2,1,0:T(8,128)(2,1)} %broadcast_in_dim.67), calls=%async_computation | async-start | bytes 131072 | tf_op jit(solution)/shard_map/all_to_all | solution.py:21
  15.1 1.3 fusion.28
  16.4 2.0 %fusion.31 = (s32[]{:T(128)}, s32[]{:T(128)}) fusion(s32[8]{0:T(128)} %param.9, s32[]{:T(128)} %get-tuple-element.17), kind=kLoop, calls=%fused_computation.54 | loop fusion | flops 46 | bytes 44 | tf_op jit(solution)/shard_map/reduce_sum | solution.py:105
  21.0 3.9 %all-to-all-done = bf16[8,8,512]{2,1,0:T(8,128)(2,1)S(1)} async-done(((bf16[8,8,512]{2,1,0:T(8,128)(2,1)}), bf16[8,8,512]{2,1,0:T(8,128)(2,1)S(1)}, u32[]{:S(2)}, u32[]{:S(2)}) %all-to-all-start) | async-done | bytes 65568 | tf_op jit(solution)/shard_map/all_to_all | solution.py:21
  25.7 8.9 %all-to-all-start.1 = ((bf16[8,64,512]{2,1,0:T(8,128)(2,1)}), bf16[8,64,512]{2,1,0:T(8,128)(2,1)S(1)}, u32[]{:S(2)}, u32[]{:S(2)}) async-start(bf16[8,64,512]{2,1,0:T(8,128)(2,1)} %broadcast_in_dim.69), calls=%async_computation.1 | async-start | bytes 1048576 | tf_op jit(solution)/shard_map/all_to_all | solution.py:23
  35.2 1.1 slice.45
  38.5 5.6 %all-to-all-done.1 = bf16[8,64,512]{2,1,0:T(8,128)(2,1)S(1)} async-done(((bf16[8,64,512]{2,1,0:T(8,128)(2,1)}), bf16[8,64,512]{2,1,0:T(8,128)(2,1)S(1)}, u32[]{:S(2)}, u32[]{:S(2)}) %all-to-all-start.1) | async-done | bytes 524320 | tf_op jit(solution)/shard_map/all_to_all | solution.py:23
  50.8 1.1 copy.128
  51.8 4.5 %all-to-all-start.2 = ((f32[8,64,512]{2,1,0:T(8,128)}), f32[8,64,512]{2,1,0:T(8,128)S(1)}, u32[]{:S(2)}, u32[]{:S(2)}) async-start(f32[8,64,512]{2,1,0:T(8,128)} %bitcast.88), calls=%async_computation.2 | async-start | bytes 2097152 | tf_op jit(solution)/shard_map/all_to_all | solution.py:35
  56.3 1.4 fusion.7
  58.7 15.1 %collective-permute-start = (bf16[1,104,2048]{2,1,0:T(8,128)(2,1)}, bf16[1,104,2048]{2,1,0:T(8,128)(2,1)}, u32[]{:S(2)}, u32[]{:S(2)}) collective-permute-start(bf16[1,104,2048]{2,1,0:T(8,128)(2,1)} %copy.99), channel_id=1, source_target_pairs={{0,15},{1,0},{2,1},{3,2},{4,3},{5,4},{6,5},{7,6},{8,7},{9,8},{10,9... | collective-permute-start | bytes 1277960 | tf_op jit(solution)/shard_map/ppermute | solution.py:54
  73.8 1.0 slice.48
  74.8 1.3 copy.100
  76.1 1.9 %collective-permute-start.1 = (bf16[1,24,2048]{2,1,0:T(8,128)(2,1)S(1)}, bf16[1,24,2048]{2,1,0:T(8,128)(2,1)S(1)}, u32[]{:S(2)}, u32[]{:S(2)}) collective-permute-start(bf16[1,24,2048]{2,1,0:T(8,128)(2,1)S(1)} %copy.100), channel_id=1, source_target_pairs={{0,1},{1,2},{2,3},{3,0},{4,5},{5,6},{6,7},{7,4},{8,9},{9,10},{10,1... | collective-permute-start | bytes 294920 | tf_op jit(solution)/shard_map/ppermute | solution.py:57
  78.0 23.8 %collective-permute-done.1 = bf16[1,24,2048]{2,1,0:T(8,128)(2,1)S(1)} collective-permute-done((bf16[1,24,2048]{2,1,0:T(8,128)(2,1)S(1)}, bf16[1,24,2048]{2,1,0:T(8,128)(2,1)S(1)}, u32[]{:S(2)}, u32[]{:S(2)}) %collective-permute-start.1) | collective-permute-done | bytes 98336 | tf_op jit(solution)/shard_map/ppermute | solution.py:57
  101.9 1.9 %collective-permute-start.2 = (bf16[1,24,2048]{2,1,0:T(8,128)(2,1)S(1)}, bf16[1,24,2048]{2,1,0:T(8,128)(2,1)}, u32[]{:S(2)}, u32[]{:S(2)}) collective-permute-start(bf16[1,24,2048]{2,1,0:T(8,128)(2,1)S(1)} %collective-permute-done.1), channel_id=1, source_target_pairs={{0,1},{1,2},{2,3},{3,0},{4,5},{5,6},{6,7},{7,4},{8,9},{9,10},{10,1... | collective-permute-start | bytes 294920 | tf_op jit(solution)/shard_map/ppermute | solution.py:58
  103.8 21.2 %collective-permute-done.2 = bf16[1,24,2048]{2,1,0:T(8,128)(2,1)} collective-permute-done((bf16[1,24,2048]{2,1,0:T(8,128)(2,1)S(1)}, bf16[1,24,2048]{2,1,0:T(8,128)(2,1)}, u32[]{:S(2)}, u32[]{:S(2)}) %collective-permute-start.2) | collective-permute-done | bytes 98336 | tf_op jit(solution)/shard_map/ppermute | solution.py:58
  125.0 2.5 %collective-permute-start.3 = (bf16[1,24,2048]{2,1,0:T(8,128)(2,1)}, bf16[1,24,2048]{2,1,0:T(8,128)(2,1)}, u32[]{:S(2)}, u32[]{:S(2)}) collective-permute-start(bf16[1,24,2048]{2,1,0:T(8,128)(2,1)} %collective-permute-done.2), channel_id=1, source_target_pairs={{0,1},{1,2},{2,15},{3,0},{4,5},{5,6},{6,3},{7,4},{8,9},{9,10},{10,... | collective-permute-start | bytes 294920 | tf_op jit(solution)/shard_map/ppermute | solution.py:60
  128.2 8.2 %all-to-all-start.3 = ((f32[8,8,512]{2,1,0:T(8,128)}), f32[8,8,512]{2,1,0:T(8,128)S(1)}, u32[]{:S(2)}, u32[]{:S(2)}) async-start(f32[8,8,512]{2,1,0:T(8,128)} %bitcast.34), calls=%async_computation.3 | async-start | bytes 262144 | tf_op jit(solution)/shard_map/all_to_all | solution.py:37
  136.4 3.6 %collective-permute-done.3 = bf16[1,24,2048]{2,1,0:T(8,128)(2,1)} collective-permute-done((bf16[1,24,2048]{2,1,0:T(8,128)(2,1)}, bf16[1,24,2048]{2,1,0:T(8,128)(2,1)}, u32[]{:S(2)}, u32[]{:S(2)}) %collective-permute-start.3) | collective-permute-done | bytes 98336 | tf_op jit(solution)/shard_map/ppermute | solution.py:60
  140.0 6.1 %collective-permute-done = bf16[1,104,2048]{2,1,0:T(8,128)(2,1)} collective-permute-done((bf16[1,104,2048]{2,1,0:T(8,128)(2,1)}, bf16[1,104,2048]{2,1,0:T(8,128)(2,1)}, u32[]{:S(2)}, u32[]{:S(2)}) %collective-permute-start) | collective-permute-done | bytes 426016 | tf_op jit(solution)/shard_map/ppermute | solution.py:54
  146.0 1.9 %pad_maximum_fusion = bf16[1,128,2048]{2,1,0:T(8,128)(2,1)} fusion(bf16[1,24,2048]{2,1,0:T(8,128)(2,1)} %collective-permute-done.3, bf16[1,104,2048]{2,1,0:T(8,128)(2,1)} %collective-permute-done), kind=kLoop, calls=%fused_computation.28 | loop fusion | flops 1048576 | bytes 1048576 | tf_op jit(solution)/shard_map/concatenate | solution.py:61
  149.6 4.2 %all-to-all-done.3 = f32[8,8,512]{2,1,0:T(8,128)S(1)} async-done(((f32[8,8,512]{2,1,0:T(8,128)}), f32[8,8,512]{2,1,0:T(8,128)S(1)}, u32[]{:S(2)}, u32[]{:S(2)}) %all-to-all-start.3) | async-done | bytes 131104 | tf_op jit(solution)/shard_map/all_to_all | solution.py:37
  (55 shorter events, 14.7 us)
Async XLA Ops:
  0.6 36.0 %copy-start.4 = (bf16[1,128,2048]{2,1,0:T(8,128)(2,1)S(1)}, bf16[1,128,2048]{2,1,0:T(8,128)(2,1)}, u32[]{:S(2)}) copy-start(bf16[1,128,2048]{2,1,0:T(8,128)(2,1)} %param.7) | copy-start | bytes 1572868
  2.0 22.8 %all-to-all-start = ((bf16[8,8,512]{2,1,0:T(8,128)(2,1)}), bf16[8,8,512]{2,1,0:T(8,128)(2,1)S(1)}, u32[]{:S(2)}, u32[]{:S(2)}) async-start(bf16[8,8,512]{2,1,0:T(8,128)(2,1)} %broadcast_in_dim.67), calls=%async_computation | async-start | bytes 131072 | tf_op jit(solution)/shard_map/all_to_all | solution.py:21
  25.7 18.4 %all-to-all-start.1 = ((bf16[8,64,512]{2,1,0:T(8,128)(2,1)}), bf16[8,64,512]{2,1,0:T(8,128)(2,1)S(1)}, u32[]{:S(2)}, u32[]{:S(2)}) async-start(bf16[8,64,512]{2,1,0:T(8,128)(2,1)} %broadcast_in_dim.69), calls=%async_computation.1 | async-start | bytes 1048576 | tf_op jit(solution)/shard_map/all_to_all | solution.py:23
  44.4 1.7 %copy-start.3 = (bf16[320,2,128]{2,1,0:T(2,128)(2,1)}, bf16[320,2,128]{2,1,0:T(2,128)(2,1)S(1)}, u32[]{:S(2)}) copy-start(bf16[320,2,128]{2,1,0:T(2,128)(2,1)S(1)} %reshape.117) | copy-start | bytes 491524
  46.0 1.0 copy-start.5
  46.1 1.5 copy-start.7
  46.4 2.1 %copy-start.2 = (bf16[2,8,128,320]{2,3,1,0:T(8,128)(2,1)}, bf16[2,8,128,320]{2,3,1,0:T(8,128)(2,1)S(1)}, u32[]{:S(2)}) copy-start(bf16[2,8,128,320]{2,3,1,0:T(8,128)(2,1)S(1)} %fusion.14) | copy-start | bytes 3932164
  49.1 1.1 copy-start
  50.3 6.0 %copy-start.1 = (bf16[2,8,128,320]{2,3,1,0:T(8,128)(2,1)S(1)}, bf16[2,8,128,320]{2,3,1,0:T(8,128)(2,1)}, u32[]{:S(2)}) copy-start(bf16[2,8,128,320]{2,3,1,0:T(8,128)(2,1)} %copy-done) | copy-start | bytes 3932164
  51.8 75.6 %all-to-all-start.2 = ((f32[8,64,512]{2,1,0:T(8,128)}), f32[8,64,512]{2,1,0:T(8,128)S(1)}, u32[]{:S(2)}, u32[]{:S(2)}) async-start(f32[8,64,512]{2,1,0:T(8,128)} %bitcast.88), calls=%async_computation.2 | async-start | bytes 2097152 | tf_op jit(solution)/shard_map/all_to_all | solution.py:35
  58.7 87.3 %collective-permute-start = (bf16[1,104,2048]{2,1,0:T(8,128)(2,1)}, bf16[1,104,2048]{2,1,0:T(8,128)(2,1)}, u32[]{:S(2)}, u32[]{:S(2)}) collective-permute-start(bf16[1,104,2048]{2,1,0:T(8,128)(2,1)} %copy.99), channel_id=1, source_target_pairs={{0,15},{1,0},{2,1},{3,2},{4,3},{5,4},{6,5},{7,6},{8,7},{9,8},{10,9... | collective-permute-start | bytes 1277960 | tf_op jit(solution)/shard_map/ppermute | solution.py:54
  74.8 73.1 %slice-start = ((bf16[2,8,128,320]{2,3,1,0:T(8,128)(2,1)}), bf16[2,8,128,128]{2,3,1,0:T(8,128)(2,1)S(1)}, s32[]{:S(2)}) async-start(bf16[2,8,128,320]{2,3,1,0:T(8,128)(2,1)} %copy-done), calls=%async_computation.4 | async-start | bytes 1048576 | tf_op jit(solution)/shard_map/slice | solution.py:146
  76.1 25.8 %collective-permute-start.1 = (bf16[1,24,2048]{2,1,0:T(8,128)(2,1)S(1)}, bf16[1,24,2048]{2,1,0:T(8,128)(2,1)S(1)}, u32[]{:S(2)}, u32[]{:S(2)}) collective-permute-start(bf16[1,24,2048]{2,1,0:T(8,128)(2,1)S(1)} %copy.100), channel_id=1, source_target_pairs={{0,1},{1,2},{2,3},{3,0},{4,5},{5,6},{6,7},{7,4},{8,9},{9,10},{10,1... | collective-permute-start | bytes 294920 | tf_op jit(solution)/shard_map/ppermute | solution.py:57
  101.9 23.1 %collective-permute-start.2 = (bf16[1,24,2048]{2,1,0:T(8,128)(2,1)S(1)}, bf16[1,24,2048]{2,1,0:T(8,128)(2,1)}, u32[]{:S(2)}, u32[]{:S(2)}) collective-permute-start(bf16[1,24,2048]{2,1,0:T(8,128)(2,1)S(1)} %collective-permute-done.1), channel_id=1, source_target_pairs={{0,1},{1,2},{2,3},{3,0},{4,5},{5,6},{6,7},{7,4},{8,9},{9,10},{10,1... | collective-permute-start | bytes 294920 | tf_op jit(solution)/shard_map/ppermute | solution.py:58
  125.0 15.0 %collective-permute-start.3 = (bf16[1,24,2048]{2,1,0:T(8,128)(2,1)}, bf16[1,24,2048]{2,1,0:T(8,128)(2,1)}, u32[]{:S(2)}, u32[]{:S(2)}) collective-permute-start(bf16[1,24,2048]{2,1,0:T(8,128)(2,1)} %collective-permute-done.2), channel_id=1, source_target_pairs={{0,1},{1,2},{2,15},{3,0},{4,5},{5,6},{6,3},{7,4},{8,9},{9,10},{10,... | collective-permute-start | bytes 294920 | tf_op jit(solution)/shard_map/ppermute | solution.py:60
  128.2 20.1 %slice-start.1 = ((bf16[2,8,128,320]{2,3,1,0:T(8,128)(2,1)}), bf16[2,8,128,128]{2,3,1,0:T(8,128)(2,1)S(1)}, s32[]{:S(2)}) async-start(bf16[2,8,128,320]{2,3,1,0:T(8,128)(2,1)} %copy-done.2), calls=%async_computation.5 | async-start | bytes 1048576 | tf_op jit(solution)/shard_map/slice | solution.py:146
  128.2 20.1 %copy-start.6 = (bf16[16,8,16,128]{3,2,1,0:T(8,128)(2,1)S(1)}, bf16[16,8,16,128]{3,2,1,0:T(8,128)(2,1)}, u32[]{:S(2)}) copy-start(bf16[16,8,16,128]{3,2,1,0:T(8,128)(2,1)} %copy.103) | copy-start | bytes 1572868
  128.2 25.5 %all-to-all-start.3 = ((f32[8,8,512]{2,1,0:T(8,128)}), f32[8,8,512]{2,1,0:T(8,128)S(1)}, u32[]{:S(2)}, u32[]{:S(2)}) async-start(f32[8,8,512]{2,1,0:T(8,128)} %bitcast.34), calls=%async_computation.3 | async-start | bytes 262144 | tf_op jit(solution)/shard_map/all_to_all | solution.py:37

commit v7 on v6

--- a/solution.py
+++ b/solution.py
@@ -13,16 +13,17 @@
 SECTION = ("section_y", "section_z")
 
 
-def gather_prefix(block):
+def gather_prefix(block, hold):
     far = lax.axis_size(FAR)
     near = lax.axis_size(NEAR)
     rows, width = block.shape
     spread = jnp.broadcast_to(block[None], (far, rows, width))
     column = lax.all_to_all(spread, FAR, 0, 0, tiled=True).reshape(far * rows, width)
+    column, hold = lax.optimization_barrier((column, hold))
     spread = jnp.broadcast_to(column[None], (near, far * rows, width))
     whole = lax.all_to_all(spread, NEAR, 0, 0, tiled=True)
     whole = whole.reshape(near, far, rows, width).transpose(1, 0, 2, 3)
-    return whole.reshape(far * near * rows, width)
+    return whole.reshape(far * near * rows, width), hold
 
 
 def scatter_sum(term):
@@ -106,7 +107,9 @@
     token_ids = jnp.arange(count)
     live = token_ids < length
     dout = jnp.where(live[:, None], out_grad[0], jnp.zeros_like(out_grad[0]))
-    gathered = gather_prefix(prefix_kv[0])
+    met = lax.ppermute(prefix_kv[0][:8, :128], SECTION, around(
+        lax.axis_size(SECTION), lax.axis_size(SECTION[1]), lambda n, f: (n - (f == 0), f - 1)))
+    gathered, met = gather_prefix(prefix_kv[0], met)
     slots = gathered.shape[0]
     window = min(slots, 3 * slots // prompt_count)
     first = jnp.minimum(offset, slots - window)
@@ -143,9 +146,12 @@
         jnp.zeros((slots, 2 * kv_width), jnp.float32), window_term, first, 0
     )
     prefix_grad = scatter_sum(full_term)
-    passed, d_own, w_own = lax.optimization_barrier((passed, d_low[..., window:], w_low[..., window:]))
+    passed, d_own, w_own, met = lax.optimization_barrier(
+        (passed, d_low[..., window:], w_low[..., window:], met)
+    )
     grad_own_k, grad_own_v = key_terms(d_own, w_own, q_four, d_four, count)
     own_grad = jnp.concatenate([grad_own_k, grad_own_v], axis=1).astype(jnp.bfloat16)
+    prefix_grad = jnp.where(met[0, 0] == jnp.inf, jnp.zeros_like(prefix_grad), prefix_grad)
     return (passed, own_grad[None], prefix_grad.astype(jnp.bfloat16)[None])
 
 

time: 157 us -> 165 us (1.051)
  starting transfers between devices: 56.1 us -> 92.8 us
  waiting for transfers between devices: 68.3 us -> 38 us
    ppermute x2, waiting for transfers between devices: 45 us -> 26.1 us  [pass_down(): rest = lax.ppermute(rest, axis, hop)]
    ppermute x0 -> x1, starting transfers between devices: none -> 17.7 us  [per_device(): lax.ppermute(prefix_kv[0][:8, :128], SECTION, around(lax.axis_size(SECTIO...]
    all_to_all x1, starting transfers between devices: 8.16 us -> 23.9 us  [scatter_sum(): return lax.all_to_all(parts, FAR, 0, 0, tiled=True).sum(axis=0)]
    ppermute x1, starting transfers between devices: 2.51 us -> 10.5 us  [pass_down(): rest = lax.ppermute(rest, axis, last)]
    ppermute x1, waiting for transfers between devices: 6.05 us -> 0.01 us  [pass_down(): lax.ppermute(value[:, :cut], axis, around(count, far_count, lambda n, f:...]
    ppermute x1, starting transfers between devices: 15.1 us -> 10.2 us  [pass_down(): lax.ppermute(value[:, :cut], axis, around(count, far_count, lambda n, f:...]
    all_to_all x1, waiting for transfers between devices: 3.9 us -> 0.01 us  [gather_prefix(): lax.all_to_all(spread, FAR, 0, 0, tiled=True).reshape(far * rows, width)]
    ppermute x2, starting transfers between devices: 3.83 us -> 7.6 us  [pass_down(): rest = lax.ppermute(rest, axis, hop)]
  transfers between devices with their start and end apart: 8 -> 9, of which waited for: 7 -> 4; matrix products, arithmetic and copies ran while one was open for 11% -> 11% of each run, Pallas kernels for 0% -> 0%
where the time goes in v7:
time: 165 us; the launch traced here: 163 us
  starting transfers between devices  92.8 us (56%)
  waiting for transfers between devices  38 us (23%)
  local copies, waits for them, and re-layouts  13.9 us (8%)
  other arithmetic  8.96 us (5%)
  matrix products  5.41 us (3%)
  between operations  3.51 us (2%)
    ppermute x2, waiting for transfers between devices, pass_down(): rest = lax.ppermute(rest, axis, hop)  26.1 us
    all_to_all x1, starting transfers between devices, scatter_sum(): return lax.all_to_all(parts, FAR, 0, 0, tiled=True).sum(axis=0)  23.9 us
    ppermute x1, starting transfers between devices, per_device(): lax.ppermute(prefix_kv[0][:8, :128], SECTION, around(lax.axis_size(SECTIO...  17.7 us
    all_to_all x1, starting transfers between devices, gather_prefix(): lax.all_to_all(spread, FAR, 0, 0, tiled=True).reshape(far * rows, width)  13.1 us
    ppermute x1, starting transfers between devices, pass_down(): rest = lax.ppermute(rest, axis, last)  10.5 us
    ppermute x1, starting transfers between devices, pass_down(): lax.ppermute(value[:, :cut], axis, around(count, far_count, lambda n, f:...  10.2 us
    ppermute x2, starting transfers between devices, pass_down(): rest = lax.ppermute(rest, axis, hop)  7.6 us
    all_to_all x1, waiting for transfers between devices, scatter_sum(): return lax.all_to_all(parts, FAR, 0, 0, tiled=True).sum(axis=0)  6.22 us
  transfers between devices with their start and end apart: 9, of which 4 were waited for; matrix products, arithmetic and copies ran while one was open for 11% of the time, Pallas kernels for 0%

profile of v7, /device:TPU:1, one launch (start us, length us, event | category | flops | bytes accessed | tf_op | source)
XLA Modules:
  0.0 162.6 jit_solution(17393015844470509105)
XLA Ops:
  0.6 1.4 broadcast_in_dim.69
  2.0 13.1 %all-to-all-start = ((bf16[8,8,512]{2,1,0:T(8,128)(2,1)}), bf16[8,8,512]{2,1,0:T(8,128)(2,1)S(1)}, u32[]{:S(2)}, u32[]{:S(2)}) async-start(bf16[8,8,512]{2,1,0:T(8,128)(2,1)} %broadcast_in_dim.69), calls=%async_computation | async-start | bytes 131072 | tf_op jit(solution)/shard_map/all_to_all | solution.py:21
  15.8 17.7 %collective-permute-start = (bf16[8,128]{1,0:T(8,128)(2,1)S(1)}, bf16[8,128]{1,0:T(8,128)(2,1)S(1)}, u32[]{:S(2)}, u32[]{:S(2)}) collective-permute-start(bf16[8,128]{1,0:T(8,128)(2,1)S(1)} %slice.52), channel_id=1, source_target_pairs={{0,15},{1,0},{2,1},{3,2},{4,3},{5,4},{6,5},{7,6},{8,7},{9,8},{10,9... | collective-permute-start | bytes 6152 | tf_op jit(solution)/shard_map/ppermute | solution.py:110
  33.5 1.3 fusion.29
  34.8 2.0 %fusion.32 = (s32[]{:T(128)}, s32[]{:T(128)}) fusion(s32[8]{0:T(128)} %param.9, s32[]{:T(128)} %get-tuple-element.23), kind=kLoop, calls=%fused_computation.55 | loop fusion | flops 46 | bytes 44 | tf_op jit(solution)/shard_map/reduce_sum | solution.py:106
  40.1 5.5 %all-to-all-start.1 = ((bf16[8,64,512]{2,1,0:T(8,128)(2,1)}), bf16[8,64,512]{2,1,0:T(8,128)(2,1)S(1)}, u32[]{:S(2)}, u32[]{:S(2)}) async-start(bf16[8,64,512]{2,1,0:T(8,128)(2,1)} %broadcast_in_dim.70), calls=%async_computation.1 | async-start | bytes 1048576 | tf_op jit(solution)/shard_map/all_to_all | solution.py:24
  46.3 1.1 slice.54
  49.6 5.6 %all-to-all-done.1 = bf16[8,64,512]{2,1,0:T(8,128)(2,1)S(1)} async-done(((bf16[8,64,512]{2,1,0:T(8,128)(2,1)}), bf16[8,64,512]{2,1,0:T(8,128)(2,1)S(1)}, u32[]{:S(2)}, u32[]{:S(2)}) %all-to-all-start.1) | async-done | bytes 524320 | tf_op jit(solution)/shard_map/all_to_all | solution.py:24
  56.1 0.9 fusion.37
  61.8 1.1 copy.128
  62.8 4.3 %all-to-all-start.2 = ((f32[8,64,512]{2,1,0:T(8,128)}), f32[8,64,512]{2,1,0:T(8,128)S(1)}, u32[]{:S(2)}, u32[]{:S(2)}) async-start(f32[8,64,512]{2,1,0:T(8,128)} %bitcast.88), calls=%async_computation.2 | async-start | bytes 2097152 | tf_op jit(solution)/shard_map/all_to_all | solution.py:36
  67.2 1.4 fusion.7
  68.6 1.0 copy.99
  69.5 10.2 %collective-permute-start.1 = (bf16[1,104,2048]{2,1,0:T(8,128)(2,1)}, bf16[1,104,2048]{2,1,0:T(8,128)(2,1)}, u32[]{:S(2)}, u32[]{:S(2)}) collective-permute-start(bf16[1,104,2048]{2,1,0:T(8,128)(2,1)} %copy.99), channel_id=1, source_target_pairs={{0,15},{1,0},{2,1},{3,2},{4,3},{5,4},{6,5},{7,6},{8,7},{9,8},{10,9... | collective-permute-start | bytes 1277960 | tf_op jit(solution)/shard_map/ppermute | solution.py:55
  79.8 1.0 slice.57
  80.8 1.3 copy.100
  82.0 3.8 %collective-permute-start.2 = (bf16[1,24,2048]{2,1,0:T(8,128)(2,1)S(1)}, bf16[1,24,2048]{2,1,0:T(8,128)(2,1)S(1)}, u32[]{:S(2)}, u32[]{:S(2)}) collective-permute-start(bf16[1,24,2048]{2,1,0:T(8,128)(2,1)S(1)} %copy.100), channel_id=1, source_target_pairs={{0,1},{1,2},{2,3},{3,0},{4,5},{5,6},{6,7},{7,4},{8,9},{9,10},{10,1... | collective-permute-start | bytes 294920 | tf_op jit(solution)/shard_map/ppermute | solution.py:58
  85.8 11.2 %collective-permute-done.2 = bf16[1,24,2048]{2,1,0:T(8,128)(2,1)S(1)} collective-permute-done((bf16[1,24,2048]{2,1,0:T(8,128)(2,1)S(1)}, bf16[1,24,2048]{2,1,0:T(8,128)(2,1)S(1)}, u32[]{:S(2)}, u32[]{:S(2)}) %collective-permute-start.2) | collective-permute-done | bytes 98336 | tf_op jit(solution)/shard_map/ppermute | solution.py:58
  97.0 3.8 %collective-permute-start.3 = (bf16[1,24,2048]{2,1,0:T(8,128)(2,1)S(1)}, bf16[1,24,2048]{2,1,0:T(8,128)(2,1)}, u32[]{:S(2)}, u32[]{:S(2)}) collective-permute-start(bf16[1,24,2048]{2,1,0:T(8,128)(2,1)S(1)} %collective-permute-done.2), channel_id=1, source_target_pairs={{0,1},{1,2},{2,3},{3,0},{4,5},{5,6},{6,7},{7,4},{8,9},{9,10},{10,1... | collective-permute-start | bytes 294920 | tf_op jit(solution)/shard_map/ppermute | solution.py:59
  100.8 15.0 %collective-permute-done.3 = bf16[1,24,2048]{2,1,0:T(8,128)(2,1)} collective-permute-done((bf16[1,24,2048]{2,1,0:T(8,128)(2,1)S(1)}, bf16[1,24,2048]{2,1,0:T(8,128)(2,1)}, u32[]{:S(2)}, u32[]{:S(2)}) %collective-permute-start.3) | collective-permute-done | bytes 98336 | tf_op jit(solution)/shard_map/ppermute | solution.py:59
  115.8 10.5 %collective-permute-start.4 = (bf16[1,24,2048]{2,1,0:T(8,128)(2,1)}, bf16[1,24,2048]{2,1,0:T(8,128)(2,1)}, u32[]{:S(2)}, u32[]{:S(2)}) collective-permute-start(bf16[1,24,2048]{2,1,0:T(8,128)(2,1)} %collective-permute-done.3), channel_id=1, source_target_pairs={{0,1},{1,2},{2,15},{3,0},{4,5},{5,6},{6,3},{7,4},{8,9},{9,10},{10,... | collective-permute-start | bytes 294920 | tf_op jit(solution)/shard_map/ppermute | solution.py:61
  127.1 23.9 %all-to-all-start.3 = ((f32[8,8,512]{2,1,0:T(8,128)}), f32[8,8,512]{2,1,0:T(8,128)S(1)}, u32[]{:S(2)}, u32[]{:S(2)}) async-start(f32[8,8,512]{2,1,0:T(8,128)} %bitcast.35), calls=%async_computation.3 | async-start | bytes 262144 | tf_op jit(solution)/shard_map/all_to_all | solution.py:38
  151.0 1.9 %pad_maximum_fusion = bf16[1,128,2048]{2,1,0:T(8,128)(2,1)} fusion(bf16[1,24,2048]{2,1,0:T(8,128)(2,1)} %collective-permute-done.4, bf16[1,104,2048]{2,1,0:T(8,128)(2,1)} %collective-permute-done.1), kind=kLoop, calls=%fused_computation.28 | loop fusion | flops 1048576 | bytes 1048576 | tf_op jit(solution)/shard_map/concatenate | solution.py:62
  155.7 6.2 %all-to-all-done.3 = f32[8,8,512]{2,1,0:T(8,128)S(1)} async-done(((f32[8,8,512]{2,1,0:T(8,128)}), f32[8,8,512]{2,1,0:T(8,128)S(1)}, u32[]{:S(2)}, u32[]{:S(2)}) %all-to-all-start.3) | async-done | bytes 131104 | tf_op jit(solution)/shard_map/all_to_all | solution.py:38
  (60 shorter events, 14.0 us)
Async XLA Ops:
  0.6 47.0 %copy-start.4 = (bf16[1,128,2048]{2,1,0:T(8,128)(2,1)S(1)}, bf16[1,128,2048]{2,1,0:T(8,128)(2,1)}, u32[]{:S(2)}) copy-start(bf16[1,128,2048]{2,1,0:T(8,128)(2,1)} %param.7) | copy-start | bytes 1572868
  2.0 37.2 %all-to-all-start = ((bf16[8,8,512]{2,1,0:T(8,128)(2,1)}), bf16[8,8,512]{2,1,0:T(8,128)(2,1)S(1)}, u32[]{:S(2)}, u32[]{:S(2)}) async-start(bf16[8,8,512]{2,1,0:T(8,128)(2,1)} %broadcast_in_dim.69), calls=%async_computation | async-start | bytes 131072 | tf_op jit(solution)/shard_map/all_to_all | solution.py:21
  15.8 23.5 %collective-permute-start = (bf16[8,128]{1,0:T(8,128)(2,1)S(1)}, bf16[8,128]{1,0:T(8,128)(2,1)S(1)}, u32[]{:S(2)}, u32[]{:S(2)}) collective-permute-start(bf16[8,128]{1,0:T(8,128)(2,1)S(1)} %slice.52), channel_id=1, source_target_pairs={{0,15},{1,0},{2,1},{3,2},{4,3},{5,4},{6,5},{7,6},{8,7},{9,8},{10,9... | collective-permute-start | bytes 6152 | tf_op jit(solution)/shard_map/ppermute | solution.py:110
  40.1 15.0 %all-to-all-start.1 = ((bf16[8,64,512]{2,1,0:T(8,128)(2,1)}), bf16[8,64,512]{2,1,0:T(8,128)(2,1)S(1)}, u32[]{:S(2)}, u32[]{:S(2)}) async-start(bf16[8,64,512]{2,1,0:T(8,128)(2,1)} %broadcast_in_dim.70), calls=%async_computation.1 | async-start | bytes 1048576 | tf_op jit(solution)/shard_map/all_to_all | solution.py:24
  55.4 1.7 %copy-start.3 = (bf16[320,2,128]{2,1,0:T(2,128)(2,1)}, bf16[320,2,128]{2,1,0:T(2,128)(2,1)S(1)}, u32[]{:S(2)}) copy-start(bf16[320,2,128]{2,1,0:T(2,128)(2,1)S(1)} %reshape.129) | copy-start | bytes 491524
  57.1 1.0 copy-start.5
  57.1 1.5 copy-start.7
  57.4 2.1 %copy-start.2 = (bf16[2,8,128,320]{2,3,1,0:T(8,128)(2,1)}, bf16[2,8,128,320]{2,3,1,0:T(8,128)(2,1)S(1)}, u32[]{:S(2)}) copy-start(bf16[2,8,128,320]{2,3,1,0:T(8,128)(2,1)S(1)} %fusion.14) | copy-start | bytes 3932164
  60.1 1.1 copy-start
  61.3 5.9 %copy-start.1 = (bf16[2,8,128,320]{2,3,1,0:T(8,128)(2,1)S(1)}, bf16[2,8,128,320]{2,3,1,0:T(8,128)(2,1)}, u32[]{:S(2)}) copy-start(bf16[2,8,128,320]{2,3,1,0:T(8,128)(2,1)} %copy-done) | copy-start | bytes 3932164
  62.8 63.5 %all-to-all-start.2 = ((f32[8,64,512]{2,1,0:T(8,128)}), f32[8,64,512]{2,1,0:T(8,128)S(1)}, u32[]{:S(2)}, u32[]{:S(2)}) async-start(f32[8,64,512]{2,1,0:T(8,128)} %bitcast.88), calls=%async_computation.2 | async-start | bytes 2097152 | tf_op jit(solution)/shard_map/all_to_all | solution.py:36
  69.5 81.4 %collective-permute-start.1 = (bf16[1,104,2048]{2,1,0:T(8,128)(2,1)}, bf16[1,104,2048]{2,1,0:T(8,128)(2,1)}, u32[]{:S(2)}, u32[]{:S(2)}) collective-permute-start(bf16[1,104,2048]{2,1,0:T(8,128)(2,1)} %copy.99), channel_id=1, source_target_pairs={{0,15},{1,0},{2,1},{3,2},{4,3},{5,4},{6,5},{7,6},{8,7},{9,8},{10,9... | collective-permute-start | bytes 1277960 | tf_op jit(solution)/shard_map/ppermute | solution.py:55
  80.8 72.7 %slice-start = ((bf16[2,8,128,320]{2,3,1,0:T(8,128)(2,1)}), bf16[2,8,128,128]{2,3,1,0:T(8,128)(2,1)S(1)}, s32[]{:S(2)}) async-start(bf16[2,8,128,320]{2,3,1,0:T(8,128)(2,1)} %copy-done), calls=%async_computation.4 | async-start | bytes 1048576 | tf_op jit(solution)/shard_map/slice | solution.py:150
  82.0 15.0 %collective-permute-start.2 = (bf16[1,24,2048]{2,1,0:T(8,128)(2,1)S(1)}, bf16[1,24,2048]{2,1,0:T(8,128)(2,1)S(1)}, u32[]{:S(2)}, u32[]{:S(2)}) collective-permute-start(bf16[1,24,2048]{2,1,0:T(8,128)(2,1)S(1)} %copy.100), channel_id=1, source_target_pairs={{0,1},{1,2},{2,3},{3,0},{4,5},{5,6},{6,7},{7,4},{8,9},{9,10},{10,1... | collective-permute-start | bytes 294920 | tf_op jit(solution)/shard_map/ppermute | solution.py:58
  97.0 18.8 %collective-permute-start.3 = (bf16[1,24,2048]{2,1,0:T(8,128)(2,1)S(1)}, bf16[1,24,2048]{2,1,0:T(8,128)(2,1)}, u32[]{:S(2)}, u32[]{:S(2)}) collective-permute-start(bf16[1,24,2048]{2,1,0:T(8,128)(2,1)S(1)} %collective-permute-done.2), channel_id=1, source_target_pairs={{0,1},{1,2},{2,3},{3,0},{4,5},{5,6},{6,7},{7,4},{8,9},{9,10},{10,1... | collective-permute-start | bytes 294920 | tf_op jit(solution)/shard_map/ppermute | solution.py:59
  115.8 35.2 %collective-permute-start.4 = (bf16[1,24,2048]{2,1,0:T(8,128)(2,1)}, bf16[1,24,2048]{2,1,0:T(8,128)(2,1)}, u32[]{:S(2)}, u32[]{:S(2)}) collective-permute-start(bf16[1,24,2048]{2,1,0:T(8,128)(2,1)} %collective-permute-done.3), channel_id=1, source_target_pairs={{0,1},{1,2},{2,15},{3,0},{4,5},{5,6},{6,3},{7,4},{8,9},{9,10},{10,... | collective-permute-start | bytes 294920 | tf_op jit(solution)/shard_map/ppermute | solution.py:61
  127.1 26.8 %slice-start.1 = ((bf16[2,8,128,320]{2,3,1,0:T(8,128)(2,1)}), bf16[2,8,128,128]{2,3,1,0:T(8,128)(2,1)S(1)}, s32[]{:S(2)}) async-start(bf16[2,8,128,320]{2,3,1,0:T(8,128)(2,1)} %copy-done.2), calls=%async_computation.5 | async-start | bytes 1048576 | tf_op jit(solution)/shard_map/slice | solution.py:150
  127.1 26.8 %copy-start.6 = (bf16[16,8,16,128]{3,2,1,0:T(8,128)(2,1)S(1)}, bf16[16,8,16,128]{3,2,1,0:T(8,128)(2,1)}, u32[]{:S(2)}) copy-start(bf16[16,8,16,128]{3,2,1,0:T(8,128)(2,1)} %copy.103) | copy-start | bytes 1572868
  127.1 34.9 %all-to-all-start.3 = ((f32[8,8,512]{2,1,0:T(8,128)}), f32[8,8,512]{2,1,0:T(8,128)S(1)}, u32[]{:S(2)}, u32[]{:S(2)}) async-start(f32[8,8,512]{2,1,0:T(8,128)} %bitcast.35), calls=%async_computation.3 | async-start | bytes 262144 | tf_op jit(solution)/shard_map/all_to_all | solution.py:38

commit v8 on v6

--- a/solution.py
+++ b/solution.py
@@ -25,7 +25,7 @@
     return whole.reshape(far * near * rows, width)
 
 
-def scatter_sum(term):
+def scatter_near(term):
     far = lax.axis_size(FAR)
     near = lax.axis_size(NEAR)
     slots, width = term.shape
@@ -33,7 +33,10 @@
     parts = term.reshape(far, near, rows, width).transpose(1, 0, 2, 3)
     parts = parts.reshape(near, far * rows, width)
     parts = lax.all_to_all(parts, NEAR, 0, 0, tiled=True).sum(axis=0)
-    parts = parts.reshape(far, rows, width)
+    return parts.reshape(far, rows, width)
+
+
+def scatter_far(parts):
     return lax.all_to_all(parts, FAR, 0, 0, tiled=True).sum(axis=0)
 
 
@@ -136,13 +139,14 @@
         "gqrm,mgh->rgqh", d_low, k_three, preferred_element_type=jnp.float32
     ) * HEAD_DIM ** (-0.5)
     grad_q = grad_q.reshape(count, width).astype(jnp.bfloat16)
-    passed = pass_down(grad_q[None], SECTION)
     grad_pk, grad_pv = key_terms(d_low[..., :window], w_low[..., :window], q_four, d_four, window)
     window_term = jnp.concatenate([grad_pk, grad_pv], axis=1)
     full_term = lax.dynamic_update_slice_in_dim(
         jnp.zeros((slots, 2 * kv_width), jnp.float32), window_term, first, 0
     )
-    prefix_grad = scatter_sum(full_term)
+    near_sum, grad_q = lax.optimization_barrier((scatter_near(full_term), grad_q))
+    passed = pass_down(grad_q[None], SECTION)
+    prefix_grad = scatter_far(near_sum)
     passed, d_own, w_own = lax.optimization_barrier((passed, d_low[..., window:], w_low[..., window:]))
     grad_own_k, grad_own_v = key_terms(d_own, w_own, q_four, d_four, count)
     own_grad = jnp.concatenate([grad_own_k, grad_own_v], axis=1).astype(jnp.bfloat16)

time: 157 us -> 176 us (1.12)
  starting transfers between devices: 56.1 us -> 76.3 us
  waiting for transfers between devices: 68.3 us -> 63.7 us
  other arithmetic: 8.98 us -> 11.7 us
  matrix products: 5.41 us -> 7.83 us
    ppermute x2, waiting for transfers between devices: 45 us -> 28.8 us  [pass_down(): rest = lax.ppermute(rest, axis, hop)]
    all_to_all x2, starting transfers between devices: 12.6 us -> 27.5 us  [the longest x1 23.1 us: scatter_far(): return lax.all_to_all(parts, FAR, 0, 0, tiled=True).sum(axis=0)]
    all_to_all x2, waiting for transfers between devices: 4.15 us -> 17 us  [the longest x1 12.4 us: scatter_near(): parts = lax.all_to_all(parts, NEAR, 0, 0, tiled=True).sum(axis=0)]
    ppermute x1, starting transfers between devices: 2.51 us -> 7.85 us  [pass_down(): rest = lax.ppermute(rest, axis, last)]
    unnamed x19 -> x11, local copies, waits for them, and re-layouts: 4.48 us -> 0.86 us
    ppermute x1, waiting for transfers between devices: 3.59 us -> 0.01 us  [pass_down(): rest = lax.ppermute(rest, axis, last)]
    ppermute x1, waiting for transfers between devices: 6.05 us -> 8.46 us  [pass_down(): lax.ppermute(value[:, :cut], axis, around(count, far_count, lambda n, f:...]
    convert_element_type x1, other arithmetic: 0.31 us -> 2.08 us  [per_device(): w_low = weights.astype(jnp.bfloat16)]
  transfers between devices with their start and end apart: 8 -> 8, of which waited for: 7 -> 7; matrix products, arithmetic and copies ran while one was open for 11% -> 8% of each run, Pallas kernels for 0% -> 0%
where the time goes in v8:
time: 176 us; the launch traced here: 175 us
  starting transfers between devices  76.3 us (43%)
  waiting for transfers between devices  63.7 us (36%)
  local copies, waits for them, and re-layouts  12.4 us (7%)
  other arithmetic  11.7 us (7%)
  matrix products  7.83 us (4%)
  between operations  3.03 us (2%)
    ppermute x2, waiting for transfers between devices, pass_down(): rest = lax.ppermute(rest, axis, hop)  28.8 us
    all_to_all x1, starting transfers between devices, scatter_far(): return lax.all_to_all(parts, FAR, 0, 0, tiled=True).sum(axis=0)  23.1 us
    ppermute x1, starting transfers between devices, pass_down(): lax.ppermute(value[:, :cut], axis, around(count, far_count, lambda n, f:...  14.5 us
    all_to_all x1, starting transfers between devices, gather_prefix(): lax.all_to_all(spread, FAR, 0, 0, tiled=True).reshape(far * rows, width)  13.1 us
    all_to_all x1, waiting for transfers between devices, scatter_near(): parts = lax.all_to_all(parts, NEAR, 0, 0, tiled=True).sum(axis=0)  12.4 us
    all_to_all x1, starting transfers between devices, gather_prefix(): whole = lax.all_to_all(spread, NEAR, 0, 0, tiled=True)  9.54 us
    ppermute x1, waiting for transfers between devices, pass_down(): lax.ppermute(value[:, :cut], axis, around(count, far_count, lambda n, f:...  8.46 us
    ppermute x1, starting transfers between devices, pass_down(): rest = lax.ppermute(rest, axis, last)  7.85 us
  transfers between devices with their start and end apart: 8, of which 7 were waited for; matrix products, arithmetic and copies ran while one was open for 8% of the time, Pallas kernels for 0%

profile of v8, /device:TPU:1, one launch (start us, length us, event | category | flops | bytes accessed | tf_op | source)
XLA Modules:
  0.0 174.9 jit_solution(12205731939708520467)
XLA Ops:
  0.6 1.4 broadcast_in_dim.74
  2.0 13.1 %all-to-all-start = ((bf16[8,8,512]{2,1,0:T(8,128)(2,1)}), bf16[8,8,512]{2,1,0:T(8,128)(2,1)S(1)}, u32[]{:S(2)}, u32[]{:S(2)}) async-start(bf16[8,8,512]{2,1,0:T(8,128)(2,1)} %broadcast_in_dim.74), calls=%async_computation | async-start | bytes 131072 | tf_op jit(solution)/shard_map/all_to_all | solution.py:21
  15.1 1.3 fusion.31
  16.4 2.0 %fusion.34 = (s32[]{:T(128)}, s32[]{:T(128)}) fusion(s32[8]{0:T(128)} %param.9, s32[]{:T(128)} %get-tuple-element.21), kind=kLoop, calls=%fused_computation.58 | loop fusion | flops 46 | bytes 44 | tf_op jit(solution)/shard_map/reduce_sum | solution.py:108
  20.5 1.3 copy.95
  22.6 2.3 %all-to-all-done = bf16[8,8,512]{2,1,0:T(8,128)(2,1)S(1)} async-done(((bf16[8,8,512]{2,1,0:T(8,128)(2,1)}), bf16[8,8,512]{2,1,0:T(8,128)(2,1)S(1)}, u32[]{:S(2)}, u32[]{:S(2)}) %all-to-all-start) | async-done | bytes 65568 | tf_op jit(solution)/shard_map/all_to_all | solution.py:21
  25.7 9.5 %all-to-all-start.1 = ((bf16[8,64,512]{2,1,0:T(8,128)(2,1)}), bf16[8,64,512]{2,1,0:T(8,128)(2,1)}, u32[]{:S(2)}, u32[]{:S(2)}) async-start(bf16[8,64,512]{2,1,0:T(8,128)(2,1)} %broadcast_in_dim.76), calls=%async_computation.1 | async-start | bytes 1048576 | tf_op jit(solution)/shard_map/all_to_all | solution.py:23
  37.7 7.2 %all-to-all-done.1 = bf16[8,64,512]{2,1,0:T(8,128)(2,1)} async-done(((bf16[8,64,512]{2,1,0:T(8,128)(2,1)}), bf16[8,64,512]{2,1,0:T(8,128)(2,1)}, u32[]{:S(2)}, u32[]{:S(2)}) %all-to-all-start.1) | async-done | bytes 524320 | tf_op jit(solution)/shard_map/all_to_all | solution.py:23
  46.9 2.4 %fusion.42 = (f32[2,8,128]{2,1,0:T(8,128)S(1)}, f32[2,8,128,320]{2,3,1,0:T(8,128)}) fusion(pred[128,320]{0,1:T(8,128)(4,1)S(1)} %pad_add_fusion, bf16[128,2,8,128]{0,3,2,1:T(8,128)(2,1)S(1)} %bitcast.94, bf16[320,2,128,1]{2,1,0,3:T(2,128)(2,1)S(1)} %bitcast.107), kind=kOutput, calls=%fused_computation.68 | convolution fusion | flops 170393920 | bytes 3358720 | tf_op jit(solution)/shard_map/sub | solution.py:129
  49.3 2.1 %fusion.14 = bf16[2,8,128,320]{2,3,1,0:T(8,128)(2,1)S(1)} fusion(f32[2,8,128,320]{2,3,1,0:T(8,128)} %get-tuple-element.20, f32[2,8,128]{2,1,0:T(8,128)S(1)} %get-tuple-element.19), kind=kLoop, calls=%fused_computation.24 | loop fusion | flops 1310720 | bytes 3940352 | tf_op jit(solution)/shard_map/convert_element_type | solution.py:132
  57.4 4.4 %all-to-all-start.2 = ((f32[8,64,512]{2,1,0:T(8,128)}), f32[8,64,512]{2,1,0:T(8,128)S(1)}, u32[]{:S(2)}, u32[]{:S(2)}) async-start(f32[8,64,512]{2,1,0:T(8,128)} %bitcast.86), calls=%async_computation.2 | async-start | bytes 2097152 | tf_op jit(solution)/shard_map/all_to_all | solution.py:35
  61.7 2.7 %fusion.7 = bf16[2,128,8,128]{3,1,2,0:T(8,128)(2,1)} fusion(bf16[2,8,128,320]{2,3,1,0:T(8,128)(2,1)} %copy-done.1, bf16[320,2,128,1]{2,1,0,3:T(2,128)(2,1)} %bitcast.108), kind=kOutput, calls=%fused_computation.13 | convolution fusion | flops 168296448 | bytes 1998848 | tf_op jit(solution)/shard_map/gqrm,mgh->rgqh/dot_general | solution.py:138
  64.4 12.4 %all-to-all-done.2 = f32[8,64,512]{2,1,0:T(8,128)S(1)} async-done(((f32[8,64,512]{2,1,0:T(8,128)}), f32[8,64,512]{2,1,0:T(8,128)S(1)}, u32[]{:S(2)}, u32[]{:S(2)}) %all-to-all-start.2) | async-done | bytes 1048608 | tf_op jit(solution)/shard_map/all_to_all | solution.py:35
  77.6 1.3 copy.67
  79.7 14.5 %collective-permute-start = (bf16[1,104,2048]{2,1,0:T(8,128)(2,1)}, bf16[1,104,2048]{2,1,0:T(8,128)(2,1)}, u32[]{:S(2)}, u32[]{:S(2)}) collective-permute-start(bf16[1,104,2048]{2,1,0:T(8,128)(2,1)} %slice.49), channel_id=1, source_target_pairs={{0,15},{1,0},{2,1},{3,2},{4,3},{5,4},{6,5},{7,6},{8,7},{9,8},{10,9... | collective-permute-start | bytes 1277960 | tf_op jit(solution)/shard_map/ppermute | solution.py:57
  94.2 1.9 %collective-permute-start.1 = (bf16[1,24,2048]{2,1,0:T(8,128)(2,1)S(1)}, bf16[1,24,2048]{2,1,0:T(8,128)(2,1)S(1)}, u32[]{:S(2)}, u32[]{:S(2)}) collective-permute-start(bf16[1,24,2048]{2,1,0:T(8,128)(2,1)S(1)} %slice.50), channel_id=1, source_target_pairs={{0,1},{1,2},{2,3},{3,0},{4,5},{5,6},{6,7},{7,4},{8,9},{9,10},{10,1... | collective-permute-start | bytes 294920 | tf_op jit(solution)/shard_map/ppermute | solution.py:60
  96.1 16.2 %collective-permute-done.1 = bf16[1,24,2048]{2,1,0:T(8,128)(2,1)S(1)} collective-permute-done((bf16[1,24,2048]{2,1,0:T(8,128)(2,1)S(1)}, bf16[1,24,2048]{2,1,0:T(8,128)(2,1)S(1)}, u32[]{:S(2)}, u32[]{:S(2)}) %collective-permute-start.1) | collective-permute-done | bytes 98336 | tf_op jit(solution)/shard_map/ppermute | solution.py:60
  112.4 1.9 %collective-permute-start.2 = (bf16[1,24,2048]{2,1,0:T(8,128)(2,1)S(1)}, bf16[1,24,2048]{2,1,0:T(8,128)(2,1)}, u32[]{:S(2)}, u32[]{:S(2)}) collective-permute-start(bf16[1,24,2048]{2,1,0:T(8,128)(2,1)S(1)} %collective-permute-done.1), channel_id=1, source_target_pairs={{0,1},{1,2},{2,3},{3,0},{4,5},{5,6},{6,7},{7,4},{8,9},{9,10},{10,1... | collective-permute-start | bytes 294920 | tf_op jit(solution)/shard_map/ppermute | solution.py:61
  114.3 12.6 %collective-permute-done.2 = bf16[1,24,2048]{2,1,0:T(8,128)(2,1)} collective-permute-done((bf16[1,24,2048]{2,1,0:T(8,128)(2,1)S(1)}, bf16[1,24,2048]{2,1,0:T(8,128)(2,1)}, u32[]{:S(2)}, u32[]{:S(2)}) %collective-permute-start.2) | collective-permute-done | bytes 98336 | tf_op jit(solution)/shard_map/ppermute | solution.py:61
  126.9 7.8 %collective-permute-start.3 = (bf16[1,24,2048]{2,1,0:T(8,128)(2,1)}, bf16[1,24,2048]{2,1,0:T(8,128)(2,1)}, u32[]{:S(2)}, u32[]{:S(2)}) collective-permute-start(bf16[1,24,2048]{2,1,0:T(8,128)(2,1)} %collective-permute-done.2), channel_id=1, source_target_pairs={{0,1},{1,2},{2,15},{3,0},{4,5},{5,6},{6,3},{7,4},{8,9},{9,10},{10,... | collective-permute-start | bytes 294920 | tf_op jit(solution)/shard_map/ppermute | solution.py:63
  134.7 23.1 %all-to-all-start.3 = ((f32[8,8,512]{2,1,0:T(8,128)}), f32[8,8,512]{2,1,0:T(8,128)S(1)}, u32[]{:S(2)}, u32[]{:S(2)}) async-start(f32[8,8,512]{2,1,0:T(8,128)} %bitcast.23), calls=%async_computation.3 | async-start | bytes 262144 | tf_op jit(solution)/shard_map/all_to_all | solution.py:40
  157.9 8.5 %collective-permute-done = bf16[1,104,2048]{2,1,0:T(8,128)(2,1)} collective-permute-done((bf16[1,104,2048]{2,1,0:T(8,128)(2,1)}, bf16[1,104,2048]{2,1,0:T(8,128)(2,1)}, u32[]{:S(2)}, u32[]{:S(2)}) %collective-permute-start) | collective-permute-done | bytes 426016 | tf_op jit(solution)/shard_map/ppermute | solution.py:57
  166.3 1.9 %pad_maximum_fusion = bf16[1,128,2048]{2,1,0:T(8,128)(2,1)} fusion(bf16[1,24,2048]{2,1,0:T(8,128)(2,1)} %collective-permute-done.3, bf16[1,104,2048]{2,1,0:T(8,128)(2,1)} %collective-permute-done), kind=kLoop, calls=%fused_computation.28 | loop fusion | flops 1048576 | bytes 1048576 | tf_op jit(solution)/shard_map/concatenate | solution.py:64
  169.7 4.5 %all-to-all-done.3 = f32[8,8,512]{2,1,0:T(8,128)S(1)} async-done(((f32[8,8,512]{2,1,0:T(8,128)}), f32[8,8,512]{2,1,0:T(8,128)S(1)}, u32[]{:S(2)}, u32[]{:S(2)}) %all-to-all-start.3) | async-done | bytes 131104 | tf_op jit(solution)/shard_map/all_to_all | solution.py:40
  (50 shorter events, 15.5 us)
Async XLA Ops:
  0.6 35.3 %copy-start.3 = (bf16[1,128,2560]{2,1,0:T(8,128)(2,1)S(1)}, bf16[1,128,2560]{2,1,0:T(8,128)(2,1)}, u32[]{:S(2)}) copy-start(bf16[1,128,2560]{2,1,0:T(8,128)(2,1)} %param.6) | copy-start | bytes 1966084
  2.0 22.8 %all-to-all-start = ((bf16[8,8,512]{2,1,0:T(8,128)(2,1)}), bf16[8,8,512]{2,1,0:T(8,128)(2,1)S(1)}, u32[]{:S(2)}, u32[]{:S(2)}) async-start(bf16[8,8,512]{2,1,0:T(8,128)(2,1)} %broadcast_in_dim.74), calls=%async_computation | async-start | bytes 131072 | tf_op jit(solution)/shard_map/all_to_all | solution.py:21
  25.7 19.1 %all-to-all-start.1 = ((bf16[8,64,512]{2,1,0:T(8,128)(2,1)}), bf16[8,64,512]{2,1,0:T(8,128)(2,1)}, u32[]{:S(2)}, u32[]{:S(2)}) async-start(bf16[8,64,512]{2,1,0:T(8,128)(2,1)} %broadcast_in_dim.76), calls=%async_computation.1 | async-start | bytes 1048576 | tf_op jit(solution)/shard_map/all_to_all | solution.py:23
  46.1 3.2 %copy-start.4 = (bf16[320,2,128]{2,1,0:T(2,128)(2,1)}, bf16[320,2,128]{2,1,0:T(2,128)(2,1)S(1)}, u32[]{:S(2)}) copy-start(bf16[320,2,128]{2,1,0:T(2,128)(2,1)S(1)} %reshape.107) | copy-start | bytes 491524
  49.3 2.5 %copy-start.2 = (bf16[320,2,128]{2,1,0:T(2,128)(2,1)S(1)}, bf16[320,2,128]{2,1,0:T(2,128)(2,1)}, u32[]{:S(2)}) copy-start(bf16[320,2,128]{2,1,0:T(2,128)(2,1)} %reshape.109) | copy-start | bytes 491524
  51.4 1.7 copy-start
  53.7 1.2 copy-start.1
  57.4 19.5 %all-to-all-start.2 = ((f32[8,64,512]{2,1,0:T(8,128)}), f32[8,64,512]{2,1,0:T(8,128)S(1)}, u32[]{:S(2)}, u32[]{:S(2)}) async-start(f32[8,64,512]{2,1,0:T(8,128)} %bitcast.86), calls=%async_computation.2 | async-start | bytes 2097152 | tf_op jit(solution)/shard_map/all_to_all | solution.py:35
  77.6 90.7 %slice-start = ((bf16[2,8,128,320]{2,3,1,0:T(8,128)(2,1)}), bf16[2,8,128,128]{2,3,1,0:T(8,128)(2,1)S(1)}, s32[]{:S(2)}) async-start(bf16[2,8,128,320]{2,3,1,0:T(8,128)(2,1)} %copy-done.1), calls=%async_computation.4 | async-start | bytes 1048576 | tf_op jit(solution)/shard_map/slice | solution.py:150
  79.7 86.6 %collective-permute-start = (bf16[1,104,2048]{2,1,0:T(8,128)(2,1)}, bf16[1,104,2048]{2,1,0:T(8,128)(2,1)}, u32[]{:S(2)}, u32[]{:S(2)}) collective-permute-start(bf16[1,104,2048]{2,1,0:T(8,128)(2,1)} %slice.49), channel_id=1, source_target_pairs={{0,15},{1,0},{2,1},{3,2},{4,3},{5,4},{6,5},{7,6},{8,7},{9,8},{10,9... | collective-permute-start | bytes 1277960 | tf_op jit(solution)/shard_map/ppermute | solution.py:57
  94.2 18.2 %collective-permute-start.1 = (bf16[1,24,2048]{2,1,0:T(8,128)(2,1)S(1)}, bf16[1,24,2048]{2,1,0:T(8,128)(2,1)S(1)}, u32[]{:S(2)}, u32[]{:S(2)}) collective-permute-start(bf16[1,24,2048]{2,1,0:T(8,128)(2,1)S(1)} %slice.50), channel_id=1, source_target_pairs={{0,1},{1,2},{2,3},{3,0},{4,5},{5,6},{6,7},{7,4},{8,9},{9,10},{10,1... | collective-permute-start | bytes 294920 | tf_op jit(solution)/shard_map/ppermute | solution.py:60
  112.4 14.5 %collective-permute-start.2 = (bf16[1,24,2048]{2,1,0:T(8,128)(2,1)S(1)}, bf16[1,24,2048]{2,1,0:T(8,128)(2,1)}, u32[]{:S(2)}, u32[]{:S(2)}) collective-permute-start(bf16[1,24,2048]{2,1,0:T(8,128)(2,1)S(1)} %collective-permute-done.1), channel_id=1, source_target_pairs={{0,1},{1,2},{2,3},{3,0},{4,5},{5,6},{6,7},{7,4},{8,9},{9,10},{10,1... | collective-permute-start | bytes 294920 | tf_op jit(solution)/shard_map/ppermute | solution.py:61
  126.9 31.0 %collective-permute-start.3 = (bf16[1,24,2048]{2,1,0:T(8,128)(2,1)}, bf16[1,24,2048]{2,1,0:T(8,128)(2,1)}, u32[]{:S(2)}, u32[]{:S(2)}) collective-permute-start(bf16[1,24,2048]{2,1,0:T(8,128)(2,1)} %collective-permute-done.2), channel_id=1, source_target_pairs={{0,1},{1,2},{2,15},{3,0},{4,5},{5,6},{6,3},{7,4},{8,9},{9,10},{10,... | collective-permute-start | bytes 294920 | tf_op jit(solution)/shard_map/ppermute | solution.py:63
  134.7 39.6 %all-to-all-start.3 = ((f32[8,8,512]{2,1,0:T(8,128)}), f32[8,8,512]{2,1,0:T(8,128)S(1)}, u32[]{:S(2)}, u32[]{:S(2)}) async-start(f32[8,8,512]{2,1,0:T(8,128)} %bitcast.23), calls=%async_computation.3 | async-start | bytes 262144 | tf_op jit(solution)/shard_map/all_to_all | solution.py:40

commit v9 on v6

--- a/solution.py
+++ b/solution.py
@@ -34,7 +34,8 @@
     parts = parts.reshape(near, far * rows, width)
     parts = lax.all_to_all(parts, NEAR, 0, 0, tiled=True).sum(axis=0)
     parts = parts.reshape(far, rows, width)
-    return lax.all_to_all(parts, FAR, 0, 0, tiled=True).sum(axis=0)
+    parts = lax.all_to_all(parts.astype(jnp.bfloat16), FAR, 0, 0, tiled=True)
+    return parts.astype(jnp.float32).sum(axis=0)
 
 
 def around(count, far_count, move):

time: 157 us -> 165 us (1.051); the launches traced: 154 us -> 164 us
  waiting for transfers between devices: 68.3 us -> 81.3 us
  local copies, waits for them, and re-layouts: 12.7 us -> 10.2 us
    ppermute x1, waiting for transfers between devices: 3.59 us -> 11.8 us  [pass_down(): rest = lax.ppermute(rest, axis, last)]
    all_to_all x1, waiting for transfers between devices: 4.15 us -> 7.07 us  [scatter_sum(): parts = lax.all_to_all(parts.astype(jnp.bfloat16), FAR, 0, 0, tiled=True)]
    ppermute x1, waiting for transfers between devices: 6.05 us -> 8.22 us  [pass_down(): lax.ppermute(value[:, :cut], axis, around(count, far_count, lambda n, f:...]
    unnamed x19 -> x17, local copies, waits for them, and re-layouts: 4.48 us -> 3.45 us
  transfers between devices with their start and end apart: 8 -> 8, of which waited for: 7 -> 7; matrix products, arithmetic and copies ran while one was open for 11% -> 9% of each run, Pallas kernels for 0% -> 0%
where the time goes in v9:
time: 165 us; the launch traced here: 164 us
  waiting for transfers between devices  81.3 us (49%)
  starting transfers between devices  55.3 us (34%)
  local copies, waits for them, and re-layouts  10.2 us (6%)
  other arithmetic  8.9 us (5%)
  matrix products  5.54 us (3%)
  between operations  2.87 us (2%)
    ppermute x2, waiting for transfers between devices, pass_down(): rest = lax.ppermute(rest, axis, hop)  44.8 us
    ppermute x1, starting transfers between devices, pass_down(): lax.ppermute(value[:, :cut], axis, around(count, far_count, lambda n, f:...  15.2 us
    all_to_all x1, starting transfers between devices, gather_prefix(): lax.all_to_all(spread, FAR, 0, 0, tiled=True).reshape(far * rows, width)  13.1 us
    ppermute x1, waiting for transfers between devices, pass_down(): rest = lax.ppermute(rest, axis, last)  11.8 us
    all_to_all x1, starting transfers between devices, gather_prefix(): whole = lax.all_to_all(spread, NEAR, 0, 0, tiled=True)  8.92 us
    ppermute x1, waiting for transfers between devices, pass_down(): lax.ppermute(value[:, :cut], axis, around(count, far_count, lambda n, f:...  8.22 us
    all_to_all x1, waiting for transfers between devices, scatter_sum(): parts = lax.all_to_all(parts.astype(jnp.bfloat16), FAR, 0, 0, tiled=True)  7.07 us
    all_to_all x1, starting transfers between devices, scatter_sum(): parts = lax.all_to_all(parts.astype(jnp.bfloat16), FAR, 0, 0, tiled=True)  6.97 us
  transfers between devices with their start and end apart: 8, of which 7 were waited for; matrix products, arithmetic and copies ran while one was open for 9% of the time, Pallas kernels for 0%

profile of v9, /device:TPU:1, one launch (start us, length us, event | category | flops | bytes accessed | tf_op | source)
XLA Modules:
  0.0 164.1 jit_solution(4977075945286047122)
XLA Ops:
  0.6 1.4 broadcast_in_dim.69
  2.0 13.1 %all-to-all-start = ((bf16[8,8,512]{2,1,0:T(8,128)(2,1)}), bf16[8,8,512]{2,1,0:T(8,128)(2,1)S(1)}, u32[]{:S(2)}, u32[]{:S(2)}) async-start(bf16[8,8,512]{2,1,0:T(8,128)(2,1)} %broadcast_in_dim.69), calls=%async_computation | async-start | bytes 131072 | tf_op jit(solution)/shard_map/all_to_all | solution.py:21
  15.1 1.3 fusion.28
  16.4 2.0 %fusion.31 = (s32[]{:T(128)}, s32[]{:T(128)}) fusion(s32[8]{0:T(128)} %param.9, s32[]{:T(128)} %get-tuple-element.17), kind=kLoop, calls=%fused_computation.54 | loop fusion | flops 46 | bytes 44 | tf_op jit(solution)/shard_map/reduce_sum | solution.py:106
  21.0 3.8 %all-to-all-done = bf16[8,8,512]{2,1,0:T(8,128)(2,1)S(1)} async-done(((bf16[8,8,512]{2,1,0:T(8,128)(2,1)}), bf16[8,8,512]{2,1,0:T(8,128)(2,1)S(1)}, u32[]{:S(2)}, u32[]{:S(2)}) %all-to-all-start) | async-done | bytes 65568 | tf_op jit(solution)/shard_map/all_to_all | solution.py:21
  25.7 8.9 %all-to-all-start.1 = ((bf16[8,64,512]{2,1,0:T(8,128)(2,1)}), bf16[8,64,512]{2,1,0:T(8,128)(2,1)S(1)}, u32[]{:S(2)}, u32[]{:S(2)}) async-start(bf16[8,64,512]{2,1,0:T(8,128)(2,1)} %broadcast_in_dim.71), calls=%async_computation.1 | async-start | bytes 1048576 | tf_op jit(solution)/shard_map/all_to_all | solution.py:23
  35.3 1.1 slice.45
  36.6 0.9 copy.103
  38.6 5.5 %all-to-all-done.1 = bf16[8,64,512]{2,1,0:T(8,128)(2,1)S(1)} async-done(((bf16[8,64,512]{2,1,0:T(8,128)(2,1)}), bf16[8,64,512]{2,1,0:T(8,128)(2,1)S(1)}, u32[]{:S(2)}, u32[]{:S(2)}) %all-to-all-start.1) | async-done | bytes 524320 | tf_op jit(solution)/shard_map/all_to_all | solution.py:23
  50.1 1.1 copy.128
  51.2 4.3 %all-to-all-start.2 = ((f32[8,64,512]{2,1,0:T(8,128)}), f32[8,64,512]{2,1,0:T(8,128)S(1)}, u32[]{:S(2)}, u32[]{:S(2)}) async-start(f32[8,64,512]{2,1,0:T(8,128)} %bitcast.88), calls=%async_computation.2 | async-start | bytes 2097152 | tf_op jit(solution)/shard_map/all_to_all | solution.py:35
  56.0 1.0 copy.99
  57.0 15.2 %collective-permute-start = (bf16[1,104,2048]{2,1,0:T(8,128)(2,1)}, bf16[1,104,2048]{2,1,0:T(8,128)(2,1)}, u32[]{:S(2)}, u32[]{:S(2)}) collective-permute-start(bf16[1,104,2048]{2,1,0:T(8,128)(2,1)} %copy.99), channel_id=1, source_target_pairs={{0,15},{1,0},{2,1},{3,2},{4,3},{5,4},{6,5},{7,6},{8,7},{9,8},{10,9... | collective-permute-start | bytes 1277960 | tf_op jit(solution)/shard_map/ppermute | solution.py:55
  72.5 2.1 %collective-permute-start.1 = (bf16[1,24,2048]{2,1,0:T(8,128)(2,1)S(1)}, bf16[1,24,2048]{2,1,0:T(8,128)(2,1)S(1)}, u32[]{:S(2)}, u32[]{:S(2)}) collective-permute-start(bf16[1,24,2048]{2,1,0:T(8,128)(2,1)S(1)} %copy.100), channel_id=1, source_target_pairs={{0,1},{1,2},{2,3},{3,0},{4,5},{5,6},{6,7},{7,4},{8,9},{9,10},{10,1... | collective-permute-start | bytes 294920 | tf_op jit(solution)/shard_map/ppermute | solution.py:58
  74.6 24.0 %collective-permute-done.1 = bf16[1,24,2048]{2,1,0:T(8,128)(2,1)S(1)} collective-permute-done((bf16[1,24,2048]{2,1,0:T(8,128)(2,1)S(1)}, bf16[1,24,2048]{2,1,0:T(8,128)(2,1)S(1)}, u32[]{:S(2)}, u32[]{:S(2)}) %collective-permute-start.1) | collective-permute-done | bytes 98336 | tf_op jit(solution)/shard_map/ppermute | solution.py:58
  98.6 1.9 %collective-permute-start.2 = (bf16[1,24,2048]{2,1,0:T(8,128)(2,1)S(1)}, bf16[1,24,2048]{2,1,0:T(8,128)(2,1)S(1)}, u32[]{:S(2)}, u32[]{:S(2)}) collective-permute-start(bf16[1,24,2048]{2,1,0:T(8,128)(2,1)S(1)} %collective-permute-done.1), channel_id=1, source_target_pairs={{0,1},{1,2},{2,3},{3,0},{4,5},{5,6},{6,7},{7,4},{8,9},{9,10},{10,1... | collective-permute-start | bytes 294920 | tf_op jit(solution)/shard_map/ppermute | solution.py:59
  100.5 20.8 %collective-permute-done.2 = bf16[1,24,2048]{2,1,0:T(8,128)(2,1)S(1)} collective-permute-done((bf16[1,24,2048]{2,1,0:T(8,128)(2,1)S(1)}, bf16[1,24,2048]{2,1,0:T(8,128)(2,1)S(1)}, u32[]{:S(2)}, u32[]{:S(2)}) %collective-permute-start.2) | collective-permute-done | bytes 98336 | tf_op jit(solution)/shard_map/ppermute | solution.py:59
  121.3 2.8 %collective-permute-start.3 = (bf16[1,24,2048]{2,1,0:T(8,128)(2,1)S(1)}, bf16[1,24,2048]{2,1,0:T(8,128)(2,1)S(1)}, u32[]{:S(2)}, u32[]{:S(2)}) collective-permute-start(bf16[1,24,2048]{2,1,0:T(8,128)(2,1)S(1)} %collective-permute-done.2), channel_id=1, source_target_pairs={{0,1},{1,2},{2,15},{3,0},{4,5},{5,6},{6,3},{7,4},{8,9},{9,10},{10,... | collective-permute-start | bytes 294920 | tf_op jit(solution)/shard_map/ppermute | solution.py:61
  124.2 11.8 %collective-permute-done.3 = bf16[1,24,2048]{2,1,0:T(8,128)(2,1)S(1)} collective-permute-done((bf16[1,24,2048]{2,1,0:T(8,128)(2,1)S(1)}, bf16[1,24,2048]{2,1,0:T(8,128)(2,1)S(1)}, u32[]{:S(2)}, u32[]{:S(2)}) %collective-permute-start.3) | collective-permute-done | bytes 98336 | tf_op jit(solution)/shard_map/ppermute | solution.py:61
  136.0 8.2 %collective-permute-done = bf16[1,104,2048]{2,1,0:T(8,128)(2,1)} collective-permute-done((bf16[1,104,2048]{2,1,0:T(8,128)(2,1)}, bf16[1,104,2048]{2,1,0:T(8,128)(2,1)}, u32[]{:S(2)}, u32[]{:S(2)}) %collective-permute-start) | collective-permute-done | bytes 426016 | tf_op jit(solution)/shard_map/ppermute | solution.py:55
  144.2 1.8 %pad_maximum_fusion = bf16[1,128,2048]{2,1,0:T(8,128)(2,1)} fusion(bf16[1,24,2048]{2,1,0:T(8,128)(2,1)S(1)} %collective-permute-done.3, bf16[1,104,2048]{2,1,0:T(8,128)(2,1)} %collective-permute-done), kind=kLoop, calls=%fused_computation.28 | loop fusion | flops 1048576 | bytes 1048576 | tf_op jit(solution)/shard_map/concatenate | solution.py:62
  146.7 7.0 %all-to-all-start.3 = ((bf16[8,8,512]{2,1,0:T(8,128)(2,1)}), bf16[8,8,512]{2,1,0:T(8,128)(2,1)S(1)}, u32[]{:S(2)}, u32[]{:S(2)}) async-start(bf16[8,8,512]{2,1,0:T(8,128)(2,1)} %bitcast.78), calls=%async_computation.3 | async-start | bytes 131072 | tf_op jit(solution)/shard_map/all_to_all | solution.py:37
  153.7 1.3 fusion.12
  156.4 7.1 %all-to-all-done.3 = bf16[8,8,512]{2,1,0:T(8,128)(2,1)S(1)} async-done(((bf16[8,8,512]{2,1,0:T(8,128)(2,1)}), bf16[8,8,512]{2,1,0:T(8,128)(2,1)S(1)}, u32[]{:S(2)}, u32[]{:S(2)}) %all-to-all-start.3) | async-done | bytes 65568 | tf_op jit(solution)/shard_map/all_to_all | solution.py:37
  (53 shorter events, 12.7 us)
Async XLA Ops:
  0.6 36.0 %copy-start.4 = (bf16[1,128,2048]{2,1,0:T(8,128)(2,1)S(1)}, bf16[1,128,2048]{2,1,0:T(8,128)(2,1)}, u32[]{:S(2)}) copy-start(bf16[1,128,2048]{2,1,0:T(8,128)(2,1)} %param.7) | copy-start | bytes 1572868
  2.0 22.8 %all-to-all-start = ((bf16[8,8,512]{2,1,0:T(8,128)(2,1)}), bf16[8,8,512]{2,1,0:T(8,128)(2,1)S(1)}, u32[]{:S(2)}, u32[]{:S(2)}) async-start(bf16[8,8,512]{2,1,0:T(8,128)(2,1)} %broadcast_in_dim.69), calls=%async_computation | async-start | bytes 131072 | tf_op jit(solution)/shard_map/all_to_all | solution.py:21
  25.7 18.4 %all-to-all-start.1 = ((bf16[8,64,512]{2,1,0:T(8,128)(2,1)}), bf16[8,64,512]{2,1,0:T(8,128)(2,1)S(1)}, u32[]{:S(2)}, u32[]{:S(2)}) async-start(bf16[8,64,512]{2,1,0:T(8,128)(2,1)} %broadcast_in_dim.71), calls=%async_computation.1 | async-start | bytes 1048576 | tf_op jit(solution)/shard_map/all_to_all | solution.py:23
  36.6 11.8 %copy-start.3 = (bf16[128,2048]{0,1:T(8,128)(2,1)}, bf16[128,2048]{0,1:T(8,128)(2,1)S(1)}, u32[]{:S(2)}) copy-start(bf16[128,2048]{0,1:T(8,128)(2,1)S(1)} %copy.54) | copy-start | bytes 1572868
  45.4 1.0 copy-start.5
  45.7 2.1 %copy-start.2 = (bf16[2,8,128,320]{2,3,1,0:T(8,128)(2,1)}, bf16[2,8,128,320]{2,3,1,0:T(8,128)(2,1)S(1)}, u32[]{:S(2)}) copy-start(bf16[2,8,128,320]{2,3,1,0:T(8,128)(2,1)S(1)} %fusion.14) | copy-start | bytes 3932164
  48.4 1.1 copy-start
  49.6 5.9 %copy-start.1 = (bf16[2,8,128,320]{2,3,1,0:T(8,128)(2,1)S(1)}, bf16[2,8,128,320]{2,3,1,0:T(8,128)(2,1)}, u32[]{:S(2)}) copy-start(bf16[2,8,128,320]{2,3,1,0:T(8,128)(2,1)} %copy-done) | copy-start | bytes 3932164
  51.2 94.9 %all-to-all-start.2 = ((f32[8,64,512]{2,1,0:T(8,128)}), f32[8,64,512]{2,1,0:T(8,128)S(1)}, u32[]{:S(2)}, u32[]{:S(2)}) async-start(f32[8,64,512]{2,1,0:T(8,128)} %bitcast.88), calls=%async_computation.2 | async-start | bytes 2097152 | tf_op jit(solution)/shard_map/all_to_all | solution.py:35
  57.0 87.3 %collective-permute-start = (bf16[1,104,2048]{2,1,0:T(8,128)(2,1)}, bf16[1,104,2048]{2,1,0:T(8,128)(2,1)}, u32[]{:S(2)}, u32[]{:S(2)}) collective-permute-start(bf16[1,104,2048]{2,1,0:T(8,128)(2,1)} %copy.99), channel_id=1, source_target_pairs={{0,15},{1,0},{2,1},{3,2},{4,3},{5,4},{6,5},{7,6},{8,7},{9,8},{10,9... | collective-permute-start | bytes 1277960 | tf_op jit(solution)/shard_map/ppermute | solution.py:55
  72.3 81.4 %slice-start = ((bf16[2,8,128,320]{2,3,1,0:T(8,128)(2,1)}), bf16[2,8,128,128]{2,3,1,0:T(8,128)(2,1)S(1)}, s32[]{:S(2)}) async-start(bf16[2,8,128,320]{2,3,1,0:T(8,128)(2,1)} %copy-done), calls=%async_computation.4 | async-start | bytes 1048576 | tf_op jit(solution)/shard_map/slice | solution.py:147
  72.5 82.7 %slice-start.1 = ((bf16[2,8,128,320]{2,3,1,0:T(8,128)(2,1)}), bf16[2,8,128,128]{2,3,1,0:T(8,128)(2,1)S(1)}, s32[]{:S(2)}) async-start(bf16[2,8,128,320]{2,3,1,0:T(8,128)(2,1)} %copy-done.2), calls=%async_computation.5 | async-start | bytes 1048576 | tf_op jit(solution)/shard_map/slice | solution.py:147
  72.5 26.1 %collective-permute-start.1 = (bf16[1,24,2048]{2,1,0:T(8,128)(2,1)S(1)}, bf16[1,24,2048]{2,1,0:T(8,128)(2,1)S(1)}, u32[]{:S(2)}, u32[]{:S(2)}) collective-permute-start(bf16[1,24,2048]{2,1,0:T(8,128)(2,1)S(1)} %copy.100), channel_id=1, source_target_pairs={{0,1},{1,2},{2,3},{3,0},{4,5},{5,6},{6,7},{7,4},{8,9},{9,10},{10,1... | collective-permute-start | bytes 294920 | tf_op jit(solution)/shard_map/ppermute | solution.py:58
  98.6 22.8 %collective-permute-start.2 = (bf16[1,24,2048]{2,1,0:T(8,128)(2,1)S(1)}, bf16[1,24,2048]{2,1,0:T(8,128)(2,1)S(1)}, u32[]{:S(2)}, u32[]{:S(2)}) collective-permute-start(bf16[1,24,2048]{2,1,0:T(8,128)(2,1)S(1)} %collective-permute-done.1), channel_id=1, source_target_pairs={{0,1},{1,2},{2,3},{3,0},{4,5},{5,6},{6,7},{7,4},{8,9},{9,10},{10,1... | collective-permute-start | bytes 294920 | tf_op jit(solution)/shard_map/ppermute | solution.py:59
  121.3 14.7 %collective-permute-start.3 = (bf16[1,24,2048]{2,1,0:T(8,128)(2,1)S(1)}, bf16[1,24,2048]{2,1,0:T(8,128)(2,1)S(1)}, u32[]{:S(2)}, u32[]{:S(2)}) collective-permute-start(bf16[1,24,2048]{2,1,0:T(8,128)(2,1)S(1)} %collective-permute-done.2), channel_id=1, source_target_pairs={{0,1},{1,2},{2,15},{3,0},{4,5},{5,6},{6,3},{7,4},{8,9},{9,10},{10,... | collective-permute-start | bytes 294920 | tf_op jit(solution)/shard_map/ppermute | solution.py:61
  124.2 31.0 %copy-start.6 = (bf16[16,8,16,128]{3,2,1,0:T(8,128)(2,1)S(1)}, bf16[16,8,16,128]{3,2,1,0:T(8,128)(2,1)}, u32[]{:S(2)}) copy-start(bf16[16,8,16,128]{3,2,1,0:T(8,128)(2,1)} %copy.103) | copy-start | bytes 1572868
  146.7 16.7 %all-to-all-start.3 = ((bf16[8,8,512]{2,1,0:T(8,128)(2,1)}), bf16[8,8,512]{2,1,0:T(8,128)(2,1)S(1)}, u32[]{:S(2)}, u32[]{:S(2)}) async-start(bf16[8,8,512]{2,1,0:T(8,128)(2,1)} %bitcast.78), calls=%async_computation.3 | async-start | bytes 131072 | tf_op jit(solution)/shard_map/all_to_all | solution.py:37

commit v10 on v6

--- a/solution.py
+++ b/solution.py
@@ -121,7 +121,10 @@
     q_four = queries.reshape(count, KV_HEADS, per, HEAD_DIM)
     d_four = dout.reshape(count, KV_HEADS, per, HEAD_DIM)
     v_three = values.reshape(total_keys, KV_HEADS, HEAD_DIM)
-    scores = jnp.where(allowed[None, None], score_block(q_four, keys), jnp.float32(-1e30))
+    raw = jnp.concatenate(
+        [score_block(q_four, window_rows[:, :kv_width]), score_block(q_four, own_keys)], axis=-1
+    )
+    scores = jnp.where(allowed[None, None], raw, jnp.float32(-1e30))
     top = jnp.max(scores, axis=-1, keepdims=True)
     expo = jnp.exp(scores - top)
     denom = jnp.sum(expo, axis=-1, keepdims=True)
@@ -129,7 +132,15 @@
     w_low = weights.astype(jnp.bfloat16)
     output = jnp.einsum("gqrm,mgh->gqrh", w_low, v_three, preferred_element_type=jnp.float32)
     delta = jnp.einsum("rgqh,gqrh->gqr", d_four.astype(jnp.float32), output)
-    dprob = jnp.einsum("rgqh,mgh->gqrm", d_four, v_three, preferred_element_type=jnp.float32)
+    v_window = window_rows[:, kv_width:].reshape(window, KV_HEADS, HEAD_DIM)
+    v_own = own_values.reshape(count, KV_HEADS, HEAD_DIM)
+    dprob = jnp.concatenate(
+        [
+            jnp.einsum("rgqh,mgh->gqrm", d_four, v_window, preferred_element_type=jnp.float32),
+            jnp.einsum("rgqh,mgh->gqrm", d_four, v_own, preferred_element_type=jnp.float32),
+        ],
+        axis=-1,
+    )
     d_low = (weights * (dprob - delta[..., None])).astype(jnp.bfloat16)
     k_three = keys.reshape(total_keys, KV_HEADS, HEAD_DIM)
     grad_q = jnp.einsum(

time: 157 us -> 163 us (1.038)
  starting transfers between devices: 56.1 us -> 77.4 us
  waiting for transfers between devices: 68.3 us -> 47.4 us
  other arithmetic: 8.98 us -> 14.9 us
  matrix products: 5.41 us -> 7.5 us
    all_to_all x1, starting transfers between devices: 8.16 us -> 23.8 us  [scatter_sum(): return lax.all_to_all(parts, FAR, 0, 0, tiled=True).sum(axis=0)]
    ppermute x2, waiting for transfers between devices: 45 us -> 31.7 us  [pass_down(): rest = lax.ppermute(rest, axis, hop)]
    ppermute x1, waiting for transfers between devices: 6.05 us -> 0.01 us  [pass_down(): lax.ppermute(value[:, :cut], axis, around(count, far_count, lambda n, f:...]
    ppermute x1, starting transfers between devices: 2.51 us -> 8.36 us  [pass_down(): rest = lax.ppermute(rest, axis, last)]
    dot_general x1 -> x4, matrix products: 0.65 us -> 4.61 us  [the longest x2 3.77 us: score_block(): jnp.einsum('rgqh,mgh->gqrm', q_four, k_three, preferred_element_type=jnp....]
    all_to_all x1, waiting for transfers between devices: 3.9 us -> 0.01 us  [gather_prefix(): lax.all_to_all(spread, FAR, 0, 0, tiled=True).reshape(far * rows, width)]
    ppermute x1, waiting for transfers between devices: 3.59 us -> 0.01 us  [pass_down(): rest = lax.ppermute(rest, axis, last)]
    all_to_all x1, waiting for transfers between devices: 5.59 us -> 9 us  [gather_prefix(): whole = lax.all_to_all(spread, NEAR, 0, 0, tiled=True)]
  transfers between devices with their start and end apart: 8 -> 8, of which waited for: 7 -> 4; matrix products, arithmetic and copies ran while one was open for 11% -> 11% of each run, Pallas kernels for 0% -> 0%
where the time goes in v10:
time: 163 us; the launch traced here: 161 us
  starting transfers between devices  77.4 us (47%)
  waiting for transfers between devices  47.4 us (29%)
  other arithmetic  14.9 us (9%)
  local copies, waits for them, and re-layouts  11.2 us (7%)
  matrix products  7.5 us (5%)
  between operations  2.92 us (2%)
    ppermute x2, waiting for transfers between devices, pass_down(): rest = lax.ppermute(rest, axis, hop)  31.7 us
    all_to_all x1, starting transfers between devices, scatter_sum(): return lax.all_to_all(parts, FAR, 0, 0, tiled=True).sum(axis=0)  23.8 us
    ppermute x1, starting transfers between devices, pass_down(): lax.ppermute(value[:, :cut], axis, around(count, far_count, lambda n, f:...  15 us
    all_to_all x1, starting transfers between devices, gather_prefix(): lax.all_to_all(spread, FAR, 0, 0, tiled=True).reshape(far * rows, width)  13.1 us
    all_to_all x1, waiting for transfers between devices, gather_prefix(): whole = lax.all_to_all(spread, NEAR, 0, 0, tiled=True)  9 us
    ppermute x1, starting transfers between devices, pass_down(): rest = lax.ppermute(rest, axis, last)  8.36 us
    all_to_all x1, starting transfers between devices, gather_prefix(): whole = lax.all_to_all(spread, NEAR, 0, 0, tiled=True)  7.84 us
    all_to_all x1, waiting for transfers between devices, scatter_sum(): return lax.all_to_all(parts, FAR, 0, 0, tiled=True).sum(axis=0)  6.69 us
  transfers between devices with their start and end apart: 8, of which 4 were waited for; matrix products, arithmetic and copies ran while one was open for 11% of the time, Pallas kernels for 0%

profile of v10, /device:TPU:1, one launch (start us, length us, event | category | flops | bytes accessed | tf_op | source)
XLA Modules:
  0.0 161.3 jit_solution(2292904305463524901)
XLA Ops:
  0.7 1.4 broadcast_in_dim.67
  2.0 13.1 %all-to-all-start = ((bf16[8,8,512]{2,1,0:T(8,128)(2,1)}), bf16[8,8,512]{2,1,0:T(8,128)(2,1)S(1)}, u32[]{:S(2)}, u32[]{:S(2)}) async-start(bf16[8,8,512]{2,1,0:T(8,128)(2,1)} %broadcast_in_dim.67), calls=%async_computation | async-start | bytes 131072 | tf_op jit(solution)/shard_map/all_to_all | solution.py:21
  15.1 1.1 slice.47
  17.1 1.3 fusion.21
  18.4 2.0 %fusion.24 = (s32[]{:T(128)}, s32[]{:T(128)}) fusion(s32[8]{0:T(128)} %param.9, s32[]{:T(128)} %fusion.21), kind=kLoop, calls=%fused_computation.55 | loop fusion | flops 46 | bytes 44 | tf_op jit(solution)/shard_map/reduce_sum | solution.py:105
  24.9 1.3 fusion.4
  27.1 7.8 %all-to-all-start.1 = ((bf16[8,64,512]{2,1,0:T(8,128)(2,1)}), bf16[8,64,512]{2,1,0:T(8,128)(2,1)S(1)}, u32[]{:S(2)}, u32[]{:S(2)}) async-start(bf16[8,64,512]{2,1,0:T(8,128)(2,1)} %broadcast_in_dim.69), calls=%async_computation.1 | async-start | bytes 1048576 | tf_op jit(solution)/shard_map/all_to_all | solution.py:23
  35.4 9.0 %all-to-all-done.1 = bf16[8,64,512]{2,1,0:T(8,128)(2,1)S(1)} async-done(((bf16[8,64,512]{2,1,0:T(8,128)(2,1)}), bf16[8,64,512]{2,1,0:T(8,128)(2,1)S(1)}, u32[]{:S(2)}, u32[]{:S(2)}) %all-to-all-start.1) | async-done | bytes 524320 | tf_op jit(solution)/shard_map/all_to_all | solution.py:23
  46.1 2.5 %multiply_bitcast_fusion = f32[2,8,128,192]{2,3,1,0:T(8,128)} fusion(bf16[128,2,8,128]{0,3,2,1:T(8,128)(2,1)S(1)} %bitcast.101, bf16[192,2,128,1]{2,1,0,3:T(2,128)(2,1)} %bitcast.121), kind=kOutput, calls=%fused_computation.7 | convolution fusion | flops 101056512 | bytes 2195456 | tf_op jit(solution)/shard_map/rgqh,mgh->gqrm/dot_general | solution.py:73
  49.2 2.1 %fusion.28 = (f32[2,8,128]{2,1,0:T(8,128)S(1)}, f32[2,8,128,320]{2,3,1,0:T(8,128)S(1)}) fusion(f32[2,8,128,128]{2,3,1,0:T(8,128)S(1)} %copy-done.2, f32[2,8,128,192]{2,3,1,0:T(8,128)} %multiply_bitcast_fusion, pred[128,320]{0,1:T(8,128)(4,1)S(1)} %pad_add_fusion), kind=kOutput, calls=%fused_computation.61 | output fusion | flops 2621759 | bytes 5292032 | tf_op jit(solution)/shard_map/sub | solution.py:129
  55.9 1.3 dynamic_update_slice.3
  57.2 1.1 copy.167
  58.3 5.1 %all-to-all-start.2 = ((f32[8,64,512]{2,1,0:T(8,128)}), f32[8,64,512]{2,1,0:T(8,128)}, u32[]{:S(2)}, u32[]{:S(2)}) async-start(f32[8,64,512]{2,1,0:T(8,128)} %bitcast.96), calls=%async_computation.2 | async-start | bytes 2097152 | tf_op jit(solution)/shard_map/all_to_all | solution.py:35
  63.9 1.0 copy.144
  64.9 15.0 %collective-permute-start = (bf16[1,104,2048]{2,1,0:T(8,128)(2,1)}, bf16[1,104,2048]{2,1,0:T(8,128)(2,1)}, u32[]{:S(2)}, u32[]{:S(2)}) collective-permute-start(bf16[1,104,2048]{2,1,0:T(8,128)(2,1)} %copy.144), channel_id=1, source_target_pairs={{0,15},{1,0},{2,1},{3,2},{4,3},{5,4},{6,5},{7,6},{8,7},{9,8},{10,9... | collective-permute-start | bytes 1277960 | tf_op jit(solution)/shard_map/ppermute | solution.py:54
  80.3 1.9 %collective-permute-start.1 = (bf16[1,24,2048]{2,1,0:T(8,128)(2,1)S(1)}, bf16[1,24,2048]{2,1,0:T(8,128)(2,1)S(1)}, u32[]{:S(2)}, u32[]{:S(2)}) collective-permute-start(bf16[1,24,2048]{2,1,0:T(8,128)(2,1)S(1)} %copy.145), channel_id=1, source_target_pairs={{0,1},{1,2},{2,3},{3,0},{4,5},{5,6},{6,7},{7,4},{8,9},{9,10},{10,1... | collective-permute-start | bytes 294920 | tf_op jit(solution)/shard_map/ppermute | solution.py:57
  82.2 12.9 %collective-permute-done.1 = bf16[1,24,2048]{2,1,0:T(8,128)(2,1)S(1)} collective-permute-done((bf16[1,24,2048]{2,1,0:T(8,128)(2,1)S(1)}, bf16[1,24,2048]{2,1,0:T(8,128)(2,1)S(1)}, u32[]{:S(2)}, u32[]{:S(2)}) %collective-permute-start.1) | collective-permute-done | bytes 98336 | tf_op jit(solution)/shard_map/ppermute | solution.py:57
  95.2 2.3 %collective-permute-start.2 = (bf16[1,24,2048]{2,1,0:T(8,128)(2,1)S(1)}, bf16[1,24,2048]{2,1,0:T(8,128)(2,1)S(1)}, u32[]{:S(2)}, u32[]{:S(2)}) collective-permute-start(bf16[1,24,2048]{2,1,0:T(8,128)(2,1)S(1)} %collective-permute-done.1), channel_id=1, source_target_pairs={{0,1},{1,2},{2,3},{3,0},{4,5},{5,6},{6,7},{7,4},{8,9},{9,10},{10,1... | collective-permute-start | bytes 294920 | tf_op jit(solution)/shard_map/ppermute | solution.py:58
  97.5 18.8 %collective-permute-done.2 = bf16[1,24,2048]{2,1,0:T(8,128)(2,1)S(1)} collective-permute-done((bf16[1,24,2048]{2,1,0:T(8,128)(2,1)S(1)}, bf16[1,24,2048]{2,1,0:T(8,128)(2,1)S(1)}, u32[]{:S(2)}, u32[]{:S(2)}) %collective-permute-start.2) | collective-permute-done | bytes 98336 | tf_op jit(solution)/shard_map/ppermute | solution.py:58
  116.3 8.4 %collective-permute-start.3 = (bf16[1,24,2048]{2,1,0:T(8,128)(2,1)S(1)}, bf16[1,24,2048]{2,1,0:T(8,128)(2,1)S(1)}, u32[]{:S(2)}, u32[]{:S(2)}) collective-permute-start(bf16[1,24,2048]{2,1,0:T(8,128)(2,1)S(1)} %collective-permute-done.2), channel_id=1, source_target_pairs={{0,1},{1,2},{2,15},{3,0},{4,5},{5,6},{6,3},{7,4},{8,9},{9,10},{10,... | collective-permute-start | bytes 294920 | tf_op jit(solution)/shard_map/ppermute | solution.py:60
  124.7 2.0 %reduce_sum.68 = f32[64,512]{1,0:T(8,128)} reduce(f32[8,64,512]{2,1,0:T(8,128)} %all-to-all-done.2, f32[]{:T(128)} %constant.13.clone.1), dimensions={0}, to_apply=%region_6.7 | reduce | flops 229376 | bytes 1179652 | tf_op jit(solution)/shard_map/reduce_sum | solution.py:35
  126.6 23.8 %all-to-all-start.3 = ((f32[8,8,512]{2,1,0:T(8,128)}), f32[8,8,512]{2,1,0:T(8,128)S(1)}, u32[]{:S(2)}, u32[]{:S(2)}) async-start(f32[8,8,512]{2,1,0:T(8,128)} %bitcast.40), calls=%async_computation.3 | async-start | bytes 262144 | tf_op jit(solution)/shard_map/all_to_all | solution.py:37
  150.5 1.9 %pad_maximum_fusion = bf16[1,128,2048]{2,1,0:T(8,128)(2,1)} fusion(bf16[1,24,2048]{2,1,0:T(8,128)(2,1)S(1)} %collective-permute-done.3, bf16[1,104,2048]{2,1,0:T(8,128)(2,1)} %collective-permute-done), kind=kLoop, calls=%fused_computation.32 | loop fusion | flops 1048576 | bytes 1048576 | tf_op jit(solution)/shard_map/concatenate | solution.py:61
  154.0 6.7 %all-to-all-done.3 = f32[8,8,512]{2,1,0:T(8,128)S(1)} async-done(((f32[8,8,512]{2,1,0:T(8,128)}), f32[8,8,512]{2,1,0:T(8,128)S(1)}, u32[]{:S(2)}, u32[]{:S(2)}) %all-to-all-start.3) | async-done | bytes 131104 | tf_op jit(solution)/shard_map/all_to_all | solution.py:37
  (63 shorter events, 14.7 us)
Async XLA Ops:
  0.6 22.7 %copy-start.7 = (s32[64]{0:T(128)S(1)}, s32[64]{0:T(128)}, u32[]{:S(2)}) copy-start(s32[64]{0:T(128)} %param.10) | copy-start | bytes 772
  0.6 23.4 %copy-start.5 = (bf16[1,128,2048]{2,1,0:T(8,128)(2,1)S(1)}, bf16[1,128,2048]{2,1,0:T(8,128)(2,1)}, u32[]{:S(2)}) copy-start(bf16[1,128,2048]{2,1,0:T(8,128)(2,1)} %param.7) | copy-start | bytes 1572868
  2.0 24.2 %all-to-all-start = ((bf16[8,8,512]{2,1,0:T(8,128)(2,1)}), bf16[8,8,512]{2,1,0:T(8,128)(2,1)S(1)}, u32[]{:S(2)}, u32[]{:S(2)}) async-start(bf16[8,8,512]{2,1,0:T(8,128)(2,1)} %broadcast_in_dim.67), calls=%async_computation | async-start | bytes 131072 | tf_op jit(solution)/shard_map/all_to_all | solution.py:21
  27.1 17.3 %all-to-all-start.1 = ((bf16[8,64,512]{2,1,0:T(8,128)(2,1)}), bf16[8,64,512]{2,1,0:T(8,128)(2,1)S(1)}, u32[]{:S(2)}, u32[]{:S(2)}) async-start(bf16[8,64,512]{2,1,0:T(8,128)(2,1)} %broadcast_in_dim.69), calls=%async_computation.1 | async-start | bytes 1048576 | tf_op jit(solution)/shard_map/all_to_all | solution.py:23
  45.3 4.0 %copy-start.2 = (f32[2,8,128,128]{2,3,1,0:T(8,128)S(1)}, f32[2,8,128,128]{2,3,1,0:T(8,128)}, u32[]{:S(2)}) copy-start(f32[2,8,128,128]{2,3,1,0:T(8,128)} %fusion.4) | copy-start | bytes 3145732
  46.0 2.5 %copy-start.4 = (bf16[320,256]{1,0:T(8,128)(2,1)S(1)}, bf16[320,256]{1,0:T(8,128)(2,1)}, u32[]{:S(2)}) copy-start(bf16[320,256]{1,0:T(8,128)(2,1)} %get-tuple-element.18) | copy-start | bytes 491524
  51.6 2.0 %copy-start.1 = (bf16[2,8,128,320]{2,3,1,0:T(8,128)(2,1)}, bf16[2,8,128,320]{2,3,1,0:T(8,128)(2,1)S(1)}, u32[]{:S(2)}) copy-start(bf16[2,8,128,320]{2,3,1,0:T(8,128)(2,1)S(1)} %fusion.14) | copy-start | bytes 3932164
  51.6 1.1 copy-start.6
  54.6 95.9 %copy-start = (bf16[2,8,128,320]{2,3,1,0:T(8,128)(2,1)}, bf16[2,8,128,320]{2,3,1,0:T(8,128)(2,1)S(1)}, u32[]{:S(2)}) copy-start(bf16[2,8,128,320]{2,3,1,0:T(8,128)(2,1)S(1)} %fusion.2) | copy-start | bytes 3932164
  58.3 5.1 %copy-start.3 = (bf16[320,256]{1,0:T(8,128)(2,1)S(1)}, bf16[320,256]{1,0:T(8,128)(2,1)}, u32[]{:S(2)}) copy-start(bf16[320,256]{1,0:T(8,128)(2,1)} %get-tuple-element.17) | copy-start | bytes 491524
  58.3 66.4 %all-to-all-start.2 = ((f32[8,64,512]{2,1,0:T(8,128)}), f32[8,64,512]{2,1,0:T(8,128)}, u32[]{:S(2)}, u32[]{:S(2)}) async-start(f32[8,64,512]{2,1,0:T(8,128)} %bitcast.96), calls=%async_computation.2 | async-start | bytes 2097152 | tf_op jit(solution)/shard_map/all_to_all | solution.py:35
  64.9 85.6 %collective-permute-start = (bf16[1,104,2048]{2,1,0:T(8,128)(2,1)}, bf16[1,104,2048]{2,1,0:T(8,128)(2,1)}, u32[]{:S(2)}, u32[]{:S(2)}) collective-permute-start(bf16[1,104,2048]{2,1,0:T(8,128)(2,1)} %copy.144), channel_id=1, source_target_pairs={{0,15},{1,0},{2,1},{3,2},{4,3},{5,4},{6,5},{7,6},{8,7},{9,8},{10,9... | collective-permute-start | bytes 1277960 | tf_op jit(solution)/shard_map/ppermute | solution.py:54
  80.3 14.9 %collective-permute-start.1 = (bf16[1,24,2048]{2,1,0:T(8,128)(2,1)S(1)}, bf16[1,24,2048]{2,1,0:T(8,128)(2,1)S(1)}, u32[]{:S(2)}, u32[]{:S(2)}) collective-permute-start(bf16[1,24,2048]{2,1,0:T(8,128)(2,1)S(1)} %copy.145), channel_id=1, source_target_pairs={{0,1},{1,2},{2,3},{3,0},{4,5},{5,6},{6,7},{7,4},{8,9},{9,10},{10,1... | collective-permute-start | bytes 294920 | tf_op jit(solution)/shard_map/ppermute | solution.py:57
  95.2 21.1 %collective-permute-start.2 = (bf16[1,24,2048]{2,1,0:T(8,128)(2,1)S(1)}, bf16[1,24,2048]{2,1,0:T(8,128)(2,1)S(1)}, u32[]{:S(2)}, u32[]{:S(2)}) collective-permute-start(bf16[1,24,2048]{2,1,0:T(8,128)(2,1)S(1)} %collective-permute-done.1), channel_id=1, source_target_pairs={{0,1},{1,2},{2,3},{3,0},{4,5},{5,6},{6,7},{7,4},{8,9},{9,10},{10,1... | collective-permute-start | bytes 294920 | tf_op jit(solution)/shard_map/ppermute | solution.py:58
  116.3 34.2 %collective-permute-start.3 = (bf16[1,24,2048]{2,1,0:T(8,128)(2,1)S(1)}, bf16[1,24,2048]{2,1,0:T(8,128)(2,1)S(1)}, u32[]{:S(2)}, u32[]{:S(2)}) collective-permute-start(bf16[1,24,2048]{2,1,0:T(8,128)(2,1)S(1)} %collective-permute-done.2), channel_id=1, source_target_pairs={{0,1},{1,2},{2,15},{3,0},{4,5},{5,6},{6,3},{7,4},{8,9},{9,10},{10,... | collective-permute-start | bytes 294920 | tf_op jit(solution)/shard_map/ppermute | solution.py:60
  126.6 34.1 %all-to-all-start.3 = ((f32[8,8,512]{2,1,0:T(8,128)}), f32[8,8,512]{2,1,0:T(8,128)S(1)}, u32[]{:S(2)}, u32[]{:S(2)}) async-start(f32[8,8,512]{2,1,0:T(8,128)} %bitcast.40), calls=%async_computation.3 | async-start | bytes 262144 | tf_op jit(solution)/shard_map/all_to_all | solution.py:37
  150.4 2.0 %slice-start = ((bf16[2,8,128,320]{2,3,1,0:T(8,128)(2,1)}), bf16[2,8,128,128]{2,3,1,0:T(8,128)(2,1)S(1)}, s32[]{:S(2)}) async-start(bf16[2,8,128,320]{2,3,1,0:T(8,128)(2,1)} %copy-done), calls=%async_computation.4 | async-start | bytes 1048576 | tf_op jit(solution)/shard_map/slice | solution.py:157
  150.4 2.4 %slice-start.1 = ((bf16[2,8,128,320]{2,3,1,0:T(8,128)(2,1)}), bf16[2,8,128,128]{2,3,1,0:T(8,128)(2,1)S(1)}, s32[]{:S(2)}) async-start(bf16[2,8,128,320]{2,3,1,0:T(8,128)(2,1)} %copy-done.1), calls=%async_computation.5 | async-start | bytes 1048576 | tf_op jit(solution)/shard_map/slice | solution.py:157

commit v11 on v6

--- a/solution.py
+++ b/solution.py
@@ -50,7 +50,7 @@
     count = lax.axis_size(axis)
     far_count = lax.axis_size(axis[1])
     rows = value.shape[1]
-    cut = rows - 3 * rows // 16
+    cut = rows - rows // 4
     direct = lax.ppermute(value[:, :cut], axis, around(count, far_count, lambda n, f: (n - (f == 0), f - 1)))
     rest = value[:, cut:]
     hop = around(count, far_count, lambda n, f: (n, f + 1))

time: 157 us -> 158 us (level)
  starting transfers between devices: 56.1 us -> 85.8 us
  waiting for transfers between devices: 68.3 us -> 44.3 us
  local copies, waits for them, and re-layouts: 12.7 us -> 10.3 us
    ppermute x2, waiting for transfers between devices: 45 us -> 18.1 us  [pass_down(): rest = lax.ppermute(rest, axis, hop)]
    all_to_all x1, starting transfers between devices: 8.16 us -> 29.3 us  [scatter_sum(): return lax.all_to_all(parts, FAR, 0, 0, tiled=True).sum(axis=0)]
    ppermute x2, starting transfers between devices: 3.83 us -> 23.9 us  [pass_down(): rest = lax.ppermute(rest, axis, hop)]
    ppermute x1, starting transfers between devices: 15.1 us -> 4.14 us  [pass_down(): lax.ppermute(value[:, :cut], axis, around(count, far_count, lambda n, f:...]
    ppermute x1, waiting for transfers between devices: 6.05 us -> 15.2 us  [pass_down(): lax.ppermute(value[:, :cut], axis, around(count, far_count, lambda n, f:...]
    ppermute x1, waiting for transfers between devices: 3.59 us -> 0.01 us  [pass_down(): rest = lax.ppermute(rest, axis, last)]
    all_to_all x1, waiting for transfers between devices: 4.15 us -> 1.52 us  [scatter_sum(): return lax.all_to_all(parts, FAR, 0, 0, tiled=True).sum(axis=0)]
  transfers between devices with their start and end apart: 8 -> 8, of which waited for: 7 -> 5; matrix products, arithmetic and copies ran while one was open for 11% -> 9% of each run, Pallas kernels for 0% -> 0%
where the time goes in v11:
time: 158 us; the launch traced here: 157 us
  starting transfers between devices  85.8 us (54%)
  waiting for transfers between devices  44.3 us (28%)
  local copies, waits for them, and re-layouts  10.3 us (7%)
  other arithmetic  8.98 us (6%)
  matrix products  4.49 us (3%)
  between operations  2.83 us (2%)
    all_to_all x1, starting transfers between devices, scatter_sum(): return lax.all_to_all(parts, FAR, 0, 0, tiled=True).sum(axis=0)  29.3 us
    ppermute x2, starting transfers between devices, pass_down(): rest = lax.ppermute(rest, axis, hop)  23.9 us
    ppermute x2, waiting for transfers between devices, pass_down(): rest = lax.ppermute(rest, axis, hop)  18.1 us
    ppermute x1, waiting for transfers between devices, pass_down(): lax.ppermute(value[:, :cut], axis, around(count, far_count, lambda n, f:...  15.2 us
    all_to_all x1, starting transfers between devices, gather_prefix(): lax.all_to_all(spread, FAR, 0, 0, tiled=True).reshape(far * rows, width)  13.1 us
    all_to_all x1, starting transfers between devices, gather_prefix(): whole = lax.all_to_all(spread, NEAR, 0, 0, tiled=True)  8.92 us
    all_to_all x1, waiting for transfers between devices, gather_prefix(): whole = lax.all_to_all(spread, NEAR, 0, 0, tiled=True)  5.53 us
    all_to_all x1, starting transfers between devices, scatter_sum(): parts = lax.all_to_all(parts, NEAR, 0, 0, tiled=True).sum(axis=0)  4.33 us
  transfers between devices with their start and end apart: 8, of which 5 were waited for; matrix products, arithmetic and copies ran while one was open for 9% of the time, Pallas kernels for 0%

profile of v11, /device:TPU:1, one launch (start us, length us, event | category | flops | bytes accessed | tf_op | source)
XLA Modules:
  0.0 156.7 jit_solution(2540334707965956384)
XLA Ops:
  0.6 1.4 broadcast_in_dim.67
  2.0 13.1 %all-to-all-start = ((bf16[8,8,512]{2,1,0:T(8,128)(2,1)}), bf16[8,8,512]{2,1,0:T(8,128)(2,1)S(1)}, u32[]{:S(2)}, u32[]{:S(2)}) async-start(bf16[8,8,512]{2,1,0:T(8,128)(2,1)} %broadcast_in_dim.67), calls=%async_computation | async-start | bytes 131072 | tf_op jit(solution)/shard_map/all_to_all | solution.py:21
  15.1 1.3 fusion.28
  16.4 2.0 %fusion.31 = (s32[]{:T(128)}, s32[]{:T(128)}) fusion(s32[8]{0:T(128)} %param.9, s32[]{:T(128)} %get-tuple-element.17), kind=kLoop, calls=%fused_computation.54 | loop fusion | flops 46 | bytes 44 | tf_op jit(solution)/shard_map/reduce_sum | solution.py:105
  21.0 3.9 %all-to-all-done = bf16[8,8,512]{2,1,0:T(8,128)(2,1)S(1)} async-done(((bf16[8,8,512]{2,1,0:T(8,128)(2,1)}), bf16[8,8,512]{2,1,0:T(8,128)(2,1)S(1)}, u32[]{:S(2)}, u32[]{:S(2)}) %all-to-all-start) | async-done | bytes 65568 | tf_op jit(solution)/shard_map/all_to_all | solution.py:21
  25.7 8.9 %all-to-all-start.1 = ((bf16[8,64,512]{2,1,0:T(8,128)(2,1)}), bf16[8,64,512]{2,1,0:T(8,128)(2,1)S(1)}, u32[]{:S(2)}, u32[]{:S(2)}) async-start(bf16[8,64,512]{2,1,0:T(8,128)(2,1)} %broadcast_in_dim.69), calls=%async_computation.1 | async-start | bytes 1048576 | tf_op jit(solution)/shard_map/all_to_all | solution.py:23
  35.2 1.1 slice.45
  36.6 1.0 copy.103
  37.7 0.9 fusion.34
  38.6 5.5 %all-to-all-done.1 = bf16[8,64,512]{2,1,0:T(8,128)(2,1)S(1)} async-done(((bf16[8,64,512]{2,1,0:T(8,128)(2,1)}), bf16[8,64,512]{2,1,0:T(8,128)(2,1)S(1)}, u32[]{:S(2)}, u32[]{:S(2)}) %all-to-all-start.1) | async-done | bytes 524320 | tf_op jit(solution)/shard_map/all_to_all | solution.py:23
  44.4 0.9 fusion.36
  46.9 0.9 fusion.8
  50.1 1.1 copy.128
  51.2 4.3 %all-to-all-start.2 = ((f32[8,64,512]{2,1,0:T(8,128)}), f32[8,64,512]{2,1,0:T(8,128)S(1)}, u32[]{:S(2)}, u32[]{:S(2)}) async-start(f32[8,64,512]{2,1,0:T(8,128)} %bitcast.88), calls=%async_computation.2 | async-start | bytes 2097152 | tf_op jit(solution)/shard_map/all_to_all | solution.py:35
  56.4 12.9 %collective-permute-start.1 = (bf16[1,32,2048]{2,1,0:T(8,128)(2,1)S(1)}, bf16[1,32,2048]{2,1,0:T(8,128)(2,1)}, u32[]{:S(2)}, u32[]{:S(2)}) collective-permute-start(bf16[1,32,2048]{2,1,0:T(8,128)(2,1)S(1)} %copy.100), channel_id=1, source_target_pairs={{0,1},{1,2},{2,3},{3,0},{4,5},{5,6},{6,7},{7,4},{8,9},{9,10},{10,1... | collective-permute-start | bytes 393224 | tf_op jit(solution)/shard_map/ppermute | solution.py:57
  69.4 1.0 copy.99
  70.3 4.1 %collective-permute-start = (bf16[1,96,2048]{2,1,0:T(8,128)(2,1)}, bf16[1,96,2048]{2,1,0:T(8,128)(2,1)}, u32[]{:S(2)}, u32[]{:S(2)}) collective-permute-start(bf16[1,96,2048]{2,1,0:T(8,128)(2,1)} %copy.99), channel_id=1, source_target_pairs={{0,15},{1,0},{2,1},{3,2},{4,3},{5,4},{6,5},{7,6},{8,7},{9,8},{10,9... | collective-permute-start | bytes 1179656 | tf_op jit(solution)/shard_map/ppermute | solution.py:54
  74.5 11.0 %collective-permute-start.2 = (bf16[1,32,2048]{2,1,0:T(8,128)(2,1)}, bf16[1,32,2048]{2,1,0:T(8,128)(2,1)}, u32[]{:S(2)}, u32[]{:S(2)}) collective-permute-start(bf16[1,32,2048]{2,1,0:T(8,128)(2,1)} %collective-permute-done.1), channel_id=1, source_target_pairs={{0,1},{1,2},{2,3},{3,0},{4,5},{5,6},{6,7},{7,4},{8,9},{9,10},{10,1... | collective-permute-start | bytes 393224 | tf_op jit(solution)/shard_map/ppermute | solution.py:58
  85.5 18.1 %collective-permute-done.2 = bf16[1,32,2048]{2,1,0:T(8,128)(2,1)} collective-permute-done((bf16[1,32,2048]{2,1,0:T(8,128)(2,1)}, bf16[1,32,2048]{2,1,0:T(8,128)(2,1)}, u32[]{:S(2)}, u32[]{:S(2)}) %collective-permute-start.2) | collective-permute-done | bytes 131104 | tf_op jit(solution)/shard_map/ppermute | solution.py:58
  103.6 2.1 %collective-permute-start.3 = (bf16[1,32,2048]{2,1,0:T(8,128)(2,1)}, bf16[1,32,2048]{2,1,0:T(8,128)(2,1)}, u32[]{:S(2)}, u32[]{:S(2)}) collective-permute-start(bf16[1,32,2048]{2,1,0:T(8,128)(2,1)} %collective-permute-done.2), channel_id=1, source_target_pairs={{0,1},{1,2},{2,15},{3,0},{4,5},{5,6},{6,3},{7,4},{8,9},{9,10},{10,... | collective-permute-start | bytes 393224 | tf_op jit(solution)/shard_map/ppermute | solution.py:60
  106.5 29.3 %all-to-all-start.3 = ((f32[8,8,512]{2,1,0:T(8,128)}), f32[8,8,512]{2,1,0:T(8,128)S(1)}, u32[]{:S(2)}, u32[]{:S(2)}) async-start(f32[8,8,512]{2,1,0:T(8,128)} %bitcast.34), calls=%async_computation.3 | async-start | bytes 262144 | tf_op jit(solution)/shard_map/all_to_all | solution.py:37
  135.8 15.2 %collective-permute-done = bf16[1,96,2048]{2,1,0:T(8,128)(2,1)} collective-permute-done((bf16[1,96,2048]{2,1,0:T(8,128)(2,1)}, bf16[1,96,2048]{2,1,0:T(8,128)(2,1)}, u32[]{:S(2)}, u32[]{:S(2)}) %collective-permute-start) | collective-permute-done | bytes 393248 | tf_op jit(solution)/shard_map/ppermute | solution.py:54
  151.0 1.9 %pad_maximum_fusion = bf16[1,128,2048]{2,1,0:T(8,128)(2,1)} fusion(bf16[1,32,2048]{2,1,0:T(8,128)(2,1)} %collective-permute-done.3, bf16[1,96,2048]{2,1,0:T(8,128)(2,1)} %collective-permute-done), kind=kLoop, calls=%fused_computation.28 | loop fusion | flops 1048576 | bytes 1048576 | tf_op jit(solution)/shard_map/concatenate | solution.py:61
  154.6 1.5 all-to-all-done.3
  (55 shorter events, 10.4 us)
Async XLA Ops:
  0.6 36.0 %copy-start.5 = (bf16[1,128,2048]{2,1,0:T(8,128)(2,1)S(1)}, bf16[1,128,2048]{2,1,0:T(8,128)(2,1)}, u32[]{:S(2)}) copy-start(bf16[1,128,2048]{2,1,0:T(8,128)(2,1)} %param.7) | copy-start | bytes 1572868
  2.0 22.8 %all-to-all-start = ((bf16[8,8,512]{2,1,0:T(8,128)(2,1)}), bf16[8,8,512]{2,1,0:T(8,128)(2,1)S(1)}, u32[]{:S(2)}, u32[]{:S(2)}) async-start(bf16[8,8,512]{2,1,0:T(8,128)(2,1)} %broadcast_in_dim.67), calls=%async_computation | async-start | bytes 131072 | tf_op jit(solution)/shard_map/all_to_all | solution.py:21
  25.7 18.4 %all-to-all-start.1 = ((bf16[8,64,512]{2,1,0:T(8,128)(2,1)}), bf16[8,64,512]{2,1,0:T(8,128)(2,1)S(1)}, u32[]{:S(2)}, u32[]{:S(2)}) async-start(bf16[8,64,512]{2,1,0:T(8,128)(2,1)} %broadcast_in_dim.69), calls=%async_computation.1 | async-start | bytes 1048576 | tf_op jit(solution)/shard_map/all_to_all | solution.py:23
  36.6 11.8 %copy-start.3 = (bf16[128,2048]{0,1:T(8,128)(2,1)}, bf16[128,2048]{0,1:T(8,128)(2,1)S(1)}, u32[]{:S(2)}) copy-start(bf16[128,2048]{0,1:T(8,128)(2,1)S(1)} %copy.54) | copy-start | bytes 1572868
  45.4 1.0 copy-start.6
  45.7 2.1 %copy-start.2 = (bf16[2,8,128,320]{2,3,1,0:T(8,128)(2,1)}, bf16[2,8,128,320]{2,3,1,0:T(8,128)(2,1)S(1)}, u32[]{:S(2)}) copy-start(bf16[2,8,128,320]{2,3,1,0:T(8,128)(2,1)S(1)} %fusion.14) | copy-start | bytes 3932164
  48.4 1.1 copy-start
  49.6 5.9 %copy-start.1 = (bf16[2,8,128,320]{2,3,1,0:T(8,128)(2,1)S(1)}, bf16[2,8,128,320]{2,3,1,0:T(8,128)(2,1)}, u32[]{:S(2)}) copy-start(bf16[2,8,128,320]{2,3,1,0:T(8,128)(2,1)} %copy-done) | copy-start | bytes 3932164
  51.2 54.5 %all-to-all-start.2 = ((f32[8,64,512]{2,1,0:T(8,128)}), f32[8,64,512]{2,1,0:T(8,128)S(1)}, u32[]{:S(2)}, u32[]{:S(2)}) async-start(f32[8,64,512]{2,1,0:T(8,128)} %bitcast.88), calls=%async_computation.2 | async-start | bytes 2097152 | tf_op jit(solution)/shard_map/all_to_all | solution.py:35
  56.4 18.0 %collective-permute-start.1 = (bf16[1,32,2048]{2,1,0:T(8,128)(2,1)S(1)}, bf16[1,32,2048]{2,1,0:T(8,128)(2,1)}, u32[]{:S(2)}, u32[]{:S(2)}) collective-permute-start(bf16[1,32,2048]{2,1,0:T(8,128)(2,1)S(1)} %copy.100), channel_id=1, source_target_pairs={{0,1},{1,2},{2,3},{3,0},{4,5},{5,6},{6,7},{7,4},{8,9},{9,10},{10,1... | collective-permute-start | bytes 393224 | tf_op jit(solution)/shard_map/ppermute | solution.py:57
  69.4 83.6 %slice-start = ((bf16[2,8,128,320]{2,3,1,0:T(8,128)(2,1)}), bf16[2,8,128,128]{2,3,1,0:T(8,128)(2,1)S(1)}, s32[]{:S(2)}) async-start(bf16[2,8,128,320]{2,3,1,0:T(8,128)(2,1)} %copy-done), calls=%async_computation.4 | async-start | bytes 1048576 | tf_op jit(solution)/shard_map/slice | solution.py:146
  70.3 80.7 %collective-permute-start = (bf16[1,96,2048]{2,1,0:T(8,128)(2,1)}, bf16[1,96,2048]{2,1,0:T(8,128)(2,1)}, u32[]{:S(2)}, u32[]{:S(2)}) collective-permute-start(bf16[1,96,2048]{2,1,0:T(8,128)(2,1)} %copy.99), channel_id=1, source_target_pairs={{0,15},{1,0},{2,1},{3,2},{4,3},{5,4},{6,5},{7,6},{8,7},{9,8},{10,9... | collective-permute-start | bytes 1179656 | tf_op jit(solution)/shard_map/ppermute | solution.py:54
  74.5 29.1 %collective-permute-start.2 = (bf16[1,32,2048]{2,1,0:T(8,128)(2,1)}, bf16[1,32,2048]{2,1,0:T(8,128)(2,1)}, u32[]{:S(2)}, u32[]{:S(2)}) collective-permute-start(bf16[1,32,2048]{2,1,0:T(8,128)(2,1)} %collective-permute-done.1), channel_id=1, source_target_pairs={{0,1},{1,2},{2,3},{3,0},{4,5},{5,6},{6,7},{7,4},{8,9},{9,10},{10,1... | collective-permute-start | bytes 393224 | tf_op jit(solution)/shard_map/ppermute | solution.py:58
  103.6 32.2 %collective-permute-start.3 = (bf16[1,32,2048]{2,1,0:T(8,128)(2,1)}, bf16[1,32,2048]{2,1,0:T(8,128)(2,1)}, u32[]{:S(2)}, u32[]{:S(2)}) collective-permute-start(bf16[1,32,2048]{2,1,0:T(8,128)(2,1)} %collective-permute-done.2), channel_id=1, source_target_pairs={{0,1},{1,2},{2,15},{3,0},{4,5},{5,6},{6,3},{7,4},{8,9},{9,10},{10,... | collective-permute-start | bytes 393224 | tf_op jit(solution)/shard_map/ppermute | solution.py:60
  106.5 46.5 %copy-start.4 = (bf16[128,2048]{0,1:T(8,128)(2,1)S(1)}, bf16[128,2048]{0,1:T(8,128)(2,1)}, u32[]{:S(2)}) copy-start(bf16[128,2048]{0,1:T(8,128)(2,1)} %copy-done.3) | copy-start | bytes 1572868
  106.5 46.9 %slice-start.1 = ((bf16[2,8,128,320]{2,3,1,0:T(8,128)(2,1)}), bf16[2,8,128,128]{2,3,1,0:T(8,128)(2,1)S(1)}, s32[]{:S(2)}) async-start(bf16[2,8,128,320]{2,3,1,0:T(8,128)(2,1)} %copy-done.2), calls=%async_computation.5 | async-start | bytes 1048576 | tf_op jit(solution)/shard_map/slice | solution.py:146
  106.5 46.9 %copy-start.7 = (bf16[16,8,16,128]{3,2,1,0:T(8,128)(2,1)S(1)}, bf16[16,8,16,128]{3,2,1,0:T(8,128)(2,1)}, u32[]{:S(2)}) copy-start(bf16[16,8,16,128]{3,2,1,0:T(8,128)(2,1)} %copy.103) | copy-start | bytes 1572868
  106.5 49.7 %all-to-all-start.3 = ((f32[8,8,512]{2,1,0:T(8,128)}), f32[8,8,512]{2,1,0:T(8,128)S(1)}, u32[]{:S(2)}, u32[]{:S(2)}) async-start(f32[8,8,512]{2,1,0:T(8,128)} %bitcast.34), calls=%async_computation.3 | async-start | bytes 262144 | tf_op jit(solution)/shard_map/all_to_all | solution.py:37

commit v12 on v11

--- a/solution.py
+++ b/solution.py
@@ -50,7 +50,7 @@
     count = lax.axis_size(axis)
     far_count = lax.axis_size(axis[1])
     rows = value.shape[1]
-    cut = rows - rows // 4
+    cut = rows - 7 * rows // 32
     direct = lax.ppermute(value[:, :cut], axis, around(count, far_count, lambda n, f: (n - (f == 0), f - 1)))
     rest = value[:, cut:]
     hop = around(count, far_count, lambda n, f: (n, f + 1))

time: 158 us -> 168 us (1.063)
  the two profiles are of different devices: /device:TPU:1 before, /device:TPU:6 now
where the time goes in v12:
time: 168 us; the launch traced here: 167 us
  waiting for transfers between devices  81.6 us (49%)
  starting transfers between devices  58.3 us (35%)
  local copies, waits for them, and re-layouts  10.4 us (6%)
  other arithmetic  9.01 us (5%)
  matrix products  4.49 us (3%)
  between operations  2.82 us (2%)
    ppermute x2, waiting for transfers between devices, pass_down(): rest = lax.ppermute(rest, axis, hop)  53.2 us
    ppermute x1, waiting for transfers between devices, pass_down(): rest = lax.ppermute(rest, axis, last)  19 us
    ppermute x1, starting transfers between devices, pass_down(): lax.ppermute(value[:, :cut], axis, around(count, far_count, lambda n, f:...  15.4 us
    all_to_all x1, starting transfers between devices, gather_prefix(): lax.all_to_all(spread, FAR, 0, 0, tiled=True).reshape(far * rows, width)  12.5 us
    all_to_all x1, starting transfers between devices, scatter_sum(): return lax.all_to_all(parts, FAR, 0, 0, tiled=True).sum(axis=0)  11.6 us
    all_to_all x1, starting transfers between devices, gather_prefix(): whole = lax.all_to_all(spread, NEAR, 0, 0, tiled=True)  7.33 us
    all_to_all x1, starting transfers between devices, scatter_sum(): parts = lax.all_to_all(parts, NEAR, 0, 0, tiled=True).sum(axis=0)  5.57 us
    all_to_all x1, waiting for transfers between devices, gather_prefix(): lax.all_to_all(spread, FAR, 0, 0, tiled=True).reshape(far * rows, width)  5.05 us
  transfers between devices with their start and end apart: 8, of which 5 were waited for; matrix products, arithmetic and copies ran while one was open for 8% of the time, Pallas kernels for 0%

profile of v12, /device:TPU:6, one launch (start us, length us, event | category | flops | bytes accessed | tf_op | source)
XLA Modules:
  0.0 166.6 jit_solution(2495629334220581081)
XLA Ops:
  0.6 1.4 broadcast_in_dim.67
  2.0 12.5 %all-to-all-start = ((bf16[8,8,512]{2,1,0:T(8,128)(2,1)}), bf16[8,8,512]{2,1,0:T(8,128)(2,1)S(1)}, u32[]{:S(2)}, u32[]{:S(2)}) async-start(bf16[8,8,512]{2,1,0:T(8,128)(2,1)} %broadcast_in_dim.67), calls=%async_computation | async-start | bytes 131072 | tf_op jit(solution)/shard_map/all_to_all | solution.py:21
  14.6 1.3 fusion.28
  15.9 2.0 %fusion.31 = (s32[]{:T(128)}, s32[]{:T(128)}) fusion(s32[8]{0:T(128)} %param.9, s32[]{:T(128)} %get-tuple-element.17), kind=kLoop, calls=%fused_computation.54 | loop fusion | flops 46 | bytes 44 | tf_op jit(solution)/shard_map/reduce_sum | solution.py:105
  20.4 5.1 %all-to-all-done = bf16[8,8,512]{2,1,0:T(8,128)(2,1)S(1)} async-done(((bf16[8,8,512]{2,1,0:T(8,128)(2,1)}), bf16[8,8,512]{2,1,0:T(8,128)(2,1)S(1)}, u32[]{:S(2)}, u32[]{:S(2)}) %all-to-all-start) | async-done | bytes 65568 | tf_op jit(solution)/shard_map/all_to_all | solution.py:21
  26.3 7.3 %all-to-all-start.1 = ((bf16[8,64,512]{2,1,0:T(8,128)(2,1)}), bf16[8,64,512]{2,1,0:T(8,128)(2,1)S(1)}, u32[]{:S(2)}, u32[]{:S(2)}) async-start(bf16[8,64,512]{2,1,0:T(8,128)(2,1)} %broadcast_in_dim.69), calls=%async_computation.1 | async-start | bytes 1048576 | tf_op jit(solution)/shard_map/all_to_all | solution.py:23
  34.2 1.1 slice.45
  35.6 1.0 copy.103
  36.7 0.9 fusion.34
  37.6 4.3 %all-to-all-done.1 = bf16[8,64,512]{2,1,0:T(8,128)(2,1)S(1)} async-done(((bf16[8,64,512]{2,1,0:T(8,128)(2,1)}), bf16[8,64,512]{2,1,0:T(8,128)(2,1)S(1)}, u32[]{:S(2)}, u32[]{:S(2)}) %all-to-all-start.1) | async-done | bytes 524320 | tf_op jit(solution)/shard_map/all_to_all | solution.py:23
  42.2 0.9 fusion.36
  44.6 0.9 fusion.8
  47.8 1.1 copy.128
  48.9 5.6 %all-to-all-start.2 = ((f32[8,64,512]{2,1,0:T(8,128)}), f32[8,64,512]{2,1,0:T(8,128)S(1)}, u32[]{:S(2)}, u32[]{:S(2)}) async-start(f32[8,64,512]{2,1,0:T(8,128)} %bitcast.88), calls=%async_computation.2 | async-start | bytes 2097152 | tf_op jit(solution)/shard_map/all_to_all | solution.py:35
  55.0 1.0 copy.99
  56.0 15.4 %collective-permute-start = (bf16[1,100,2048]{2,1,0:T(8,128)(2,1)}, bf16[1,100,2048]{2,1,0:T(8,128)(2,1)}, u32[]{:S(2)}, u32[]{:S(2)}) collective-permute-start(bf16[1,100,2048]{2,1,0:T(8,128)(2,1)} %copy.99), channel_id=1, source_target_pairs={{0,15},{1,0},{2,1},{3,2},{4,3},{5,4},{6,5},{7,6},{8,7},{9,8},{10,9... | collective-permute-start | bytes 1228808 | tf_op jit(solution)/shard_map/ppermute | solution.py:54
  71.9 2.0 %collective-permute-start.1 = (bf16[1,28,2048]{2,1,0:T(8,128)(2,1)S(1)}, bf16[1,28,2048]{2,1,0:T(8,128)(2,1)S(1)}, u32[]{:S(2)}, u32[]{:S(2)}) collective-permute-start(bf16[1,28,2048]{2,1,0:T(8,128)(2,1)S(1)} %copy.100), channel_id=1, source_target_pairs={{0,1},{1,2},{2,3},{3,0},{4,5},{5,6},{6,7},{7,4},{8,9},{9,10},{10,1... | collective-permute-start | bytes 344072 | tf_op jit(solution)/shard_map/ppermute | solution.py:57
  73.9 24.4 %collective-permute-done.1 = bf16[1,28,2048]{2,1,0:T(8,128)(2,1)S(1)} collective-permute-done((bf16[1,28,2048]{2,1,0:T(8,128)(2,1)S(1)}, bf16[1,28,2048]{2,1,0:T(8,128)(2,1)S(1)}, u32[]{:S(2)}, u32[]{:S(2)}) %collective-permute-start.1) | collective-permute-done | bytes 114720 | tf_op jit(solution)/shard_map/ppermute | solution.py:57
  98.4 1.9 %collective-permute-start.2 = (bf16[1,28,2048]{2,1,0:T(8,128)(2,1)S(1)}, bf16[1,28,2048]{2,1,0:T(8,128)(2,1)}, u32[]{:S(2)}, u32[]{:S(2)}) collective-permute-start(bf16[1,28,2048]{2,1,0:T(8,128)(2,1)S(1)} %collective-permute-done.1), channel_id=1, source_target_pairs={{0,1},{1,2},{2,3},{3,0},{4,5},{5,6},{6,7},{7,4},{8,9},{9,10},{10,1... | collective-permute-start | bytes 344072 | tf_op jit(solution)/shard_map/ppermute | solution.py:58
  100.3 28.8 %collective-permute-done.2 = bf16[1,28,2048]{2,1,0:T(8,128)(2,1)} collective-permute-done((bf16[1,28,2048]{2,1,0:T(8,128)(2,1)S(1)}, bf16[1,28,2048]{2,1,0:T(8,128)(2,1)}, u32[]{:S(2)}, u32[]{:S(2)}) %collective-permute-start.2) | collective-permute-done | bytes 114720 | tf_op jit(solution)/shard_map/ppermute | solution.py:58
  129.1 1.9 %collective-permute-start.3 = (bf16[1,28,2048]{2,1,0:T(8,128)(2,1)}, bf16[1,28,2048]{2,1,0:T(8,128)(2,1)}, u32[]{:S(2)}, u32[]{:S(2)}) collective-permute-start(bf16[1,28,2048]{2,1,0:T(8,128)(2,1)} %collective-permute-done.2), channel_id=1, source_target_pairs={{0,1},{1,2},{2,15},{3,0},{4,5},{5,6},{6,3},{7,4},{8,9},{9,10},{10,... | collective-permute-start | bytes 344072 | tf_op jit(solution)/shard_map/ppermute | solution.py:60
  131.7 11.6 %all-to-all-start.3 = ((f32[8,8,512]{2,1,0:T(8,128)}), f32[8,8,512]{2,1,0:T(8,128)S(1)}, u32[]{:S(2)}, u32[]{:S(2)}) async-start(f32[8,8,512]{2,1,0:T(8,128)} %bitcast.34), calls=%async_computation.3 | async-start | bytes 262144 | tf_op jit(solution)/shard_map/all_to_all | solution.py:37
  143.3 19.0 %collective-permute-done.3 = bf16[1,28,2048]{2,1,0:T(8,128)(2,1)} collective-permute-done((bf16[1,28,2048]{2,1,0:T(8,128)(2,1)}, bf16[1,28,2048]{2,1,0:T(8,128)(2,1)}, u32[]{:S(2)}, u32[]{:S(2)}) %collective-permute-start.3) | collective-permute-done | bytes 114720 | tf_op jit(solution)/shard_map/ppermute | solution.py:60
  162.4 1.9 %pad_maximum_fusion = bf16[1,128,2048]{2,1,0:T(8,128)(2,1)} fusion(bf16[1,28,2048]{2,1,0:T(8,128)(2,1)} %collective-permute-done.3, bf16[1,100,2048]{2,1,0:T(8,128)(2,1)} %collective-permute-done), kind=kLoop, calls=%fused_computation.28 | loop fusion | flops 1048576 | bytes 1048576 | tf_op jit(solution)/shard_map/concatenate | solution.py:61
  (55 shorter events, 10.4 us)
Async XLA Ops:
  0.6 35.0 %copy-start.5 = (bf16[1,128,2048]{2,1,0:T(8,128)(2,1)S(1)}, bf16[1,128,2048]{2,1,0:T(8,128)(2,1)}, u32[]{:S(2)}) copy-start(bf16[1,128,2048]{2,1,0:T(8,128)(2,1)} %param.7) | copy-start | bytes 1572868
  2.0 23.4 %all-to-all-start = ((bf16[8,8,512]{2,1,0:T(8,128)(2,1)}), bf16[8,8,512]{2,1,0:T(8,128)(2,1)S(1)}, u32[]{:S(2)}, u32[]{:S(2)}) async-start(bf16[8,8,512]{2,1,0:T(8,128)(2,1)} %broadcast_in_dim.67), calls=%async_computation | async-start | bytes 131072 | tf_op jit(solution)/shard_map/all_to_all | solution.py:21
  26.3 15.6 %all-to-all-start.1 = ((bf16[8,64,512]{2,1,0:T(8,128)(2,1)}), bf16[8,64,512]{2,1,0:T(8,128)(2,1)S(1)}, u32[]{:S(2)}, u32[]{:S(2)}) async-start(bf16[8,64,512]{2,1,0:T(8,128)(2,1)} %broadcast_in_dim.69), calls=%async_computation.1 | async-start | bytes 1048576 | tf_op jit(solution)/shard_map/all_to_all | solution.py:23
  35.6 10.6 %copy-start.3 = (bf16[128,2048]{0,1:T(8,128)(2,1)}, bf16[128,2048]{0,1:T(8,128)(2,1)S(1)}, u32[]{:S(2)}) copy-start(bf16[128,2048]{0,1:T(8,128)(2,1)S(1)} %copy.54) | copy-start | bytes 1572868
  43.1 1.0 copy-start.6
  43.5 2.1 %copy-start.2 = (bf16[2,8,128,320]{2,3,1,0:T(8,128)(2,1)}, bf16[2,8,128,320]{2,3,1,0:T(8,128)(2,1)S(1)}, u32[]{:S(2)}) copy-start(bf16[2,8,128,320]{2,3,1,0:T(8,128)(2,1)S(1)} %fusion.14) | copy-start | bytes 3932164
  46.2 1.1 copy-start
  47.4 7.1 %copy-start.1 = (bf16[2,8,128,320]{2,3,1,0:T(8,128)(2,1)S(1)}, bf16[2,8,128,320]{2,3,1,0:T(8,128)(2,1)}, u32[]{:S(2)}) copy-start(bf16[2,8,128,320]{2,3,1,0:T(8,128)(2,1)} %copy-done) | copy-start | bytes 3932164
  48.9 82.1 %all-to-all-start.2 = ((f32[8,64,512]{2,1,0:T(8,128)}), f32[8,64,512]{2,1,0:T(8,128)S(1)}, u32[]{:S(2)}, u32[]{:S(2)}) async-start(f32[8,64,512]{2,1,0:T(8,128)} %bitcast.88), calls=%async_computation.2 | async-start | bytes 2097152 | tf_op jit(solution)/shard_map/all_to_all | solution.py:35
  56.0 106.3 %collective-permute-start = (bf16[1,100,2048]{2,1,0:T(8,128)(2,1)}, bf16[1,100,2048]{2,1,0:T(8,128)(2,1)}, u32[]{:S(2)}, u32[]{:S(2)}) collective-permute-start(bf16[1,100,2048]{2,1,0:T(8,128)(2,1)} %copy.99), channel_id=1, source_target_pairs={{0,15},{1,0},{2,1},{3,2},{4,3},{5,4},{6,5},{7,6},{8,7},{9,8},{10,9... | collective-permute-start | bytes 1228808 | tf_op jit(solution)/shard_map/ppermute | solution.py:54
  71.6 92.6 %slice-start = ((bf16[2,8,128,320]{2,3,1,0:T(8,128)(2,1)}), bf16[2,8,128,128]{2,3,1,0:T(8,128)(2,1)S(1)}, s32[]{:S(2)}) async-start(bf16[2,8,128,320]{2,3,1,0:T(8,128)(2,1)} %copy-done), calls=%async_computation.4 | async-start | bytes 1048576 | tf_op jit(solution)/shard_map/slice | solution.py:146
  71.9 92.4 %copy-start.4 = (bf16[128,2048]{0,1:T(8,128)(2,1)S(1)}, bf16[128,2048]{0,1:T(8,128)(2,1)}, u32[]{:S(2)}) copy-start(bf16[128,2048]{0,1:T(8,128)(2,1)} %copy-done.3) | copy-start | bytes 1572868
  71.9 26.5 %collective-permute-start.1 = (bf16[1,28,2048]{2,1,0:T(8,128)(2,1)S(1)}, bf16[1,28,2048]{2,1,0:T(8,128)(2,1)S(1)}, u32[]{:S(2)}, u32[]{:S(2)}) collective-permute-start(bf16[1,28,2048]{2,1,0:T(8,128)(2,1)S(1)} %copy.100), channel_id=1, source_target_pairs={{0,1},{1,2},{2,3},{3,0},{4,5},{5,6},{6,7},{7,4},{8,9},{9,10},{10,1... | collective-permute-start | bytes 344072 | tf_op jit(solution)/shard_map/ppermute | solution.py:57
  98.4 30.7 %collective-permute-start.2 = (bf16[1,28,2048]{2,1,0:T(8,128)(2,1)S(1)}, bf16[1,28,2048]{2,1,0:T(8,128)(2,1)}, u32[]{:S(2)}, u32[]{:S(2)}) collective-permute-start(bf16[1,28,2048]{2,1,0:T(8,128)(2,1)S(1)} %collective-permute-done.1), channel_id=1, source_target_pairs={{0,1},{1,2},{2,3},{3,0},{4,5},{5,6},{6,7},{7,4},{8,9},{9,10},{10,1... | collective-permute-start | bytes 344072 | tf_op jit(solution)/shard_map/ppermute | solution.py:58
  129.1 33.3 %collective-permute-start.3 = (bf16[1,28,2048]{2,1,0:T(8,128)(2,1)}, bf16[1,28,2048]{2,1,0:T(8,128)(2,1)}, u32[]{:S(2)}, u32[]{:S(2)}) collective-permute-start(bf16[1,28,2048]{2,1,0:T(8,128)(2,1)} %collective-permute-done.2), channel_id=1, source_target_pairs={{0,1},{1,2},{2,15},{3,0},{4,5},{5,6},{6,3},{7,4},{8,9},{9,10},{10,... | collective-permute-start | bytes 344072 | tf_op jit(solution)/shard_map/ppermute | solution.py:60
  131.7 33.0 %slice-start.1 = ((bf16[2,8,128,320]{2,3,1,0:T(8,128)(2,1)}), bf16[2,8,128,128]{2,3,1,0:T(8,128)(2,1)S(1)}, s32[]{:S(2)}) async-start(bf16[2,8,128,320]{2,3,1,0:T(8,128)(2,1)} %copy-done.2), calls=%async_computation.5 | async-start | bytes 1048576 | tf_op jit(solution)/shard_map/slice | solution.py:146
  131.7 33.0 %copy-start.7 = (bf16[16,8,16,128]{3,2,1,0:T(8,128)(2,1)S(1)}, bf16[16,8,16,128]{3,2,1,0:T(8,128)(2,1)}, u32[]{:S(2)}) copy-start(bf16[16,8,16,128]{3,2,1,0:T(8,128)(2,1)} %copy.103) | copy-start | bytes 1572868
  131.7 34.2 %all-to-all-start.3 = ((f32[8,8,512]{2,1,0:T(8,128)}), f32[8,8,512]{2,1,0:T(8,128)S(1)}, u32[]{:S(2)}, u32[]{:S(2)}) async-start(f32[8,8,512]{2,1,0:T(8,128)} %bitcast.34), calls=%async_computation.3 | async-start | bytes 262144 | tf_op jit(solution)/shard_map/all_to_all | solution.py:37
